TPU v7x, 128 devices: a whole 4x4x4 slice. The times are simulated.
128 devices in a mesh: pipe: 2 (over core), dp: 16 (over y, x), tensor: 4 (over z).
Axes of the slice: x: 4, y: 4, z: 4, core: 2. Of those that a mesh axis runs over, the one named last changes fastest.
Arguments:
- weights: bfloat16 [2, 8192, 8192], P('pipe', 'tensor', 'dp'), may hold values from -0.0625 to 0.0625
- inputs: bfloat16 [2, 2, 32, 64, 8192], P('pipe', None, 'dp', None, 'tensor'), may hold values from -150 to 150
- cotangent: bfloat16 [2, 32, 64, 8192], P(None, 'dp', None, 'tensor'), may hold values from -6 to 6
- clip_norm: float32 [1], replicated, may hold values from 8192 to 12582912
- noise: bfloat16 [2, 8192, 8192], P('pipe', 'tensor', 'dp'), may hold values from -6 to 6
Outputs:
- grads: float32 [2, 8192, 8192], P('pipe', 'tensor', 'dp')
- clip_factors: float32 [2, 32], P(None, 'dp')
All inputs are finite; a program needn't handle non-finite values.
Results may differ from a plain program's by a relative error of at most 0.015.
Values may be sent and summed in bfloat16 or wider, within the bound.
No kernel may reach another device: no remote copies, remote signals or barrier semaphores. Data moves between devices by JAX's collectives and lax.ppermute only.
A program may use at most 128 MiB of HBM per device.

v0:
```python
import jax
import jax.numpy as jnp
from jax import lax
from jax.sharding import PartitionSpec as P


def shifted(value, axis, steps):
    count = lax.axis_size(axis)
    first, last = (max(0, -steps), min(count, count - steps))
    return lax.ppermute(value, axis, [(source, source + steps) for source in range(first, last)])


def carried_in(shard, axis, combine, identity):
    peers, position = (lax.axis_size(axis), lax.axis_index(axis))
    everything = lax.all_gather(shard, axis)
    start = jnp.broadcast_to(jnp.asarray(identity, shard.dtype), shard.shape)

    def hop(k, before):
        at = peers - 1 - k
        reached = at > position
        new = combine(before, everything[at])
        return jnp.where(reached, new, before)

    return lax.fori_loop(0, peers, hop, start)


def spread(block, axis, holder):
    block = jnp.where(lax.axis_index(axis) == holder, block, jnp.zeros_like(block))
    return lax.psum(block, axis)


def add_terms(earlier, later):
    return earlier + later


def local(weights, inputs, cotangent, clip_norm, noise):
    section_count = lax.axis_size("pipe")
    section_index = lax.axis_index("pipe")
    group_count = lax.axis_size("dp")
    weight_block = weights[0]
    local_inputs = inputs[0]
    micro_count, example_count, length_count, width_part = local_inputs.shape
    token_count = example_count * length_count
    column_part = weight_block.shape[1]
    full_width = column_part * group_count
    partial_grams = jnp.einsum(
        "mbld,mbkd->mblk", local_inputs, local_inputs, preferred_element_type=jnp.float32
    )
    input_grams = lax.psum(partial_grams.astype(jnp.bfloat16), "tensor").astype(jnp.float32)
    received = jnp.zeros((example_count, length_count, width_part), jnp.bfloat16)
    norm_part = jnp.zeros((micro_count, example_count), jnp.float32)
    stored = jnp.zeros((micro_count, group_count * token_count, column_part), jnp.bfloat16)
    micro_ids = jnp.arange(micro_count)
    for step_number in range(micro_count + section_count - 1):
        position = step_number - (section_count - 1 - section_index)
        is_running = jnp.logical_and(position >= 0, position < micro_count)
        chosen = jnp.clip(position, 0, micro_count - 1)
        incoming = lax.dynamic_index_in_dim(cotangent, chosen, 0, keepdims=False)
        current = jnp.where(section_index == section_count - 1, incoming, received)
        incoming_gradient = lax.all_gather(current, "tensor", axis=2, tiled=True)
        grad_grams = jnp.einsum(
            "xeh,xph->xep", incoming_gradient, incoming_gradient, preferred_element_type=jnp.float32
        )
        own_grams = lax.dynamic_index_in_dim(input_grams, chosen, 0, keepdims=False)
        section_terms = jnp.sum(grad_grams * own_grams, axis=(1, 2))
        picked = jnp.logical_and(is_running, micro_ids == chosen)
        norm_part = norm_part + jnp.where(picked[:, None], section_terms[None, :], 0.0)
        by_block = incoming_gradient.reshape(token_count, group_count, column_part)
        scattered_rows = lax.all_to_all(
            by_block, "dp", split_axis=1, concat_axis=0, tiled=True
        ).reshape(group_count * token_count, column_part)
        stored = jnp.where(
            is_running, lax.dynamic_update_index_in_dim(stored, scattered_rows, chosen, 0), stored
        )
        if step_number < micro_count + section_count - 2:
            summed = lax.psum_scatter(
                lax.dot_general(
                    scattered_rows,
                    weight_block,
                    (((1,), (1,)), ((), ())),
                    preferred_element_type=jnp.float32,
                ).astype(jnp.bfloat16),
                "dp",
                scatter_dimension=0,
                tiled=True,
            ).astype(jnp.float32)
            updated = current.reshape(token_count, width_part).astype(jnp.float32) + summed
            outgoing = updated.astype(jnp.bfloat16).reshape(example_count, length_count, width_part)
            received = shifted(outgoing, "pipe", -1)
    bound = clip_norm[0]
    higher = carried_in(norm_part, "pipe", add_terms, jnp.zeros_like(norm_part))
    root_factors = bound / jnp.maximum(jnp.sqrt(higher + norm_part), bound)
    scale_terms = spread(root_factors, "pipe", 0)
    own_clipped = (local_inputs.astype(jnp.float32) * scale_terms[:, :, None, None]).astype(
        jnp.bfloat16
    )
    clipped = lax.all_gather(own_clipped, "dp", axis=1, tiled=True)
    flat_inputs = clipped.reshape(micro_count * group_count * token_count, width_part)
    flat_grads = stored.reshape(micro_count * group_count * token_count, column_part)
    summed_grad = lax.dot_general(
        flat_inputs, flat_grads, (((0,), (0,)), ((), ())), preferred_element_type=jnp.float32
    )
    noise_weight = 1.5 / full_width
    per_example_sum = micro_count * group_count * example_count
    final_output = (
        summed_grad + noise_weight * bound * noise[0].astype(jnp.float32)
    ) / per_example_sum
    return (final_output[None], scale_terms)


def solution(mesh):
    in_specs = (
        P("pipe", "tensor", "dp"),
        P("pipe", None, "dp", None, "tensor"),
        P(None, "dp", None, "tensor"),
        P(),
        P("pipe", "tensor", "dp"),
    )
    out_specs = (P("pipe", "tensor", "dp"), P(None, "dp"))
    return jax.shard_map(local, mesh=mesh, in_specs=in_specs, out_specs=out_specs, check_vma=False)
```

profile of v0, /device:TPU:1, one launch (start us, length us, event | category | flops | bytes accessed | tf_op | source)
XLA Modules:
  0.0 538.4 jit_solution(2224717927570439957)
XLA Ops:
  9.3 34.4 %all-gather.12.cloned.1.call-done = bf16[1,2,64,8192]{3,2,1,0:T(8,128)(2,1)} async-done(((bf16[1,2,64,2048]{3,2,1,0:T(8,128)(2,1)}), bf16[1,2,64,8192]{3,2,1,0:T(8,128)(2,1)}) %all-gather.12.cloned.1.call-update) | async-done | bytes 2097168 | tf_op jit(solution)/shard_map/all_gather | solution.py:60
  43.7 2.4 copy.13
  47.3 33.7 %all_to_all.45 = bf16[128,16,512]{2,0,1:T(8,128)(2,1)S(1)} all-to-all(bf16[128,16,512]{2,0,1:T(8,128)(2,1)S(1)} %copy.10), channel_id=1, replica_groups=mesh['pipe'=2,'dp'=16,'tensor'=4] {'dp'}, dimensions={1} | all-to-all | bytes 4194304 | tf_op jit(solution)/shard_map/all_to_all | solution.py:69
  82.4 6.9 %convolution_convert_fusion.1 = bf16[2048,2048]{1,0:T(8,128)(2,1)} fusion(bf16[2048,512]{1,0:T(8,128)(2,1)S(1)} %bitcast.92, bf16[1,2048,512]{2,1,0:T(8,128)(2,1)S(1)} %copy-done), kind=kOutput, calls=%fused_computation.2 | convolution fusion | flops 4299161600 | bytes 12582912 | tf_op jit(solution)/shard_map/dot_general | solution.py:77
  89.3 81.8 %reduce-scatter.3.cloned.1.call-done = bf16[128,2048]{1,0:T(8,128)(2,1)} async-done(((bf16[2048,2048]{1,0:T(8,128)(2,1)}), bf16[128,2048]{1,0:T(8,128)(2,1)}) %reduce-scatter.3.cloned.1.call-update) | async-done | bytes 524304 | tf_op jit(solution)/shard_map/reduce_scatter | solution.py:76
  172.4 4.1 collective-permute-start
  180.0 30.0 %all-gather.6.cloned.1.call-done = bf16[2,64,8192]{2,1,0:T(8,128)(2,1)} async-done(((bf16[2,64,2048]{2,1,0:T(8,128)(2,1)}), bf16[2,64,8192]{2,1,0:T(8,128)(2,1)}) %all-gather.6.cloned.1.call-update) | async-done | bytes 2097168 | tf_op jit(solution)/shard_map/all_gather | solution.py:60
  209.9 2.4 copy.14
  213.5 33.7 %all_to_all.46 = bf16[128,16,512]{2,0,1:T(8,128)(2,1)S(1)} all-to-all(bf16[128,16,512]{2,0,1:T(8,128)(2,1)S(1)} %copy.11), channel_id=1, replica_groups=mesh['pipe'=2,'dp'=16,'tensor'=4] {'dp'}, dimensions={1} | all-to-all | bytes 4194304 | tf_op jit(solution)/shard_map/all_to_all | solution.py:69
  248.6 6.9 %convolution_convert_fusion = bf16[2048,2048]{1,0:T(8,128)(2,1)} fusion(bf16[2048,512]{1,0:T(8,128)(2,1)S(1)} %bitcast.93, bf16[1,2048,512]{2,1,0:T(8,128)(2,1)S(1)} %copy-done), kind=kOutput, calls=%fused_computation.1 | convolution fusion | flops 4299161600 | bytes 12582912 | tf_op jit(solution)/shard_map/dot_general | solution.py:77
  255.6 81.7 %reduce-scatter.5.cloned.1.call-done = bf16[128,2048]{1,0:T(8,128)(2,1)} async-done(((bf16[2048,2048]{1,0:T(8,128)(2,1)}), bf16[128,2048]{1,0:T(8,128)(2,1)}) %reduce-scatter.5.cloned.1.call-update) | async-done | bytes 524304 | tf_op jit(solution)/shard_map/reduce_scatter | solution.py:76
  338.5 4.1 collective-permute-start.1
  345.5 14.7 %psum.14 = bf16[2,2,64,64]{3,2,1,0:T(8,128)(2,1)S(1)} all-reduce(bf16[2,2,64,64]{3,2,1,0:T(8,128)(2,1)S(1)} %convolution_convert_fusion.2), channel_id=1, replica_groups=mesh['pipe'=2,'dp'=16,'tensor'=4] {'tensor'}, use_global_device_ids=true, to_apply=%region_0.0 | all-reduce | flops 16384 | bytes 65536 | tf_op jit(solution)/shard_map/psum | solution.py:49
  360.3 3.0 fusion.11
  364.2 11.1 %all-gather.8.cloned.1.call-done = bf16[2,64,8192]{2,1,0:T(8,128)(2,1)} async-done(((bf16[2,64,2048]{2,1,0:T(8,128)(2,1)}), bf16[2,64,8192]{2,1,0:T(8,128)(2,1)}) %all-gather.8.cloned.1.call-update) | async-done | bytes 2097168 | tf_op jit(solution)/shard_map/all_gather | solution.py:60
  375.3 3.0 fusion.10
  381.6 2.5 psum.15
  386.2 2.5 copy.12
  388.7 6.6 %all-to-all-start.2 = ((bf16[128,16,512]{2,0,1:T(8,128)(2,1)}), bf16[128,16,512]{2,0,1:T(8,128)(2,1)}, u32[]{:S(2)}, u32[]{:S(2)}) async-start(bf16[128,16,512]{2,0,1:T(8,128)(2,1)} %copy.12), calls=%async_computation.4 | async-start | bytes 4194304 | tf_op jit(solution)/shard_map/all_to_all | solution.py:69
  400.1 3.5 constant_dynamic-update-slice_fusion.1
  403.6 37.3 %all-to-all-done.2 = bf16[128,16,512]{2,0,1:T(8,128)(2,1)} async-done(((bf16[128,16,512]{2,0,1:T(8,128)(2,1)}), bf16[128,16,512]{2,0,1:T(8,128)(2,1)}, u32[]{:S(2)}, u32[]{:S(2)}) %all-to-all-start.2) | async-done | bytes 2097184 | tf_op jit(solution)/shard_map/all_to_all | solution.py:69
  440.9 4.1 constant_dynamic-update-slice_fusion
  445.1 71.0 %all-gather.10.cloned.1.call-done = bf16[2,32,64,2048]{3,2,1,0:T(8,128)(2,1)} async-done(((bf16[2,2,64,2048]{3,2,1,0:T(8,128)(2,1)}), bf16[2,32,64,2048]{3,2,1,0:T(8,128)(2,1)}) %all-gather.10.cloned.1.call-update) | async-done | bytes 16777232 | tf_op jit(solution)/shard_map/all_gather | solution.py:97
  516.1 15.4 %fusion.1 = f32[1,2048,512]{2,1,0:T(8,128)} fusion(bf16[1,2048,512]{2,1,0:T(8,128)(2,1)} %param.11, bf16[4096,2048]{1,0:T(8,128)(2,1)} %bitcast.101, bf16[4096,512]{1,0:T(8,128)(2,1)} %bitcast.27, f32[]{:T(128)S(6)} %mul_shard_map.3), kind=kOutput, calls=%fused_computation.5 | convolution fusion | flops 8594128896 | bytes 27262980 | tf_op jit(solution)/shard_map/dot_general | solution.py:100
  (64 shorter events, 26.1 us)
Async XLA Ops:
  7.2 75.2 %copy-start = (bf16[1,2048,512]{2,1,0:T(8,128)(2,1)S(1)}, bf16[1,2048,512]{2,1,0:T(8,128)(2,1)}, u32[]{:S(2)}) copy-start(bf16[1,2048,512]{2,1,0:T(8,128)(2,1)} %param.7) | copy-start | bytes 6291460
  7.2 36.5 %all-gather.12.cloned.1.call-start = ((), (), s32[]{:S(2)}) async-start(), calls=%async_computation.10 | async-start | bytes 2621440 | tf_op jit(solution)/shard_map/all_gather | solution.py:60
  9.3 161.9 %reduce-scatter.3.cloned.1.call-start = ((), (), s32[]{:S(2)}) async-start(), calls=%async_computation.5 | async-start | bytes 8912896 | tf_op jit(solution)/shard_map/reduce_scatter | solution.py:76
  81.0 1.3 copy-start.4
  89.3 81.9 %copy-start.8 = (bf16[1,2,64,2048]{3,2,1,0:T(8,128)(2,1)S(1)}, bf16[1,2,64,2048]{3,2,1,0:T(8,128)(2,1)}, u32[]{:S(2)}) copy-start(bf16[1,2,64,2048]{3,2,1,0:T(8,128)(2,1)} %dynamic-slice_select_fusion) | copy-start | bytes 1572868
  89.3 120.6 %all-gather.6.cloned.1.call-start = ((), (), s32[]{:S(2)}) async-start(), calls=%async_computation.6 | async-start | bytes 2621440 | tf_op jit(solution)/shard_map/all_gather | solution.py:60
  172.4 5.6 %collective-permute-start = (bf16[2,64,2048]{2,1,0:T(8,128)(2,1)S(1)}, bf16[2,64,2048]{2,1,0:T(8,128)(2,1)S(1)}, u32[]{:S(2)}, u32[]{:S(2)}) collective-permute-start(bf16[2,64,2048]{2,1,0:T(8,128)(2,1)S(1)} %bitcast.100), channel_id=1, source_target_pairs={{64,0},{65,1},{66,2},{67,3},{68,4},{69,5},{70,6},{71,7},{72,8},{73... | collective-permute-start | bytes 1572872 | tf_op jit(solution)/shard_map/ppermute | solution.py:10
  179.9 157.4 %reduce-scatter.5.cloned.1.call-start = ((), (), s32[]{:S(2)}) async-start(), calls=%async_computation.7 | async-start | bytes 8912896 | tf_op jit(solution)/shard_map/reduce_scatter | solution.py:76
  247.3 1.4 copy-start.6
  255.5 81.8 %copy-start.9 = (bf16[2,64,2048]{2,1,0:T(8,128)(2,1)S(1)}, bf16[2,64,2048]{2,1,0:T(8,128)(2,1)}, u32[]{:S(2)}) copy-start(bf16[2,64,2048]{2,1,0:T(8,128)(2,1)} %bitcast_select_fusion.4) | copy-start | bytes 1572868
  255.5 88.6 %copy-start.10 = (bf16[2,2,64,2048]{3,2,1,0:T(8,128)(2,1)S(1)}, bf16[2,2,64,2048]{3,2,1,0:T(8,128)(2,1)}, u32[]{:S(2)}) copy-start(bf16[2,2,64,2048]{3,2,1,0:T(8,128)(2,1)} %param.9) | copy-start | bytes 3145732
  255.5 89.5 %copy-start.11 = (bf16[1,2,2,64,2048]{4,3,2,1,0:T(8,128)(2,1)S(1)}, bf16[1,2,2,64,2048]{4,3,2,1,0:T(8,128)(2,1)}, u32[]{:S(2)}) copy-start(bf16[1,2,2,64,2048]{4,3,2,1,0:T(8,128)(2,1)} %param.8) | copy-start | bytes 3145732
  255.6 119.7 %all-gather.8.cloned.1.call-start = ((), (), s32[]{:S(2)}) async-start(), calls=%async_computation.8 | async-start | bytes 2621440 | tf_op jit(solution)/shard_map/all_gather | solution.py:60
  338.5 5.6 %collective-permute-start.1 = (bf16[2,64,2048]{2,1,0:T(8,128)(2,1)S(1)}, bf16[2,64,2048]{2,1,0:T(8,128)(2,1)S(1)}, u32[]{:S(2)}, u32[]{:S(2)}) collective-permute-start(bf16[2,64,2048]{2,1,0:T(8,128)(2,1)S(1)} %bitcast.99), channel_id=1, source_target_pairs={{64,0},{65,1},{66,2},{67,3},{68,4},{69,5},{70,6},{71,7},{72,8},{73... | collective-permute-start | bytes 1572872 | tf_op jit(solution)/shard_map/ppermute | solution.py:10
  345.0 171.1 %all-gather.10.cloned.1.call-start = ((), (), s32[]{:S(2)}) async-start(), calls=%async_computation.9 | async-start | bytes 17825792 | tf_op jit(solution)/shard_map/all_gather | solution.py:97
  345.1 18.3 %copy-start.3 = (bf16[2,64,8192]{2,1,0:T(8,128)(2,1)S(1)}, bf16[2,64,8192]{2,1,0:T(8,128)(2,1)}, u32[]{:S(2)}) copy-start(bf16[2,64,8192]{2,1,0:T(8,128)(2,1)} %all-gather.6.cloned.1.call-done) | copy-start | bytes 6291460
  378.3 7.1 %copy-start.2 = (bf16[2,64,8192]{2,1,0:T(8,128)(2,1)S(1)}, bf16[2,64,8192]{2,1,0:T(8,128)(2,1)}, u32[]{:S(2)}) copy-start(bf16[2,64,8192]{2,1,0:T(8,128)(2,1)} %all-gather.8.cloned.1.call-done) | copy-start | bytes 6291460
  384.0 2.1 copy-start.12
  388.7 6.6 %copy-start.5 = (bf16[128,16,512]{2,0,1:T(8,128)(2,1)S(1)}, bf16[128,16,512]{2,0,1:T(8,128)(2,1)}, u32[]{:S(2)}) copy-start(bf16[128,16,512]{2,0,1:T(8,128)(2,1)} %copy-done.4) | copy-start | bytes 6291460
  388.7 52.2 %all-to-all-start.2 = ((bf16[128,16,512]{2,0,1:T(8,128)(2,1)}), bf16[128,16,512]{2,0,1:T(8,128)(2,1)}, u32[]{:S(2)}, u32[]{:S(2)}) async-start(bf16[128,16,512]{2,0,1:T(8,128)(2,1)} %copy.12), calls=%async_computation.4 | async-start | bytes 4194304 | tf_op jit(solution)/shard_map/all_to_all | solution.py:69
  397.7 2.3 copy-start.7
  516.1 15.4 %copy-start.1 = (bf16[1,2048,512]{2,1,0:T(8,128)(2,1)S(1)}, bf16[1,2048,512]{2,1,0:T(8,128)(2,1)}, u32[]{:S(2)}) copy-start(bf16[1,2048,512]{2,1,0:T(8,128)(2,1)} %param.7) | copy-start | bytes 6291460
Sparse Core Ops, SparseCore 0:
  9.7 34.0 all-gather.11
  89.4 81.7 reduce-scatter.2
  180.0 29.8 all-gather.5
  255.7 81.6 reduce-scatter.4
  345.1 30.0 all-gather.7
  385.4 130.6 all-gather.9
where the time goes:
time: 539 us; the launch traced here: 538 us
  waiting for transfers between devices  350 us (65%)
  blocking collectives  87 us (16%)
  matrix products  36.5 us (7%)
  local copies, waits for them, and re-layouts  17.9 us (3%)
  other arithmetic  16.4 us (3%)
  starting transfers between devices  15.1 us (3%)
  between operations  15.1 us (3%)
    reduce_scatter x2, waiting for transfers between devices, local(): lax.psum_scatter(lax.dot_general(scattered_rows, weight_block, (((1,), (1...  164 us
    all_gather x3, waiting for transfers between devices, local(): incoming_gradient = lax.all_gather(current, 'tensor', axis=2, tiled=True)  75.4 us
    all_gather x1, waiting for transfers between devices, local(): clipped = lax.all_gather(own_clipped, 'dp', axis=1, tiled=True)  71 us
    all_to_all x2, blocking collectives, local(): lax.all_to_all(by_block, 'dp', split_axis=1, concat_axis=0, tiled=True)  67.5 us
    all_to_all x1, waiting for transfers between devices, local(): lax.all_to_all(by_block, 'dp', split_axis=1, concat_axis=0, tiled=True)  37.3 us
    dot_general x1, matrix products, local(): lax.dot_general(flat_inputs, flat_grads, (((0,), (0,)), ((), ())), prefer...  15.4 us
    psum x1, blocking collectives, local(): lax.psum(partial_grams.astype(jnp.bfloat16), 'tensor').astype(jnp.float32)  14.7 us
    dot_general x2, matrix products, local(): lax.dot_general(scattered_rows, weight_block, (((1,), (1,)), ((), ())), p...  13.8 us
  transfers between devices with their start and end apart: 9, of which 9 were waited for; matrix products, arithmetic and copies ran while one was open for 4% of the time, Pallas kernels for 0%

commit v1 on v0

v1 whole, which is shorter than its diff:
```python
import jax
import jax.numpy as jnp
from jax import lax
from jax.sharding import PartitionSpec as P


def swapped(value, axis):
    count = lax.axis_size(axis)
    return lax.ppermute(value, axis, [(source, count - 1 - source) for source in range(count)])


def to_column_blocks(values, group_count, column_part):
    micro_count, example_count, length_count, _ = values.shape
    token_count = example_count * length_count
    full = lax.all_gather(values, "tensor", axis=3, tiled=True)
    by_block = full.reshape(micro_count, token_count, group_count, column_part)
    moved = lax.all_to_all(by_block, "dp", split_axis=2, concat_axis=1, tiled=True)
    return moved.reshape(micro_count, group_count * token_count, column_part)


def grams(values):
    return lax.psum(
        jnp.einsum("...ld,...kd->...lk", values, values, preferred_element_type=jnp.float32), "tensor"
    )


def local(weights, inputs, cotangent, clip_norm, noise):
    section_index = lax.axis_index("pipe")
    group_count = lax.axis_size("dp")
    weight_block = weights[0]
    local_inputs = inputs[0]
    micro_count, example_count, length_count, width_part = local_inputs.shape
    token_count = example_count * length_count
    column_part = weight_block.shape[1]
    full_width = column_part * group_count
    is_last = section_index == 1

    gathered_inputs = lax.all_gather(local_inputs, "dp", axis=1, tiled=True)
    input_grams = grams(local_inputs)
    last_grams = grams(cotangent)
    last_blocks = to_column_blocks(cotangent, group_count, column_part)

    last_weights = jnp.where(is_last, weight_block, swapped(weight_block, "pipe"))
    own_blocks = lax.dynamic_index_in_dim(last_blocks, section_index, 0, keepdims=False)
    own_cotangent = lax.dynamic_index_in_dim(cotangent, section_index, 0, keepdims=False)
    terms = lax.dot_general(
        own_blocks, last_weights, (((1,), (1,)), ((), ())), preferred_element_type=jnp.float32
    ).astype(jnp.bfloat16)
    summed = lax.psum_scatter(terms, "dp", scatter_dimension=0, tiled=True).astype(jnp.float32)
    renewed = (own_cotangent.reshape(token_count, width_part).astype(jnp.float32) + summed).astype(
        jnp.bfloat16
    ).reshape(1, example_count, length_count, width_part)

    own_first_grams = grams(renewed)
    other_first_grams = swapped(own_first_grams, "pipe")
    first_grams = jnp.where(
        is_last,
        jnp.concatenate([other_first_grams, own_first_grams], 0),
        jnp.concatenate([own_first_grams, other_first_grams], 0),
    )
    output_grams = jnp.where(is_last, last_grams, first_grams)
    section_terms = jnp.sum(input_grams * output_grams, axis=(2, 3))
    norm_square = lax.psum(section_terms, "pipe")
    bound = clip_norm[0]
    scale_terms = bound / jnp.maximum(jnp.sqrt(norm_square), bound)
    all_scales = lax.all_gather(scale_terms, "dp", axis=1, tiled=True)

    own_first_blocks = to_column_blocks(renewed, group_count, column_part)
    other_first_blocks = swapped(own_first_blocks, "pipe")
    first_blocks = jnp.where(
        is_last,
        jnp.concatenate([other_first_blocks, own_first_blocks], 0),
        jnp.concatenate([own_first_blocks, other_first_blocks], 0),
    )
    grad_blocks = jnp.where(is_last, last_blocks, first_blocks)

    clipped = (gathered_inputs.astype(jnp.float32) * all_scales[:, :, None, None]).astype(jnp.bfloat16)
    flat_inputs = clipped.reshape(micro_count * group_count * token_count, width_part)
    flat_grads = grad_blocks.reshape(micro_count * group_count * token_count, column_part)
    summed_grad = lax.dot_general(
        flat_inputs, flat_grads, (((0,), (0,)), ((), ())), preferred_element_type=jnp.float32
    )
    noise_weight = 1.5 / full_width
    per_example_sum = micro_count * group_count * example_count
    final_output = (
        summed_grad + noise_weight * bound * noise[0].astype(jnp.float32)
    ) / per_example_sum
    return (final_output[None], scale_terms)


def solution(mesh):
    in_specs = (
        P("pipe", "tensor", "dp"),
        P("pipe", None, "dp", None, "tensor"),
        P(None, "dp", None, "tensor"),
        P(),
        P("pipe", "tensor", "dp"),
    )
    out_specs = (P("pipe", "tensor", "dp"), P(None, "dp"))
    return jax.shard_map(local, mesh=mesh, in_specs=in_specs, out_specs=out_specs, check_vma=False)
```

time: 539 us -> 457 us (0.85)
  blocking collectives: 87 us -> 37.2 us
  waiting for transfers between devices: 350 us -> 330 us
  matrix products: 36.5 us -> 20.8 us
    reduce_scatter x2 -> x1, waiting for transfers between devices: 164 us -> 83.8 us  [local(): lax.psum_scatter(terms, 'dp', scatter_dimension=0, tiled=True)]
    all_to_all x2 -> x0, blocking collectives: 67.5 us -> none  [local(): lax.all_to_all(by_block, 'dp', split_axis=1, concat_axis=0, tiled=True)]
    all_gather x4 -> x3, waiting for transfers between devices: 146 us -> 171 us  [the longest x1 88.8 us: local(): gathered_inputs = lax.all_gather(local_inputs, 'dp', axis=1, tiled=True)]
    all_to_all x1 -> x2, waiting for transfers between devices: 37.3 us -> 60.9 us  [to_column_blocks(): lax.all_to_all(by_block, 'dp', split_axis=2, concat_axis=1, tiled=True)]
    all_gather x1, blocking collectives: 2.31 us -> 19.6 us  [local(): all_scales = lax.all_gather(scale_terms, 'dp', axis=1, tiled=True)]
    psum x0 -> x1, waiting for transfers between devices: none -> 13.4 us  [grams(): lax.psum(jnp.einsum('...ld,...kd->...lk', values, values, preferred_eleme...]
    dot_general x6 -> x4, matrix products: 21.1 us -> 9.19 us  [the longest x1 6.78 us: local(): lax.dot_general(own_blocks, last_weights, (((1,), (1,)), ((), ())), prefe...]
    select_n x9 -> x1, other arithmetic: 12.7 us -> 3.92 us  [local(): grad_blocks = jnp.where(is_last, last_blocks, first_blocks)]
  transfers between devices with their start and end apart: 9 -> 10, of which waited for: 9 -> 6; matrix products, arithmetic and copies ran while one was open for 4% -> 5% of each run, Pallas kernels for 0% -> 0%
where the time goes in v1:
time: 457 us
  waiting for transfers between devices  330 us (72%)
  blocking collectives  37.2 us (8%)
  matrix products  20.8 us (5%)
  starting transfers between devices  18.9 us (4%)
  local copies, waits for them, and re-layouts  17.4 us (4%)
  other arithmetic  17.4 us (4%)
  between operations  14.6 us (3%)
    all_gather x1, waiting for transfers between devices, local(): gathered_inputs = lax.all_gather(local_inputs, 'dp', axis=1, tiled=True)  88.8 us
    reduce_scatter x1, waiting for transfers between devices, local(): lax.psum_scatter(terms, 'dp', scatter_dimension=0, tiled=True)  83.8 us
    all_gather x2, waiting for transfers between devices, to_column_blocks(): full = lax.all_gather(values, 'tensor', axis=3, tiled=True)  82.3 us
    all_to_all x2, waiting for transfers between devices, to_column_blocks(): lax.all_to_all(by_block, 'dp', split_axis=2, concat_axis=1, tiled=True)  60.9 us
    all_gather x1, blocking collectives, local(): all_scales = lax.all_gather(scale_terms, 'dp', axis=1, tiled=True)  19.6 us
    psum x1, waiting for transfers between devices, grams(): lax.psum(jnp.einsum('...ld,...kd->...lk', values, values, preferred_eleme...  13.4 us
    all_to_all x2, starting transfers between devices, to_column_blocks(): lax.all_to_all(by_block, 'dp', split_axis=2, concat_axis=1, tiled=True)  13.2 us
    psum x1, blocking collectives, grams(): lax.psum(jnp.einsum('...ld,...kd->...lk', values, values, preferred_eleme...  13 us
  transfers between devices with their start and end apart: 10, of which 6 were waited for; matrix products, arithmetic and copies ran while one was open for 5% of the time, Pallas kernels for 0%

profile of v1, /device:TPU:1, one launch (start us, length us, event | category | flops | bytes accessed | tf_op | source)
XLA Modules:
  0.0 456.7 jit_solution(14960222356371423096)
XLA Ops:
  7.9 53.2 %all-gather.6.cloned.1.call-done = bf16[2,2,64,8192]{3,2,1,0:T(8,128)(2,1)} async-done(((bf16[2,2,64,2048]{3,2,1,0:T(8,128)(2,1)}), bf16[2,2,64,8192]{3,2,1,0:T(8,128)(2,1)}) %all-gather.6.cloned.1.call-update) | async-done | bytes 4194320 | tf_op jit(solution)/shard_map/all_gather | solution.py:15
  61.1 4.0 copy.28
  65.2 4.4 copy.20
  69.6 6.7 %all-to-all-start = ((bf16[2,128,16,512]{3,1,0,2:T(8,128)(2,1)}), bf16[2,128,16,512]{3,1,0,2:T(8,128)(2,1)}, u32[]{:S(2)}, u32[]{:S(2)}) async-start(bf16[2,128,16,512]{3,1,0,2:T(8,128)(2,1)} %copy.20), calls=%async_computation | async-start | bytes 8388608 | tf_op jit(solution)/shard_map/all_to_all | solution.py:17
  76.4 1.2 collective-permute-start
  77.6 60.9 %all-to-all-done = bf16[2,128,16,512]{3,1,0,2:T(8,128)(2,1)} async-done(((bf16[2,128,16,512]{3,1,0,2:T(8,128)(2,1)}), bf16[2,128,16,512]{3,1,0,2:T(8,128)(2,1)}, u32[]{:S(2)}, u32[]{:S(2)}) %all-to-all-start) | async-done | bytes 4194336 | tf_op jit(solution)/shard_map/all_to_all | solution.py:17
  138.4 2.6 copy.21
  141.1 6.8 %convolution_convert_fusion = bf16[2048,2048]{1,0:T(8,128)(2,1)} fusion(bf16[2048,512]{1,0:T(8,128)(2,1)} %collective-permute-done, bf16[2,2048,512]{2,1,0:T(8,128)(2,1)S(1)} %bitcast.80, s32[]{:T(128)S(6)} %select_n.51, pred[]{:T(512)S(6)} %eq.3, bf16[1,2048,512]{2,1,0:T(8,128)(2,1)S(1)} %copy-done.3), kind=kOutput, calls=%fused_computation.2 | convolution fusion | flops 4300210176 | bytes 14680069 | tf_op jit(solution)/shard_map/dot_general | solution.py:46
  147.9 1.1 copy-done
  149.1 83.8 %reduce-scatter.2.cloned.1.call-done = bf16[128,2048]{1,0:T(8,128)(2,1)} async-done(((bf16[2048,2048]{1,0:T(8,128)(2,1)}), bf16[128,2048]{1,0:T(8,128)(2,1)}) %reduce-scatter.2.cloned.1.call-update) | async-done | bytes 524304 | tf_op jit(solution)/shard_map/reduce_scatter | solution.py:49
  232.9 2.0 fusion.8
  237.7 29.0 %all-gather.8.cloned.1.call-done = bf16[1,2,64,8192]{3,2,1,0:T(8,128)(2,1)} async-done(((bf16[1,2,64,2048]{3,2,1,0:T(8,128)(2,1)}), bf16[1,2,64,8192]{3,2,1,0:T(8,128)(2,1)}) %all-gather.8.cloned.1.call-update) | async-done | bytes 2097168 | tf_op jit(solution)/shard_map/all_gather | solution.py:15
  266.8 2.4 copy.29
  269.2 2.5 copy.24
  271.7 6.5 %all-to-all-start.1 = ((bf16[1,128,16,512]{3,1,0,2:T(8,128)(2,1)}), bf16[1,128,16,512]{3,1,0,2:T(8,128)(2,1)S(1)}, u32[]{:S(2)}, u32[]{:S(2)}) async-start(bf16[1,128,16,512]{3,1,0,2:T(8,128)(2,1)} %copy.24), calls=%async_computation.2 | async-start | bytes 4194304 | tf_op jit(solution)/shard_map/all_to_all | solution.py:17
  278.5 13.0 %psum.30 = f32[1,2,64,64]{3,2,1,0:T(8,128)S(1)} all-reduce(f32[1,2,64,64]{3,2,1,0:T(8,128)S(1)} %convolution_bitcast_fusion), channel_id=1, replica_groups=mesh['pipe'=2,'dp'=16,'tensor'=4] {'tensor'}, use_global_device_ids=true, to_apply=%region_3.4 | all-reduce | flops 8192 | bytes 65536 | tf_op jit(solution)/shard_map/psum | solution.py:22
  291.5 3.9 collective-permute-start.1
  296.1 13.4 %all-reduce.3.cloned.1.call-done = (f32[2,2,64,64]{3,2,1,0:T(8,128)}, f32[2,2,64,64]{3,2,1,0:T(8,128)}) async-done(((f32[2,2,64,64]{3,2,1,0:T(8,128)}, f32[2,2,64,64]{3,2,1,0:T(8,128)}), (f32[2,2,64,64]{3,2,1,0:T(8,128)}, f32[2,2,64,64]{3,2,1,0:T(8,128)})) %all-reduce.3.cloned.1.call-update) | async-done | bytes 131088 | tf_op jit(solution)/shard_map/psum | solution.py:22
  310.6 4.6 %psum.31 = f32[2,2]{1,0:T(2,128)S(1)} all-reduce(f32[2,2]{1,0:T(2,128)S(1)} %fusion.13), channel_id=1, replica_groups=mesh['pipe'=2,'dp'=16,'tensor'=4] {'pipe'}, use_global_device_ids=true, to_apply=%region_5.6 | all-reduce | flops 4 | bytes 32 | tf_op jit(solution)/shard_map/psum | solution.py:63
  315.7 19.6 %all-gather.1 = f32[16,2,2]{2,1,0:T(2,128)S(1)} all-gather(f32[1,2,2]{2,1,0:T(2,128)S(1)} %bitcast.84), channel_id=1, replica_groups=mesh['pipe'=2,'dp'=16,'tensor'=4] {'dp'}, dimensions={0}, use_global_device_ids=true | all-gather | bytes 272 | tf_op jit(solution)/shard_map/all_gather | solution.py:66
  335.9 88.8 %all-gather.10.cloned.1.call-done = bf16[1,2,32,64,2048]{4,3,2,1,0:T(8,128)(2,1)} async-done(((bf16[1,2,2,64,2048]{4,3,2,1,0:T(8,128)(2,1)}), bf16[1,2,32,64,2048]{4,3,2,1,0:T(8,128)(2,1)}) %all-gather.10.cloned.1.call-update) | async-done | bytes 16777232 | tf_op jit(solution)/shard_map/all_gather | solution.py:38
  424.8 9.8 %fusion = bf16[2,32,64,2048]{3,2,1,0:T(8,128)(2,1)S(1)} fusion(bf16[1,2,32,64,2048]{4,3,2,1,0:T(8,128)(2,1)} %all-gather.10.cloned.1.call-done, f32[2,32]{1,0:T(2,128)S(1)} %bitcast.83), kind=kLoop, calls=%fused_computation.1 | loop fusion | flops 25165824 | bytes 33554688 | tf_op jit(solution)/shard_map/convert_element_type | solution.py:77
  434.6 3.9 fusion.1
  438.5 11.6 %fusion.3 = f32[1,2048,512]{2,1,0:T(8,128)} fusion(bf16[1,2048,512]{2,1,0:T(8,128)(2,1)} %param.9, bf16[4096,2048]{1,0:T(8,128)(2,1)S(1)} %bitcast.71, bf16[4096,512]{1,0:T(8,128)(2,1)S(1)} %bitcast.79, f32[]{:T(128)S(6)} %mul_shard_map.3), kind=kOutput, calls=%fused_computation.7 | convolution fusion | flops 8594128896 | bytes 27262980 | tf_op jit(solution)/shard_map/dot_general | solution.py:80
  (31 shorter events, 6.1 us)
Async XLA Ops:
  7.2 54.0 %all-gather.6.cloned.1.call-start = ((), (), s32[]{:S(2)}) async-start(), calls=%async_computation.3 | async-start | bytes 5242880 | tf_op jit(solution)/shard_map/all_gather | solution.py:15
  69.6 6.8 %copy-start.3 = (bf16[1,2048,512]{2,1,0:T(8,128)(2,1)S(1)}, bf16[1,2048,512]{2,1,0:T(8,128)(2,1)}, u32[]{:S(2)}) copy-start(bf16[1,2048,512]{2,1,0:T(8,128)(2,1)} %param.5) | copy-start | bytes 6291460
  69.6 68.8 %all-to-all-start = ((bf16[2,128,16,512]{3,1,0,2:T(8,128)(2,1)}), bf16[2,128,16,512]{3,1,0,2:T(8,128)(2,1)}, u32[]{:S(2)}, u32[]{:S(2)}) async-start(bf16[2,128,16,512]{3,1,0,2:T(8,128)(2,1)} %copy.20), calls=%async_computation | async-start | bytes 8388608 | tf_op jit(solution)/shard_map/all_to_all | solution.py:17
  76.3 156.6 %reduce-scatter.2.cloned.1.call-start = ((), (), s32[]{:S(2)}) async-start(), calls=%async_computation.4 | async-start | bytes 8912896 | tf_op jit(solution)/shard_map/reduce_scatter | solution.py:49
  76.4 64.7 %collective-permute-start = (bf16[2048,512]{1,0:T(8,128)(2,1)S(1)}, bf16[2048,512]{1,0:T(8,128)(2,1)}, u32[]{:S(2)}, u32[]{:S(2)}) collective-permute-start(bf16[2048,512]{1,0:T(8,128)(2,1)S(1)} %bitcast.85), channel_id=1, source_target_pairs={{0,64},{64,0},{1,65},{65,1},{2,66},{66,2},{3,67},{67,3},{4,68},{68... | collective-permute-start | bytes 6291464 | tf_op jit(solution)/shard_map/ppermute | solution.py:9
  147.9 1.2 copy-start
  147.9 87.1 %copy-start.2 = (bf16[1,2,2,64,2048]{4,3,2,1,0:T(8,128)(2,1)S(1)}, bf16[1,2,2,64,2048]{4,3,2,1,0:T(8,128)(2,1)}, u32[]{:S(2)}) copy-start(bf16[1,2,2,64,2048]{4,3,2,1,0:T(8,128)(2,1)} %param.6) | copy-start | bytes 3145732
  147.9 118.9 %all-gather.8.cloned.1.call-start = ((), (), s32[]{:S(2)}) async-start(), calls=%async_computation.5 | async-start | bytes 2621440 | tf_op jit(solution)/shard_map/all_gather | solution.py:15
  234.9 74.6 %all-reduce.3.cloned.1.call-start = ((), (), s32[]{:S(2)}) async-start(), calls=%async_computation.7 | async-start | bytes 524288 | tf_op jit(solution)/shard_map/psum | solution.py:22
  237.1 187.6 %all-gather.10.cloned.1.call-start = ((), (), s32[]{:S(2)}) async-start(), calls=%async_computation.6 | async-start | bytes 17825792 | tf_op jit(solution)/shard_map/all_gather | solution.py:38
  269.2 9.0 %copy-start.1 = (bf16[128,2048]{1,0:T(8,128)(2,1)S(1)}, bf16[128,2048]{1,0:T(8,128)(2,1)}, u32[]{:S(2)}) copy-start(bf16[128,2048]{1,0:T(8,128)(2,1)} %fusion.8) | copy-start | bytes 1572868
  271.7 43.6 %all-to-all-start.1 = ((bf16[1,128,16,512]{3,1,0,2:T(8,128)(2,1)}), bf16[1,128,16,512]{3,1,0,2:T(8,128)(2,1)S(1)}, u32[]{:S(2)}, u32[]{:S(2)}) async-start(bf16[1,128,16,512]{3,1,0,2:T(8,128)(2,1)} %copy.24), calls=%async_computation.2 | async-start | bytes 4194304 | tf_op jit(solution)/shard_map/all_to_all | solution.py:17
  291.5 18.0 %collective-permute-start.1 = (f32[1,2,64,64]{3,2,1,0:T(8,128)S(1)}, f32[1,2,64,64]{3,2,1,0:T(8,128)S(1)}, u32[]{:S(2)}, u32[]{:S(2)}) collective-permute-start(f32[1,2,64,64]{3,2,1,0:T(8,128)S(1)} %psum.30), channel_id=1, source_target_pairs={{0,64},{64,0},{1,65},{65,1},{2,66},{66,2},{3,67},{67,3},{4,68},{68... | collective-permute-start | bytes 98312 | tf_op jit(solution)/shard_map/ppermute | solution.py:9
  315.3 119.3 %collective-permute-start.2 = (bf16[1,2048,512]{2,1,0:T(8,128)(2,1)S(1)}, bf16[1,2048,512]{2,1,0:T(8,128)(2,1)}, u32[]{:S(2)}, u32[]{:S(2)}) collective-permute-start(bf16[1,2048,512]{2,1,0:T(8,128)(2,1)S(1)} %bitcast.73), channel_id=1, source_target_pairs={{0,64},{64,0},{1,65},{65,1},{2,66},{66,2},{3,67},{67,3},{4,68},{68... | collective-permute-start | bytes 6291464 | tf_op jit(solution)/shard_map/ppermute | solution.py:9
Sparse Core Ops, SparseCore 0:
  9.6 51.4 all-gather.5
  148.0 84.8 reduce-scatter.1
  235.0 31.6 all-gather.7
  269.0 40.4 all-reduce.2
  311.5 113.2 all-gather.9

commit v2 on v1

v2 whole, which is shorter than its diff:
```python
import jax
import jax.numpy as jnp
from jax import lax
from jax.sharding import PartitionSpec as P


def swapped(value, axis):
    count = lax.axis_size(axis)
    return lax.ppermute(value, axis, [(source, count - 1 - source) for source in range(count)])


def gather_features(values, axis):
    count = lax.axis_size(axis)
    position = lax.axis_index(axis)
    pieces = [values]
    for offset in range(1, count):
        pieces.append(
            lax.ppermute(values, axis, [(source, (source + offset) % count) for source in range(count)])
        )
    stacked = jnp.stack(pieces)
    order = (position - jnp.arange(count)) % count
    ordered = jnp.take(stacked, order, axis=0)
    ordered = jnp.moveaxis(ordered, 0, -2)
    return ordered.reshape(values.shape[:-1] + (count * values.shape[-1],))


def to_column_blocks(full, group_count, column_part):
    example_count, length_count, _ = full.shape
    token_count = example_count * length_count
    by_block = full.reshape(token_count, group_count, column_part)
    moved = lax.all_to_all(by_block, "dp", split_axis=1, concat_axis=0, tiled=True)
    return moved.reshape(group_count * token_count, column_part)


def token_grams(values):
    return jnp.einsum("...ld,...kd->...lk", values, values, preferred_element_type=jnp.float32)


def by_micro(is_last, own, other):
    return jnp.where(is_last, jnp.stack([other, own]), jnp.stack([own, other]))


def local(weights, inputs, cotangent, clip_norm, noise):
    section_index = lax.axis_index("pipe")
    group_count = lax.axis_size("dp")
    weight_block = weights[0]
    local_inputs = inputs[0]
    micro_count, example_count, length_count, width_part = local_inputs.shape
    token_count = example_count * length_count
    column_part = weight_block.shape[1]
    full_width = column_part * group_count
    is_last = section_index == 1

    gathered_inputs = lax.all_gather(local_inputs, "dp", axis=1, tiled=True)
    input_grams = lax.psum(token_grams(local_inputs), "tensor")
    other_input_grams = swapped(input_grams, "pipe")

    own_cotangent = lax.dynamic_index_in_dim(cotangent, section_index, 0, keepdims=False)
    full_last = gather_features(own_cotangent, "tensor")
    last_grams = token_grams(full_last)
    last_blocks = to_column_blocks(full_last, group_count, column_part)
    last_blocks_other = swapped(last_blocks, "pipe")

    last_weights = jnp.where(is_last, weight_block, swapped(weight_block, "pipe"))
    terms = lax.dot_general(
        last_blocks, last_weights, (((1,), (1,)), ((), ())), preferred_element_type=jnp.float32
    ).astype(jnp.bfloat16)
    summed = lax.psum_scatter(terms, "dp", scatter_dimension=0, tiled=True).astype(jnp.float32)
    renewed = (own_cotangent.reshape(token_count, width_part).astype(jnp.float32) + summed).astype(
        jnp.bfloat16
    ).reshape(example_count, length_count, width_part)
    full_first = gather_features(renewed, "tensor")
    first_grams = token_grams(full_first)
    first_blocks = to_column_blocks(full_first, group_count, column_part)
    first_blocks_other = swapped(first_blocks, "pipe")

    own_input_grams = lax.dynamic_index_in_dim(input_grams, section_index, 0, keepdims=False)
    held_input_grams = lax.dynamic_index_in_dim(other_input_grams, section_index, 0, keepdims=False)
    last_input_grams = jnp.where(is_last, own_input_grams, held_input_grams)
    first_input_grams = jnp.where(is_last, held_input_grams, own_input_grams)
    norm_square = jnp.sum(first_input_grams * first_grams, axis=(1, 2)) + jnp.sum(
        last_input_grams * last_grams, axis=(1, 2)
    )
    bound = clip_norm[0]
    own_scales = bound / jnp.maximum(jnp.sqrt(norm_square), bound)
    scale_terms = by_micro(is_last, own_scales, swapped(own_scales, "pipe"))
    all_scales = lax.all_gather(scale_terms, "dp", axis=1, tiled=True)

    grad_blocks = jnp.where(
        is_last,
        by_micro(is_last, last_blocks, last_blocks_other),
        by_micro(is_last, first_blocks, first_blocks_other),
    )
    clipped = (gathered_inputs.astype(jnp.float32) * all_scales[:, :, None, None]).astype(jnp.bfloat16)
    flat_inputs = clipped.reshape(micro_count * group_count * token_count, width_part)
    flat_grads = grad_blocks.reshape(micro_count * group_count * token_count, column_part)
    summed_grad = lax.dot_general(
        flat_inputs, flat_grads, (((0,), (0,)), ((), ())), preferred_element_type=jnp.float32
    )
    noise_weight = 1.5 / full_width
    per_example_sum = micro_count * group_count * example_count
    final_output = (
        summed_grad + noise_weight * bound * noise[0].astype(jnp.float32)
    ) / per_example_sum
    return (final_output[None], scale_terms)


def solution(mesh):
    in_specs = (
        P("pipe", "tensor", "dp"),
        P("pipe", None, "dp", None, "tensor"),
        P(None, "dp", None, "tensor"),
        P(),
        P("pipe", "tensor", "dp"),
    )
    out_specs = (P("pipe", "tensor", "dp"), P(None, "dp"))
    return jax.shard_map(local, mesh=mesh, in_specs=in_specs, out_specs=out_specs, check_vma=False)
```

time: 457 us -> 356 us (0.78)
  waiting for transfers between devices: 330 us -> 203 us
  blocking collectives: 37.2 us -> 19 us
  local copies, waits for them, and re-layouts: 17.4 us -> 30.3 us
  other arithmetic: 17.4 us -> 29.4 us
  starting transfers between devices: 18.9 us -> 30.9 us
    all_gather x1, waiting for transfers between devices: 88.8 us -> 0.01 us  [local(): gathered_inputs = lax.all_gather(local_inputs, 'dp', axis=1, tiled=True)]
    all_gather x2 -> x0, waiting for transfers between devices: 82.3 us -> none  [to_column_blocks(): full = lax.all_gather(values, 'tensor', axis=3, tiled=True)]
    ppermute x0 -> x6, waiting for transfers between devices: none -> 41.2 us  [gather_features(): lax.ppermute(values, axis, [(source, (source + offset) % count) for sourc...]
    psum x2 -> x0, blocking collectives: 17.6 us -> none  [the longest x1 13 us: grams(): lax.psum(jnp.einsum('...ld,...kd->...lk', values, values, preferred_eleme...]
    another operation x0 -> x4, local copies, waits for them, and re-layouts: none -> 15.8 us  [to_column_blocks(): by_block = full.reshape(token_count, group_count, column_part)]
    all_to_all x2, waiting for transfers between devices: 60.9 us -> 76 us  [to_column_blocks(): lax.all_to_all(by_block, 'dp', split_axis=1, concat_axis=0, tiled=True)]
    psum x1, waiting for transfers between devices: 13.4 us -> 0.03 us  [local(): input_grams = lax.psum(token_grams(local_inputs), 'tensor')]
    ppermute x0 -> x6, starting transfers between devices: none -> 11.6 us  [gather_features(): lax.ppermute(values, axis, [(source, (source + offset) % count) for sourc...]
  transfers between devices with their start and end apart: 10 -> 16, of which waited for: 6 -> 10; matrix products, arithmetic and copies ran while one was open for 5% -> 15% of each run, Pallas kernels for 0% -> 0%
where the time goes in v2:
time: 356 us; the launch traced here: 353 us
  waiting for transfers between devices  203 us (57%)
  starting transfers between devices  30.9 us (9%)
  local copies, waits for them, and re-layouts  30.3 us (9%)
  other arithmetic  29.4 us (8%)
  matrix products  24.1 us (7%)
  blocking collectives  19 us (5%)
  between operations  16.3 us (5%)
    reduce_scatter x1, waiting for transfers between devices, local(): lax.psum_scatter(terms, 'dp', scatter_dimension=0, tiled=True)  84.4 us
    all_to_all x2, waiting for transfers between devices, to_column_blocks(): lax.all_to_all(by_block, 'dp', split_axis=1, concat_axis=0, tiled=True)  76 us
    ppermute x6, waiting for transfers between devices, gather_features(): lax.ppermute(values, axis, [(source, (source + offset) % count) for sourc...  41.2 us
    all_gather x1, blocking collectives, local(): all_scales = lax.all_gather(scale_terms, 'dp', axis=1, tiled=True)  19 us
    another operation x4, local copies, waits for them, and re-layouts, to_column_blocks(): by_block = full.reshape(token_count, group_count, column_part)  15.8 us
    dot_general x1, matrix products, local(): lax.dot_general(flat_inputs, flat_grads, (((0,), (0,)), ((), ())), prefer...  11.7 us
    ppermute x6, starting transfers between devices, gather_features(): lax.ppermute(values, axis, [(source, (source + offset) % count) for sourc...  11.6 us
    all_to_all x2, starting transfers between devices, to_column_blocks(): lax.all_to_all(by_block, 'dp', split_axis=1, concat_axis=0, tiled=True)  11.2 us
  transfers between devices with their start and end apart: 16, of which 10 were waited for; matrix products, arithmetic and copies ran while one was open for 15% of the time, Pallas kernels for 0%

profile of v2, /device:TPU:1, one launch (start us, length us, event | category | flops | bytes accessed | tf_op | source)
XLA Modules:
  0.0 353.4 jit_solution(14359453989975854433)
XLA Ops:
  11.8 3.3 collective-permute-start.2
  17.4 8.1 %collective-permute-done.1 = bf16[2,64,2048]{2,1,0:T(8,128)(2,1)S(1)} collective-permute-done((bf16[2,64,2048]{2,1,0:T(8,128)(2,1)S(1)}, bf16[2,64,2048]{2,1,0:T(8,128)(2,1)S(1)}, u32[]{:S(2)}, u32[]{:S(2)}) %collective-permute-start.1) | collective-permute-done | bytes 524320 | tf_op jit(solution)/shard_map/ppermute | solution.py:18
  25.5 12.1 %collective-permute-done.2 = bf16[2,64,2048]{2,1,0:T(8,128)(2,1)S(1)} collective-permute-done((bf16[2,64,2048]{2,1,0:T(8,128)(2,1)S(1)}, bf16[2,64,2048]{2,1,0:T(8,128)(2,1)S(1)}, u32[]{:S(2)}, u32[]{:S(2)}) %collective-permute-start.2) | collective-permute-done | bytes 524320 | tf_op jit(solution)/shard_map/ppermute | solution.py:18
  37.7 2.6 pad_maximum_fusion
  45.9 2.6 reshape_reshape.6
  48.5 4.1 %copy.38 = bf16[128,16,512]{2,0,1:T(8,128)(2,1)} copy(bf16[128,16,512]{2,1,0:T(8,128)(2,1)} %reshape_reshape.6) | data formatting | bytes 4194304 | tf_op jit(solution)/shard_map/reshape;reshape | solution.py:30
  52.6 6.8 %all-to-all-start = ((bf16[128,16,512]{2,0,1:T(8,128)(2,1)}), bf16[128,16,512]{2,0,1:T(8,128)(2,1)S(1)}, u32[]{:S(2)}, u32[]{:S(2)}) async-start(bf16[128,16,512]{2,0,1:T(8,128)(2,1)} %copy.38), calls=%async_computation | async-start | bytes 4194304 | tf_op jit(solution)/shard_map/all_to_all | solution.py:31
  59.4 28.0 %all-to-all-done = bf16[128,16,512]{2,0,1:T(8,128)(2,1)S(1)} async-done(((bf16[128,16,512]{2,0,1:T(8,128)(2,1)}), bf16[128,16,512]{2,0,1:T(8,128)(2,1)S(1)}, u32[]{:S(2)}, u32[]{:S(2)}) %all-to-all-start) | async-done | bytes 2097184 | tf_op jit(solution)/shard_map/all_to_all | solution.py:31
  87.4 8.4 %convolution_convert_fusion = bf16[2048,2048]{1,0:T(8,128)(2,1)} fusion(bf16[2048,512]{1,0:T(8,128)(2,1)S(1)} %bitcast.88, bf16[2048,512]{1,0:T(8,128)(2,1)} %collective-permute-done.4, pred[]{:T(512)S(6)} %eq.6, bf16[1,2048,512]{2,1,0:T(8,128)(2,1)} %param.7), kind=kOutput, calls=%fused_computation.4 | convolution fusion | flops 4300210176 | bytes 14680065 | tf_op jit(solution)/shard_map/dot_general | solution.py:65
  99.2 84.4 %reduce-scatter.2.cloned.1.call-done = bf16[128,2048]{1,0:T(8,128)(2,1)} async-done(((bf16[2048,2048]{1,0:T(8,128)(2,1)}), bf16[128,2048]{1,0:T(8,128)(2,1)}) %reduce-scatter.2.cloned.1.call-update) | async-done | bytes 524304 | tf_op jit(solution)/shard_map/reduce_scatter | solution.py:68
  189.8 7.6 %collective-permute-done.5 = bf16[2,64,2048]{2,1,0:T(8,128)(2,1)S(1)} collective-permute-done((bf16[2,64,2048]{2,1,0:T(8,128)(2,1)S(1)}, bf16[2,64,2048]{2,1,0:T(8,128)(2,1)S(1)}, u32[]{:S(2)}, u32[]{:S(2)}) %collective-permute-start.5) | collective-permute-done | bytes 524320 | tf_op jit(solution)/shard_map/ppermute | solution.py:18
  197.4 12.5 %collective-permute-done.6 = bf16[2,64,2048]{2,1,0:T(8,128)(2,1)S(1)} collective-permute-done((bf16[2,64,2048]{2,1,0:T(8,128)(2,1)S(1)}, bf16[2,64,2048]{2,1,0:T(8,128)(2,1)S(1)}, u32[]{:S(2)}, u32[]{:S(2)}) %collective-permute-start.6) | collective-permute-done | bytes 524320 | tf_op jit(solution)/shard_map/ppermute | solution.py:18
  212.4 3.6 %gather_fusion.1 = bf16[4,2,64,2048]{3,2,1,0:T(8,128)(2,1)} fusion(bf16[4,2,64,2048]{3,2,1,0:T(8,128)(2,1)} %pad_maximum_fusion.1, s32[1024]{0:T(1024)S(1)} %pad_clamp_fusion), kind=kCustom, calls=%fused_computation.1.clone | custom fusion | bytes 4194320 | tf_op jit(solution)/shard_map/jit(_take)/gather | solution.py:22
  216.0 3.3 fusion.10
  219.3 3.0 copy.39
  222.2 4.4 %reshape_reshape.7 = bf16[128,16,512]{2,1,0:T(8,128)(2,1)} reshape(bf16[2,64,4,2048]{3,2,1,0:T(4,128)(2,1)} %copy.39) | data formatting | bytes 4194304 | tf_op jit(solution)/shard_map/reshape;reshape | solution.py:30
  226.6 4.7 %copy.44 = bf16[128,16,512]{2,0,1:T(8,128)(2,1)} copy(bf16[128,16,512]{2,1,0:T(8,128)(2,1)} %reshape_reshape.7) | data formatting | bytes 4194304 | tf_op jit(solution)/shard_map/reshape;reshape | solution.py:30
  231.3 4.4 %all-to-all-start.1 = ((bf16[128,16,512]{2,0,1:T(8,128)(2,1)}), bf16[128,16,512]{2,0,1:T(8,128)(2,1)}, u32[]{:S(2)}, u32[]{:S(2)}) async-start(bf16[128,16,512]{2,0,1:T(8,128)(2,1)} %copy.44), calls=%async_computation.2 | async-start | bytes 4194304 | tf_op jit(solution)/shard_map/all_to_all | solution.py:31
  238.3 48.0 %all-to-all-done.1 = bf16[128,16,512]{2,0,1:T(8,128)(2,1)} async-done(((bf16[128,16,512]{2,0,1:T(8,128)(2,1)}), bf16[128,16,512]{2,0,1:T(8,128)(2,1)}, u32[]{:S(2)}, u32[]{:S(2)}) %all-to-all-start.1) | async-done | bytes 2097184 | tf_op jit(solution)/shard_map/all_to_all | solution.py:31
  286.3 3.3 collective-permute-start.10
  296.1 19.0 %all-gather.1 = f32[16,2,2]{2,1,0:T(2,128)S(1)} all-gather(f32[1,2,2]{2,1,0:T(2,128)S(1)} %bitcast.105), channel_id=1, replica_groups=mesh['pipe'=2,'dp'=16,'tensor'=4] {'dp'}, dimensions={0}, use_global_device_ids=true | all-gather | bytes 272 | tf_op jit(solution)/shard_map/all_gather | solution.py:87
  315.8 8.4 %fusion.1 = bf16[2,2048,512]{2,1,0:T(8,128)(2,1)} fusion(bf16[1,2048,512]{2,1,0:T(8,128)(2,1)S(1)} %bitcast.90, bf16[1,2048,512]{2,1,0:T(8,128)(2,1)} %bitcast.30, bf16[1,2048,512]{2,1,0:T(8,128)(2,1)} %bitcast.38, bf16[1,2048,512]{2,1,0:T(8,128)(2,1)} %bitcast.36, pred[]{:T(512)S(6)} %eq.6), kind=kLoop, calls=%fused_computation.6 | loop fusion | flops 14680064 | bytes 12582913 | tf_op jit(solution)/shard_map/jit(_where)/select_n | solution.py:89
  324.2 10.1 %fusion = bf16[2,32,64,2048]{3,2,1,0:T(8,128)(2,1)S(1)} fusion(bf16[1,2,32,64,2048]{4,3,2,1,0:T(8,128)(2,1)} %all-gather.4.cloned.1.call-done, f32[2,32]{1,0:T(2,128)S(1)} %bitcast.104), kind=kLoop, calls=%fused_computation.3 | loop fusion | flops 25165824 | bytes 33554688 | tf_op jit(solution)/shard_map/convert_element_type | solution.py:94
  334.3 11.7 %fusion.3 = f32[1,2048,512]{2,1,0:T(8,128)} fusion(bf16[1,2048,512]{2,1,0:T(8,128)(2,1)} %param.11, bf16[4096,2048]{1,0:T(8,128)(2,1)S(1)} %bitcast.87, bf16[4096,512]{1,0:T(8,128)(2,1)S(1)} %bitcast.91, f32[]{:T(128)S(6)} %mul_shard_map.3), kind=kOutput, calls=%fused_computation.10 | convolution fusion | flops 8594128896 | bytes 27262980 | tf_op jit(solution)/shard_map/dot_general | solution.py:97
  (54 shorter events, 32.8 us)
Async XLA Ops:
  8.0 1.2 copy-start
  9.3 16.3 %collective-permute-start.1 = (bf16[2,64,2048]{2,1,0:T(8,128)(2,1)S(1)}, bf16[2,64,2048]{2,1,0:T(8,128)(2,1)S(1)}, u32[]{:S(2)}, u32[]{:S(2)}) collective-permute-start(bf16[2,64,2048]{2,1,0:T(8,128)(2,1)S(1)} %fusion.26), channel_id=1, source_target_pairs={{0,1},{1,2},{2,3},{3,0},{4,5},{5,6},{6,7},{7,4},{8,9},{9,10},{10,1... | collective-permute-start | bytes 1572872 | tf_op jit(solution)/shard_map/ppermute | solution.py:18
  11.8 25.9 %collective-permute-start.2 = (bf16[2,64,2048]{2,1,0:T(8,128)(2,1)S(1)}, bf16[2,64,2048]{2,1,0:T(8,128)(2,1)S(1)}, u32[]{:S(2)}, u32[]{:S(2)}) collective-permute-start(bf16[2,64,2048]{2,1,0:T(8,128)(2,1)S(1)} %fusion.26), channel_id=1, source_target_pairs={{0,2},{1,3},{2,0},{3,1},{4,6},{5,7},{6,4},{7,5},{8,10},{9,11},{10,... | collective-permute-start | bytes 1572872 | tf_op jit(solution)/shard_map/ppermute | solution.py:18
  15.1 22.6 %collective-permute-start.3 = (bf16[2,64,2048]{2,1,0:T(8,128)(2,1)S(1)}, bf16[2,64,2048]{2,1,0:T(8,128)(2,1)}, u32[]{:S(2)}, u32[]{:S(2)}) collective-permute-start(bf16[2,64,2048]{2,1,0:T(8,128)(2,1)S(1)} %fusion.26), channel_id=1, source_target_pairs={{0,3},{1,0},{2,1},{3,2},{4,7},{5,4},{6,5},{7,6},{8,11},{9,8},{10,9... | collective-permute-start | bytes 1572872 | tf_op jit(solution)/shard_map/ppermute | solution.py:18
  15.8 43.6 %collective-permute-start.4 = (bf16[2048,512]{1,0:T(8,128)(2,1)}, bf16[2048,512]{1,0:T(8,128)(2,1)}, u32[]{:S(2)}, u32[]{:S(2)}) collective-permute-start(bf16[2048,512]{1,0:T(8,128)(2,1)} %bitcast.108), channel_id=1, source_target_pairs={{0,64},{64,0},{1,65},{65,1},{2,66},{66,2},{3,67},{67,3},{4,68},{68... | collective-permute-start | bytes 6291464 | tf_op jit(solution)/shard_map/ppermute | solution.py:9
  52.6 34.8 %all-to-all-start = ((bf16[128,16,512]{2,0,1:T(8,128)(2,1)}), bf16[128,16,512]{2,0,1:T(8,128)(2,1)S(1)}, u32[]{:S(2)}, u32[]{:S(2)}) async-start(bf16[128,16,512]{2,0,1:T(8,128)(2,1)} %copy.38), calls=%async_computation | async-start | bytes 4194304 | tf_op jit(solution)/shard_map/all_to_all | solution.py:31
  59.4 124.2 %reduce-scatter.2.cloned.1.call-start = ((), (), s32[]{:S(2)}) async-start(), calls=%async_computation.4 | async-start | bytes 8912896 | tf_op jit(solution)/shard_map/reduce_scatter | solution.py:68
  95.8 194.5 %all-reduce.2.cloned.1.call-start = ((), (), s32[]{:S(2)}) async-start(), calls=%async_computation.3 | async-start | bytes 262144 | tf_op jit(solution)/shard_map/psum | solution.py:55
  98.5 225.7 %all-gather.4.cloned.1.call-start = ((), (), s32[]{:S(2)}) async-start(), calls=%async_computation.5 | async-start | bytes 17825792 | tf_op jit(solution)/shard_map/all_gather | solution.py:54
  184.7 12.6 %collective-permute-start.5 = (bf16[2,64,2048]{2,1,0:T(8,128)(2,1)S(1)}, bf16[2,64,2048]{2,1,0:T(8,128)(2,1)S(1)}, u32[]{:S(2)}, u32[]{:S(2)}) collective-permute-start(bf16[2,64,2048]{2,1,0:T(8,128)(2,1)S(1)} %bitcast.92), channel_id=1, source_target_pairs={{0,1},{1,2},{2,3},{3,0},{4,5},{5,6},{6,7},{7,4},{8,9},{9,10},{10,1... | collective-permute-start | bytes 1572872 | tf_op jit(solution)/shard_map/ppermute | solution.py:18
  186.1 23.8 %collective-permute-start.6 = (bf16[2,64,2048]{2,1,0:T(8,128)(2,1)S(1)}, bf16[2,64,2048]{2,1,0:T(8,128)(2,1)S(1)}, u32[]{:S(2)}, u32[]{:S(2)}) collective-permute-start(bf16[2,64,2048]{2,1,0:T(8,128)(2,1)S(1)} %bitcast.93), channel_id=1, source_target_pairs={{0,2},{1,3},{2,0},{3,1},{4,6},{5,7},{6,4},{7,5},{8,10},{9,11},{10,... | collective-permute-start | bytes 1572872 | tf_op jit(solution)/shard_map/ppermute | solution.py:18
  188.7 22.1 %collective-permute-start.7 = (bf16[2,64,2048]{2,1,0:T(8,128)(2,1)S(1)}, bf16[2,64,2048]{2,1,0:T(8,128)(2,1)S(1)}, u32[]{:S(2)}, u32[]{:S(2)}) collective-permute-start(bf16[2,64,2048]{2,1,0:T(8,128)(2,1)S(1)} %bitcast.94), channel_id=1, source_target_pairs={{0,3},{1,0},{2,1},{3,2},{4,7},{5,4},{6,5},{7,6},{8,11},{9,8},{10,9... | collective-permute-start | bytes 1572872 | tf_op jit(solution)/shard_map/ppermute | solution.py:18
  231.3 55.0 %all-to-all-start.1 = ((bf16[128,16,512]{2,0,1:T(8,128)(2,1)}), bf16[128,16,512]{2,0,1:T(8,128)(2,1)}, u32[]{:S(2)}, u32[]{:S(2)}) async-start(bf16[128,16,512]{2,0,1:T(8,128)(2,1)} %copy.44), calls=%async_computation.2 | async-start | bytes 4194304 | tf_op jit(solution)/shard_map/all_to_all | solution.py:31
  235.8 80.0 %collective-permute-start.9 = (bf16[2048,512]{1,0:T(8,128)(2,1)S(1)}, bf16[2048,512]{1,0:T(8,128)(2,1)}, u32[]{:S(2)}, u32[]{:S(2)}) collective-permute-start(bf16[2048,512]{1,0:T(8,128)(2,1)S(1)} %bitcast.89), channel_id=1, source_target_pairs={{0,64},{64,0},{1,65},{65,1},{2,66},{66,2},{3,67},{67,3},{4,68},{68... | collective-permute-start | bytes 6291464 | tf_op jit(solution)/shard_map/ppermute | solution.py:9
  286.3 29.4 %collective-permute-start.10 = (bf16[2048,512]{1,0:T(8,128)(2,1)}, bf16[2048,512]{1,0:T(8,128)(2,1)}, u32[]{:S(2)}, u32[]{:S(2)}) collective-permute-start(bf16[2048,512]{1,0:T(8,128)(2,1)} %bitcast.35), channel_id=1, source_target_pairs={{0,64},{64,0},{1,65},{65,1},{2,66},{66,2},{3,67},{67,3},{4,68},{68... | collective-permute-start | bytes 6291464 | tf_op jit(solution)/shard_map/ppermute | solution.py:9
  290.3 3.5 collective-permute-start
  290.4 2.2 copy-start.2
  292.8 0.9 copy-start.4
  294.6 1.4 collective-permute-start.8
  324.2 10.1 %copy-start.3 = (bf16[2,2048,512]{2,1,0:T(8,128)(2,1)S(1)}, bf16[2,2048,512]{2,1,0:T(8,128)(2,1)}, u32[]{:S(2)}) copy-start(bf16[2,2048,512]{2,1,0:T(8,128)(2,1)} %fusion.1) | copy-start | bytes 12582916
  334.3 11.7 %copy-start.1 = (bf16[2,2,64,2048]{3,2,1,0:T(8,128)(2,1)S(1)}, bf16[2,2,64,2048]{3,2,1,0:T(8,128)(2,1)}, u32[]{:S(2)}) copy-start(bf16[2,2,64,2048]{3,2,1,0:T(8,128)(2,1)} %param.9) | copy-start | bytes 3145732
Sparse Core Ops, SparseCore 0:
  95.9 87.6 reduce-scatter.1
  185.7 134.3 all-gather.3
Sparse Core Ops, SparseCore 1:
  98.6 42.8 all-reduce.1

commit v3 on v2

--- a/solution.py
+++ b/solution.py
@@ -9,7 +9,7 @@
     return lax.ppermute(value, axis, [(source, count - 1 - source) for source in range(count)])
 
 
-def gather_features(values, axis):
+def ring_pieces(values, axis):
     count = lax.axis_size(axis)
     position = lax.axis_index(axis)
     pieces = [values]
@@ -18,18 +18,20 @@
             lax.ppermute(values, axis, [(source, (source + offset) % count) for source in range(count)])
         )
     stacked = jnp.stack(pieces)
-    order = (position - jnp.arange(count)) % count
-    ordered = jnp.take(stacked, order, axis=0)
-    ordered = jnp.moveaxis(ordered, 0, -2)
-    return ordered.reshape(values.shape[:-1] + (count * values.shape[-1],))
+    return stacked, (position - jnp.arange(count)) % count
 
 
-def to_column_blocks(full, group_count, column_part):
-    example_count, length_count, _ = full.shape
+def column_blocks(values, group_count, column_part):
+    example_count, length_count, width_part = values.shape
     token_count = example_count * length_count
-    by_block = full.reshape(token_count, group_count, column_part)
-    moved = lax.all_to_all(by_block, "dp", split_axis=1, concat_axis=0, tiled=True)
-    return moved.reshape(group_count * token_count, column_part)
+    stacked, order = ring_pieces(values, "tensor")
+    grams = jnp.einsum("jeld,jekd->elk", stacked, stacked, preferred_element_type=jnp.float32)
+    pieces = stacked.shape[0]
+    per_piece = width_part // column_part
+    chunks = stacked.reshape(pieces, token_count, per_piece, column_part).transpose(0, 2, 1, 3)
+    chunks = jnp.take(chunks, order, axis=0).reshape(pieces * per_piece, token_count, column_part)
+    moved = lax.all_to_all(chunks, "dp", split_axis=0, concat_axis=1, tiled=True)
+    return grams, moved.reshape(group_count * token_count, column_part)
 
 
 def token_grams(values):
@@ -56,9 +58,7 @@
     other_input_grams = swapped(input_grams, "pipe")
 
     own_cotangent = lax.dynamic_index_in_dim(cotangent, section_index, 0, keepdims=False)
-    full_last = gather_features(own_cotangent, "tensor")
-    last_grams = token_grams(full_last)
-    last_blocks = to_column_blocks(full_last, group_count, column_part)
+    last_grams, last_blocks = column_blocks(own_cotangent, group_count, column_part)
     last_blocks_other = swapped(last_blocks, "pipe")
 
     last_weights = jnp.where(is_last, weight_block, swapped(weight_block, "pipe"))
@@ -69,9 +69,7 @@
     renewed = (own_cotangent.reshape(token_count, width_part).astype(jnp.float32) + summed).astype(
         jnp.bfloat16
     ).reshape(example_count, length_count, width_part)
-    full_first = gather_features(renewed, "tensor")
-    first_grams = token_grams(full_first)
-    first_blocks = to_column_blocks(full_first, group_count, column_part)
+    first_grams, first_blocks = column_blocks(renewed, group_count, column_part)
     first_blocks_other = swapped(first_blocks, "pipe")
 
     own_input_grams = lax.dynamic_index_in_dim(input_grams, section_index, 0, keepdims=False)
@@ -84,16 +82,22 @@
     bound = clip_norm[0]
     own_scales = bound / jnp.maximum(jnp.sqrt(norm_square), bound)
     scale_terms = by_micro(is_last, own_scales, swapped(own_scales, "pipe"))
-    all_scales = lax.all_gather(scale_terms, "dp", axis=1, tiled=True)
+    scale_pieces, scale_order = ring_pieces(scale_terms, "dp")
+    all_scales = jnp.take(scale_pieces, scale_order, axis=0).transpose(1, 0, 2)
 
     grad_blocks = jnp.where(
         is_last,
         by_micro(is_last, last_blocks, last_blocks_other),
         by_micro(is_last, first_blocks, first_blocks_other),
     )
-    clipped = (gathered_inputs.astype(jnp.float32) * all_scales[:, :, None, None]).astype(jnp.bfloat16)
-    flat_inputs = clipped.reshape(micro_count * group_count * token_count, width_part)
-    flat_grads = grad_blocks.reshape(micro_count * group_count * token_count, column_part)
+    scaled_blocks = (
+        grad_blocks.reshape(micro_count, group_count, example_count, length_count, column_part).astype(
+            jnp.float32
+        )
+        * all_scales[:, :, :, None, None]
+    ).astype(jnp.bfloat16)
+    flat_inputs = gathered_inputs.reshape(micro_count * group_count * token_count, width_part)
+    flat_grads = scaled_blocks.reshape(micro_count * group_count * token_count, column_part)
     summed_grad = lax.dot_general(
         flat_inputs, flat_grads, (((0,), (0,)), ((), ())), preferred_element_type=jnp.float32
     )

time: 356 us -> 344 us (0.966)
  starting transfers between devices: 30.9 us -> 65.4 us
  waiting for transfers between devices: 203 us -> 177 us
  blocking collectives: 19 us -> 0 us
  other arithmetic: 29.4 us -> 20 us
  matrix products: 24.1 us -> 32.4 us
    all_to_all x2, waiting for transfers between devices: 76 us -> 28 us  [column_blocks(): lax.all_to_all(chunks, 'dp', split_axis=0, concat_axis=1, tiled=True)]
    ppermute x6 -> x21, starting transfers between devices: 11.6 us -> 40.1 us  [ring_pieces(): lax.ppermute(values, axis, [(source, (source + offset) % count) for sourc...]
    ppermute x6 -> x21, waiting for transfers between devices: 41.2 us -> 60.3 us  [ring_pieces(): lax.ppermute(values, axis, [(source, (source + offset) % count) for sourc...]
    all_gather x1 -> x0, blocking collectives: 19 us -> none  [local(): all_scales = lax.all_gather(scale_terms, 'dp', axis=1, tiled=True)]
    unnamed x12 -> x31, local copies, waits for them, and re-layouts: 1.74 us -> 10.8 us
    all_gather x1, waiting for transfers between devices: 0.01 us -> 8.5 us  [local(): gathered_inputs = lax.all_gather(local_inputs, 'dp', axis=1, tiled=True)]
    reduce_scatter x1, waiting for transfers between devices: 84.4 us -> 77.6 us  [local(): lax.psum_scatter(terms, 'dp', scatter_dimension=0, tiled=True)]
    dot_general x0 -> x2, matrix products: none -> 6.02 us  [column_blocks(): jnp.einsum('jeld,jekd->elk', stacked, stacked, preferred_element_type=jnp...]
  transfers between devices with their start and end apart: 16 -> 31, of which waited for: 10 -> 12; matrix products, arithmetic and copies ran while one was open for 15% -> 15% of each run, Pallas kernels for 0% -> 0%
where the time goes in v3:
time: 344 us; the launch traced here: 343 us
  waiting for transfers between devices  177 us (51%)
  starting transfers between devices  65.4 us (19%)
  matrix products  32.4 us (9%)
  local copies, waits for them, and re-layouts  31.4 us (9%)
  other arithmetic  20 us (6%)
  between operations  16.4 us (5%)
    reduce_scatter x1, waiting for transfers between devices, local(): lax.psum_scatter(terms, 'dp', scatter_dimension=0, tiled=True)  77.6 us
    ppermute x21, waiting for transfers between devices, ring_pieces(): lax.ppermute(values, axis, [(source, (source + offset) % count) for sourc...  60.3 us
    ppermute x21, starting transfers between devices, ring_pieces(): lax.ppermute(values, axis, [(source, (source + offset) % count) for sourc...  40.1 us
    all_to_all x2, waiting for transfers between devices, column_blocks(): lax.all_to_all(chunks, 'dp', split_axis=0, concat_axis=1, tiled=True)  28 us
    dot_general x1, matrix products, local(): lax.dot_general(flat_inputs, flat_grads, (((0,), (0,)), ((), ())), prefer...  15.3 us
    ppermute x5, starting transfers between devices, swapped(): lax.ppermute(value, axis, [(source, count - 1 - source) for source in ran...  13.6 us
    another operation x17, local copies, waits for them, and re-layouts, ring_pieces(): stacked = jnp.stack(pieces)  12.8 us
    all_to_all x2, starting transfers between devices, column_blocks(): lax.all_to_all(chunks, 'dp', split_axis=0, concat_axis=1, tiled=True)  11.6 us
  transfers between devices with their start and end apart: 31, of which 12 were waited for; matrix products, arithmetic and copies ran while one was open for 15% of the time, Pallas kernels for 0%

profile of v3, /device:TPU:1, one launch (start us, length us, event | category | flops | bytes accessed | tf_op | source)
XLA Modules:
  0.0 342.8 jit_solution(15328813472558895320)
XLA Ops:
  12.5 3.3 collective-permute-start.1
  19.5 7.0 %collective-permute-done = bf16[2,64,2048]{2,1,0:T(8,128)(2,1)S(1)} collective-permute-done((bf16[2,64,2048]{2,1,0:T(8,128)(2,1)}, bf16[2,64,2048]{2,1,0:T(8,128)(2,1)S(1)}, u32[]{:S(2)}, u32[]{:S(2)}) %collective-permute-start) | collective-permute-done | bytes 524320 | tf_op jit(solution)/shard_map/ppermute | solution.py:18
  27.8 10.9 %collective-permute-done.1 = bf16[2,64,2048]{2,1,0:T(8,128)(2,1)S(1)} collective-permute-done((bf16[2,64,2048]{2,1,0:T(8,128)(2,1)}, bf16[2,64,2048]{2,1,0:T(8,128)(2,1)S(1)}, u32[]{:S(2)}, u32[]{:S(2)}) %collective-permute-start.1) | collective-permute-done | bytes 524320 | tf_op jit(solution)/shard_map/ppermute | solution.py:18
  45.1 3.2 broadcast_select_fusion.1
  48.2 6.8 %all-to-all-start = ((bf16[16,128,512]{2,1,0:T(8,128)(2,1)}), bf16[16,128,512]{2,1,0:T(8,128)(2,1)S(1)}, u32[]{:S(2)}, u32[]{:S(2)}) async-start(bf16[16,128,512]{2,1,0:T(8,128)(2,1)} %bitcast.129), calls=%async_computation | async-start | bytes 4194304 | tf_op jit(solution)/shard_map/all_to_all | solution.py:33
  55.1 28.0 %all-to-all-done = bf16[16,128,512]{2,1,0:T(8,128)(2,1)S(1)} async-done(((bf16[16,128,512]{2,1,0:T(8,128)(2,1)}), bf16[16,128,512]{2,1,0:T(8,128)(2,1)S(1)}, u32[]{:S(2)}, u32[]{:S(2)}) %all-to-all-start) | async-done | bytes 2097184 | tf_op jit(solution)/shard_map/all_to_all | solution.py:33
  83.0 8.4 %convolution_convert_fusion = bf16[2048,2048]{1,0:T(8,128)(2,1)} fusion(bf16[2048,512]{1,0:T(8,128)(2,1)S(1)} %bitcast.125, bf16[2048,512]{1,0:T(8,128)(2,1)} %collective-permute-done.4, pred[]{:T(512)S(6)} %eq.8, bf16[1,2048,512]{2,1,0:T(8,128)(2,1)} %param.7), kind=kOutput, calls=%fused_computation.4 | convolution fusion | flops 4300210176 | bytes 14680065 | tf_op jit(solution)/shard_map/dot_general | solution.py:65
  95.6 4.0 %copy.140 = bf16[1,2048,512]{1,2,0:T(8,128)(2,1)} copy(bf16[1,2048,512]{2,1,0:T(8,128)(2,1)} %param.11) | data formatting | bytes 4194304 | tf_op args[4]
  100.4 77.6 %reduce-scatter.2.cloned.1.call-done = bf16[128,2048]{1,0:T(8,128)(2,1)} async-done(((bf16[2048,2048]{1,0:T(8,128)(2,1)}), bf16[128,2048]{1,0:T(8,128)(2,1)}) %reduce-scatter.2.cloned.1.call-update) | async-done | bytes 524304 | tf_op jit(solution)/shard_map/reduce_scatter | solution.py:68
  184.3 3.1 collective-permute-start.9
  188.6 3.2 fusion.30
  195.9 8.6 %collective-permute-done.6 = bf16[2,64,2048]{2,1,0:T(8,128)(2,1)} collective-permute-done((bf16[2,64,2048]{2,1,0:T(8,128)(2,1)S(1)}, bf16[2,64,2048]{2,1,0:T(8,128)(2,1)}, u32[]{:S(2)}, u32[]{:S(2)}) %collective-permute-start.6) | collective-permute-done | bytes 524320 | tf_op jit(solution)/shard_map/ppermute | solution.py:18
  211.3 3.6 %gather_fusion.2 = bf16[4,4,128,512]{3,2,1,0:T(8,128)(2,1)} fusion(bf16[4,4,128,512]{3,2,1,0:T(8,128)(2,1)} %maximum_bitcast_fusion.1, s32[1024]{0:T(1024)S(1)} %pad_clamp_fusion.1), kind=kCustom, calls=%fused_computation.1.clone | custom fusion | bytes 4194320 | tf_op jit(solution)/shard_map/jit(_take)/gather | solution.py:32
  214.9 3.2 broadcast_select_fusion
  218.1 4.8 %all-to-all-start.1 = ((bf16[16,128,512]{2,1,0:T(8,128)(2,1)}), bf16[16,128,512]{2,1,0:T(8,128)(2,1)}, u32[]{:S(2)}, u32[]{:S(2)}) async-start(bf16[16,128,512]{2,1,0:T(8,128)(2,1)} %bitcast.128), calls=%async_computation.2 | async-start | bytes 4194304 | tf_op jit(solution)/shard_map/all_to_all | solution.py:33
  225.8 3.1 collective-permute-start.10
  237.2 30.4 %collective-permute-done.11 = f32[2,2]{1,0:T(2,128)S(1)} collective-permute-done((f32[2,2]{1,0:T(2,128)S(1)}, f32[2,2]{1,0:T(2,128)S(1)}, u32[]{:S(2)}, u32[]{:S(2)}) %collective-permute-start.11) | collective-permute-done | bytes 48 | tf_op jit(solution)/shard_map/ppermute | solution.py:18
  267.6 3.3 collective-permute-start.15
  279.9 3.3 collective-permute-start.20
  283.3 5.3 %collective-permute-start.8 = (bf16[2048,512]{1,0:T(8,128)(2,1)}, bf16[2048,512]{1,0:T(8,128)(2,1)}, u32[]{:S(2)}, u32[]{:S(2)}) collective-permute-start(bf16[2048,512]{1,0:T(8,128)(2,1)} %bitcast.11), channel_id=1, source_target_pairs={{0,64},{64,0},{1,65},{65,1},{2,66},{66,2},{3,67},{67,3},{4,68},{68... | collective-permute-start | bytes 6291464 | tf_op jit(solution)/shard_map/ppermute | solution.py:9
  298.4 7.6 %multiply_convert_fusion = bf16[2,16,2,64,512]{4,3,2,1,0:T(8,128)(2,1)} fusion(bf16[1,16,2,64,512]{4,3,2,1,0:T(8,128)(2,1)S(1)} %bitcast.127, bf16[1,16,2,64,512]{4,3,2,1,0:T(8,128)(2,1)} %bitcast.4, bf16[1,16,2,64,512]{4,3,2,1,0:T(8,128)(2,1)} %bitcast.13, bf16[1,16,2,64,512]{4,3,2,1,0:T(8,128)(2,1)} %bitcast.12, f32[2,16,2]{2,1,0:T(8,128)S(1)} %copy.139, ...), kind=kLoop, calls=%fused_computation.3 | loop fusion | flops 20971520 | bytes 12583169 | tf_op jit(solution)/shard_map/convert_element_type | solution.py:98
  306.0 8.5 %all-gather.3.cloned.1.call-done = bf16[1,2,32,64,2048]{4,3,2,1,0:T(8,128)(2,1)} async-done(((bf16[1,2,2,64,2048]{4,3,2,1,0:T(8,128)(2,1)}), bf16[1,2,32,64,2048]{4,3,2,1,0:T(8,128)(2,1)}) %all-gather.3.cloned.1.call-update) | async-done | bytes 16777232 | tf_op jit(solution)/shard_map/all_gather | solution.py:56
  314.5 15.3 %fusion.2 = f32[1,2048,512]{1,2,0:T(8,128)} fusion(bf16[1,2048,512]{1,2,0:T(8,128)(2,1)} %copy.140, bf16[4096,512]{1,0:T(8,128)(2,1)} %bitcast.130, bf16[4096,2048]{1,0:T(8,128)(2,1)} %bitcast.141, f32[]{:T(128)S(6)} %mul_shard_map.3), kind=kOutput, calls=%fused_computation.10 | convolution fusion | flops 8594128896 | bytes 27262980 | tf_op jit(solution)/shard_map/dot_general | solution.py:101
  329.9 5.4 %copy.141 = f32[1,2048,512]{2,1,0:T(8,128)} copy(f32[1,2048,512]{1,2,0:T(8,128)} %fusion.2) | data formatting | bytes 8388608
  (116 shorter events, 68.4 us)
Async XLA Ops:
  10.1 16.4 %collective-permute-start = (bf16[2,64,2048]{2,1,0:T(8,128)(2,1)}, bf16[2,64,2048]{2,1,0:T(8,128)(2,1)S(1)}, u32[]{:S(2)}, u32[]{:S(2)}) collective-permute-start(bf16[2,64,2048]{2,1,0:T(8,128)(2,1)} %fusion.47), channel_id=1, source_target_pairs={{0,1},{1,2},{2,3},{3,0},{4,5},{5,6},{6,7},{7,4},{8,9},{9,10},{10,1... | collective-permute-start | bytes 1572872 | tf_op jit(solution)/shard_map/ppermute | solution.py:18
  12.5 26.1 %collective-permute-start.1 = (bf16[2,64,2048]{2,1,0:T(8,128)(2,1)}, bf16[2,64,2048]{2,1,0:T(8,128)(2,1)S(1)}, u32[]{:S(2)}, u32[]{:S(2)}) collective-permute-start(bf16[2,64,2048]{2,1,0:T(8,128)(2,1)} %fusion.47), channel_id=1, source_target_pairs={{0,2},{1,3},{2,0},{3,1},{4,6},{5,7},{6,4},{7,5},{8,10},{9,11},{10,... | collective-permute-start | bytes 1572872 | tf_op jit(solution)/shard_map/ppermute | solution.py:18
  15.8 24.1 %collective-permute-start.2 = (bf16[2,64,2048]{2,1,0:T(8,128)(2,1)}, bf16[2,64,2048]{2,1,0:T(8,128)(2,1)}, u32[]{:S(2)}, u32[]{:S(2)}) collective-permute-start(bf16[2,64,2048]{2,1,0:T(8,128)(2,1)} %fusion.47), channel_id=1, source_target_pairs={{0,3},{1,0},{2,1},{3,2},{4,7},{5,4},{6,5},{7,6},{8,11},{9,8},{10,9... | collective-permute-start | bytes 1572872 | tf_op jit(solution)/shard_map/ppermute | solution.py:18
  16.6 38.5 %collective-permute-start.4 = (bf16[2048,512]{1,0:T(8,128)(2,1)}, bf16[2048,512]{1,0:T(8,128)(2,1)}, u32[]{:S(2)}, u32[]{:S(2)}) collective-permute-start(bf16[2048,512]{1,0:T(8,128)(2,1)} %bitcast.142), channel_id=1, source_target_pairs={{0,64},{64,0},{1,65},{65,1},{2,66},{66,2},{3,67},{67,3},{4,68},{68... | collective-permute-start | bytes 6291464 | tf_op jit(solution)/shard_map/ppermute | solution.py:9
  48.2 34.8 %all-to-all-start = ((bf16[16,128,512]{2,1,0:T(8,128)(2,1)}), bf16[16,128,512]{2,1,0:T(8,128)(2,1)S(1)}, u32[]{:S(2)}, u32[]{:S(2)}) async-start(bf16[16,128,512]{2,1,0:T(8,128)(2,1)} %bitcast.129), calls=%async_computation | async-start | bytes 4194304 | tf_op jit(solution)/shard_map/all_to_all | solution.py:33
  55.0 123.0 %reduce-scatter.2.cloned.1.call-start = ((), (), s32[]{:S(2)}) async-start(), calls=%async_computation.3 | async-start | bytes 8912896 | tf_op jit(solution)/shard_map/reduce_scatter | solution.py:68
  91.4 92.9 %all-reduce.2.cloned.1.call-start = ((), (), s32[]{:S(2)}) async-start(), calls=%async_computation.4 | async-start | bytes 262144 | tf_op jit(solution)/shard_map/psum | solution.py:57
  94.2 220.4 %all-gather.3.cloned.1.call-start = ((), (), s32[]{:S(2)}) async-start(), calls=%async_computation.5 | async-start | bytes 17825792 | tf_op jit(solution)/shard_map/all_gather | solution.py:56
  179.3 14.3 %collective-permute-start.5 = (bf16[2,64,2048]{2,1,0:T(8,128)(2,1)S(1)}, bf16[2,64,2048]{2,1,0:T(8,128)(2,1)}, u32[]{:S(2)}, u32[]{:S(2)}) collective-permute-start(bf16[2,64,2048]{2,1,0:T(8,128)(2,1)S(1)} %bitcast.131), channel_id=1, source_target_pairs={{0,1},{1,2},{2,3},{3,0},{4,5},{5,6},{6,7},{7,4},{8,9},{9,10},{10,1... | collective-permute-start | bytes 1572872 | tf_op jit(solution)/shard_map/ppermute | solution.py:18
  180.6 23.9 %collective-permute-start.6 = (bf16[2,64,2048]{2,1,0:T(8,128)(2,1)S(1)}, bf16[2,64,2048]{2,1,0:T(8,128)(2,1)}, u32[]{:S(2)}, u32[]{:S(2)}) collective-permute-start(bf16[2,64,2048]{2,1,0:T(8,128)(2,1)S(1)} %bitcast.132), channel_id=1, source_target_pairs={{0,2},{1,3},{2,0},{3,1},{4,6},{5,7},{6,4},{7,5},{8,10},{9,11},{10,... | collective-permute-start | bytes 1572872 | tf_op jit(solution)/shard_map/ppermute | solution.py:18
  183.2 23.6 %collective-permute-start.7 = (bf16[2,64,2048]{2,1,0:T(8,128)(2,1)S(1)}, bf16[2,64,2048]{2,1,0:T(8,128)(2,1)}, u32[]{:S(2)}, u32[]{:S(2)}) collective-permute-start(bf16[2,64,2048]{2,1,0:T(8,128)(2,1)S(1)} %bitcast.133), channel_id=1, source_target_pairs={{0,3},{1,0},{2,1},{3,2},{4,7},{5,4},{6,5},{7,6},{8,11},{9,8},{10,9... | collective-permute-start | bytes 1572872 | tf_op jit(solution)/shard_map/ppermute | solution.py:18
  191.8 106.7 %collective-permute-start.3 = (bf16[2048,512]{1,0:T(8,128)(2,1)S(1)}, bf16[2048,512]{1,0:T(8,128)(2,1)}, u32[]{:S(2)}, u32[]{:S(2)}) collective-permute-start(bf16[2048,512]{1,0:T(8,128)(2,1)S(1)} %bitcast.126), channel_id=1, source_target_pairs={{0,64},{64,0},{1,65},{65,1},{2,66},{66,2},{3,67},{67,3},{4,68},{68... | collective-permute-start | bytes 6291464 | tf_op jit(solution)/shard_map/ppermute | solution.py:9
  218.1 65.2 %all-to-all-start.1 = ((bf16[16,128,512]{2,1,0:T(8,128)(2,1)}), bf16[16,128,512]{2,1,0:T(8,128)(2,1)}, u32[]{:S(2)}, u32[]{:S(2)}) async-start(bf16[16,128,512]{2,1,0:T(8,128)(2,1)} %bitcast.128), calls=%async_computation.2 | async-start | bytes 4194304 | tf_op jit(solution)/shard_map/all_to_all | solution.py:33
  229.8 37.8 %collective-permute-start.11 = (f32[2,2]{1,0:T(2,128)S(1)}, f32[2,2]{1,0:T(2,128)S(1)}, u32[]{:S(2)}, u32[]{:S(2)}) collective-permute-start(f32[2,2]{1,0:T(2,128)S(1)} %maximum_select_fusion.3), channel_id=1, source_target_pairs={{0,4},{4,8},{8,12},{12,16},{16,20},{20,24},{24,28},{28,32},{32,36}... | collective-permute-start | bytes 56 | tf_op jit(solution)/shard_map/ppermute | solution.py:18
  231.5 41.9 %collective-permute-start.12 = (f32[2,2]{1,0:T(2,128)S(1)}, f32[2,2]{1,0:T(2,128)S(1)}, u32[]{:S(2)}, u32[]{:S(2)}) collective-permute-start(f32[2,2]{1,0:T(2,128)S(1)} %maximum_select_fusion.3), channel_id=1, source_target_pairs={{0,8},{4,12},{8,16},{12,20},{16,24},{20,28},{24,32},{28,36},{32,40... | collective-permute-start | bytes 56 | tf_op jit(solution)/shard_map/ppermute | solution.py:18
  233.9 40.7 %collective-permute-start.13 = (f32[2,2]{1,0:T(2,128)S(1)}, f32[2,2]{1,0:T(2,128)S(1)}, u32[]{:S(2)}, u32[]{:S(2)}) collective-permute-start(f32[2,2]{1,0:T(2,128)S(1)} %maximum_select_fusion.3), channel_id=1, source_target_pairs={{0,12},{4,16},{8,20},{12,24},{16,28},{20,32},{24,36},{28,40},{32,4... | collective-permute-start | bytes 56 | tf_op jit(solution)/shard_map/ppermute | solution.py:18
  236.0 40.7 %collective-permute-start.14 = (f32[2,2]{1,0:T(2,128)S(1)}, f32[2,2]{1,0:T(2,128)S(1)}, u32[]{:S(2)}, u32[]{:S(2)}) collective-permute-start(f32[2,2]{1,0:T(2,128)S(1)} %maximum_select_fusion.3), channel_id=1, source_target_pairs={{0,16},{4,20},{8,24},{12,28},{16,32},{20,36},{24,40},{28,44},{32,4... | collective-permute-start | bytes 56 | tf_op jit(solution)/shard_map/ppermute | solution.py:18
  267.6 10.5 %collective-permute-start.15 = (f32[2,2]{1,0:T(2,128)S(1)}, f32[2,2]{1,0:T(2,128)S(1)}, u32[]{:S(2)}, u32[]{:S(2)}) collective-permute-start(f32[2,2]{1,0:T(2,128)S(1)} %maximum_select_fusion.3), channel_id=1, source_target_pairs={{0,20},{4,24},{8,28},{12,32},{16,36},{20,40},{24,44},{28,48},{32,5... | collective-permute-start | bytes 56 | tf_op jit(solution)/shard_map/ppermute | solution.py:18
  273.4 6.5 %collective-permute-start.16 = (f32[2,2]{1,0:T(2,128)S(1)}, f32[2,2]{1,0:T(2,128)S(1)}, u32[]{:S(2)}, u32[]{:S(2)}) collective-permute-start(f32[2,2]{1,0:T(2,128)S(1)} %maximum_select_fusion.3), channel_id=1, source_target_pairs={{0,24},{4,28},{8,32},{12,36},{16,40},{20,44},{24,48},{28,52},{32,5... | collective-permute-start | bytes 56 | tf_op jit(solution)/shard_map/ppermute | solution.py:18
  274.5 8.7 %collective-permute-start.17 = (f32[2,2]{1,0:T(2,128)S(1)}, f32[2,2]{1,0:T(2,128)S(1)}, u32[]{:S(2)}, u32[]{:S(2)}) collective-permute-start(f32[2,2]{1,0:T(2,128)S(1)} %maximum_select_fusion.3), channel_id=1, source_target_pairs={{0,28},{4,32},{8,36},{12,40},{16,44},{20,48},{24,52},{28,56},{32,6... | collective-permute-start | bytes 56 | tf_op jit(solution)/shard_map/ppermute | solution.py:18
  276.7 12.0 %collective-permute-start.18 = (f32[2,2]{1,0:T(2,128)S(1)}, f32[2,2]{1,0:T(2,128)S(1)}, u32[]{:S(2)}, u32[]{:S(2)}) collective-permute-start(f32[2,2]{1,0:T(2,128)S(1)} %maximum_select_fusion.3), channel_id=1, source_target_pairs={{0,32},{4,36},{8,40},{12,44},{16,48},{20,52},{24,56},{28,60},{32,0... | collective-permute-start | bytes 56 | tf_op jit(solution)/shard_map/ppermute | solution.py:18
  278.2 11.5 %collective-permute-start.19 = (f32[2,2]{1,0:T(2,128)S(1)}, f32[2,2]{1,0:T(2,128)S(1)}, u32[]{:S(2)}, u32[]{:S(2)}) collective-permute-start(f32[2,2]{1,0:T(2,128)S(1)} %maximum_select_fusion.3), channel_id=1, source_target_pairs={{0,36},{4,40},{8,44},{12,48},{16,52},{20,56},{24,60},{28,0},{32,4}... | collective-permute-start | bytes 56 | tf_op jit(solution)/shard_map/ppermute | solution.py:18
  279.9 11.3 %collective-permute-start.20 = (f32[2,2]{1,0:T(2,128)S(1)}, f32[2,2]{1,0:T(2,128)S(1)}, u32[]{:S(2)}, u32[]{:S(2)}) collective-permute-start(f32[2,2]{1,0:T(2,128)S(1)} %maximum_select_fusion.3), channel_id=1, source_target_pairs={{0,40},{4,44},{8,48},{12,52},{16,56},{20,60},{24,0},{28,4},{32,8},... | collective-permute-start | bytes 56 | tf_op jit(solution)/shard_map/ppermute | solution.py:18
  283.3 15.1 %collective-permute-start.8 = (bf16[2048,512]{1,0:T(8,128)(2,1)}, bf16[2048,512]{1,0:T(8,128)(2,1)}, u32[]{:S(2)}, u32[]{:S(2)}) collective-permute-start(bf16[2048,512]{1,0:T(8,128)(2,1)} %bitcast.11), channel_id=1, source_target_pairs={{0,64},{64,0},{1,65},{65,1},{2,66},{66,2},{3,67},{67,3},{4,68},{68... | collective-permute-start | bytes 6291464 | tf_op jit(solution)/shard_map/ppermute | solution.py:9
  (14 other events, 143.8 us)
Sparse Core Ops, SparseCore 0:
  91.6 86.3 reduce-scatter.1
  180.1 134.3 all-gather.2
Sparse Core Ops, SparseCore 1:
  94.3 41.5 all-reduce.1

commit v4 on v3

--- a/solution.py
+++ b/solution.py
@@ -21,17 +21,22 @@
     return stacked, (position - jnp.arange(count)) % count
 
 
-def column_blocks(values, group_count, column_part):
-    example_count, length_count, width_part = values.shape
-    token_count = example_count * length_count
+def feature_pieces(values):
     stacked, order = ring_pieces(values, "tensor")
     grams = jnp.einsum("jeld,jekd->elk", stacked, stacked, preferred_element_type=jnp.float32)
-    pieces = stacked.shape[0]
+    return stacked, order, grams
+
+
+def column_blocks(stacked, order, group_count, column_part, row_scales=None):
+    pieces, example_count, length_count, width_part = stacked.shape
+    token_count = example_count * length_count
+    if row_scales is not None:
+        stacked = (stacked.astype(jnp.float32) * row_scales[None, :, None, None]).astype(jnp.bfloat16)
     per_piece = width_part // column_part
     chunks = stacked.reshape(pieces, token_count, per_piece, column_part).transpose(0, 2, 1, 3)
     chunks = jnp.take(chunks, order, axis=0).reshape(pieces * per_piece, token_count, column_part)
     moved = lax.all_to_all(chunks, "dp", split_axis=0, concat_axis=1, tiled=True)
-    return grams, moved.reshape(group_count * token_count, column_part)
+    return moved.reshape(group_count * token_count, column_part)
 
 
 def token_grams(values):
@@ -58,7 +63,8 @@
     other_input_grams = swapped(input_grams, "pipe")
 
     own_cotangent = lax.dynamic_index_in_dim(cotangent, section_index, 0, keepdims=False)
-    last_grams, last_blocks = column_blocks(own_cotangent, group_count, column_part)
+    last_pieces, last_order, last_grams = feature_pieces(own_cotangent)
+    last_blocks = column_blocks(last_pieces, last_order, group_count, column_part)
     last_blocks_other = swapped(last_blocks, "pipe")
 
     last_weights = jnp.where(is_last, weight_block, swapped(weight_block, "pipe"))
@@ -69,8 +75,7 @@
     renewed = (own_cotangent.reshape(token_count, width_part).astype(jnp.float32) + summed).astype(
         jnp.bfloat16
     ).reshape(example_count, length_count, width_part)
-    first_grams, first_blocks = column_blocks(renewed, group_count, column_part)
-    first_blocks_other = swapped(first_blocks, "pipe")
+    first_pieces, first_order, first_grams = feature_pieces(renewed)
 
     own_input_grams = lax.dynamic_index_in_dim(input_grams, section_index, 0, keepdims=False)
     held_input_grams = lax.dynamic_index_in_dim(other_input_grams, section_index, 0, keepdims=False)
@@ -82,19 +87,22 @@
     bound = clip_norm[0]
     own_scales = bound / jnp.maximum(jnp.sqrt(norm_square), bound)
     scale_terms = by_micro(is_last, own_scales, swapped(own_scales, "pipe"))
-    scale_pieces, scale_order = ring_pieces(scale_terms, "dp")
-    all_scales = jnp.take(scale_pieces, scale_order, axis=0).transpose(1, 0, 2)
+    all_scales = lax.all_gather(scale_terms, "dp", axis=1, tiled=True)
+
+    first_blocks = column_blocks(first_pieces, first_order, group_count, column_part, own_scales)
+    first_blocks_other = swapped(first_blocks, "pipe")
 
     grad_blocks = jnp.where(
         is_last,
         by_micro(is_last, last_blocks, last_blocks_other),
         by_micro(is_last, first_blocks, first_blocks_other),
     )
+    row_scales = jnp.where(is_last, all_scales, jnp.ones_like(all_scales))
     scaled_blocks = (
         grad_blocks.reshape(micro_count, group_count, example_count, length_count, column_part).astype(
             jnp.float32
         )
-        * all_scales[:, :, :, None, None]
+        * row_scales.reshape(micro_count, group_count, example_count)[:, :, :, None, None]
     ).astype(jnp.bfloat16)
     flat_inputs = gathered_inputs.reshape(micro_count * group_count * token_count, width_part)
     flat_grads = scaled_blocks.reshape(micro_count * group_count * token_count, column_part)

time: 344 us -> 351 us (1.020)
  starting transfers between devices: 65.4 us -> 33.4 us
  blocking collectives: 0 us -> 18.9 us
  waiting for transfers between devices: 177 us -> 189 us
  local copies, waits for them, and re-layouts: 31.4 us -> 37.6 us
    all_to_all x2, waiting for transfers between devices: 28 us -> 75.8 us  [column_blocks(): lax.all_to_all(chunks, 'dp', split_axis=0, concat_axis=1, tiled=True)]
    ppermute x21 -> x6, waiting for transfers between devices: 60.3 us -> 29.1 us  [ring_pieces(): lax.ppermute(values, axis, [(source, (source + offset) % count) for sourc...]
    ppermute x21 -> x6, starting transfers between devices: 40.1 us -> 11.5 us  [ring_pieces(): lax.ppermute(values, axis, [(source, (source + offset) % count) for sourc...]
    all_gather x0 -> x1, blocking collectives: none -> 18.9 us  [local(): all_scales = lax.all_gather(scale_terms, 'dp', axis=1, tiled=True)]
    all_gather x1, waiting for transfers between devices: 8.5 us -> 0.01 us  [local(): gathered_inputs = lax.all_gather(local_inputs, 'dp', axis=1, tiled=True)]
    another operation x17 -> x16, local copies, waits for them, and re-layouts: 12.8 us -> 18.6 us  [ring_pieces(): stacked = jnp.stack(pieces)]
    reduce_scatter x1, waiting for transfers between devices: 77.6 us -> 82.1 us  [local(): lax.psum_scatter(terms, 'dp', scatter_dimension=0, tiled=True)]
    unnamed x31 -> x16, local copies, waits for them, and re-layouts: 10.8 us -> 10.8 us
  transfers between devices with their start and end apart: 31 -> 16, of which waited for: 12 -> 9; matrix products, arithmetic and copies ran while one was open for 15% -> 17% of each run, Pallas kernels for 0% -> 0%
where the time goes in v4:
time: 351 us; the launch traced here: 349 us
  waiting for transfers between devices  189 us (54%)
  local copies, waits for them, and re-layouts  37.6 us (11%)
  starting transfers between devices  33.4 us (10%)
  matrix products  32.2 us (9%)
  other arithmetic  20.7 us (6%)
  blocking collectives  18.9 us (5%)
  between operations  16.3 us (5%)
    reduce_scatter x1, waiting for transfers between devices, local(): lax.psum_scatter(terms, 'dp', scatter_dimension=0, tiled=True)  82.1 us
    all_to_all x2, waiting for transfers between devices, column_blocks(): lax.all_to_all(chunks, 'dp', split_axis=0, concat_axis=1, tiled=True)  75.8 us
    ppermute x6, waiting for transfers between devices, ring_pieces(): lax.ppermute(values, axis, [(source, (source + offset) % count) for sourc...  29.1 us
    all_gather x1, blocking collectives, local(): all_scales = lax.all_gather(scale_terms, 'dp', axis=1, tiled=True)  18.9 us
    another operation x16, local copies, waits for them, and re-layouts, ring_pieces(): stacked = jnp.stack(pieces)  18.6 us
    dot_general x1, matrix products, local(): lax.dot_general(flat_inputs, flat_grads, (((0,), (0,)), ((), ())), prefer...  15.3 us
    ppermute x6, starting transfers between devices, ring_pieces(): lax.ppermute(values, axis, [(source, (source + offset) % count) for sourc...  11.5 us
    all_to_all x2, starting transfers between devices, column_blocks(): lax.all_to_all(chunks, 'dp', split_axis=0, concat_axis=1, tiled=True)  11.2 us
  transfers between devices with their start and end apart: 16, of which 9 were waited for; matrix products, arithmetic and copies ran while one was open for 17% of the time, Pallas kernels for 0%

profile of v4, /device:TPU:1, one launch (start us, length us, event | category | flops | bytes accessed | tf_op | source)
XLA Modules:
  0.0 348.6 jit_solution(11068486064683663800)
XLA Ops:
  12.5 3.3 collective-permute-start.1
  19.5 7.0 %collective-permute-done = bf16[2,64,2048]{2,1,0:T(8,128)(2,1)S(1)} collective-permute-done((bf16[2,64,2048]{2,1,0:T(8,128)(2,1)}, bf16[2,64,2048]{2,1,0:T(8,128)(2,1)S(1)}, u32[]{:S(2)}, u32[]{:S(2)}) %collective-permute-start) | collective-permute-done | bytes 524320 | tf_op jit(solution)/shard_map/ppermute | solution.py:18
  27.8 10.9 %collective-permute-done.1 = bf16[2,64,2048]{2,1,0:T(8,128)(2,1)S(1)} collective-permute-done((bf16[2,64,2048]{2,1,0:T(8,128)(2,1)}, bf16[2,64,2048]{2,1,0:T(8,128)(2,1)S(1)}, u32[]{:S(2)}, u32[]{:S(2)}) %collective-permute-start.1) | collective-permute-done | bytes 524320 | tf_op jit(solution)/shard_map/ppermute | solution.py:18
  45.1 3.2 broadcast_select_fusion.1
  48.2 6.8 %all-to-all-start = ((bf16[16,128,512]{2,1,0:T(8,128)(2,1)}), bf16[16,128,512]{2,1,0:T(8,128)(2,1)S(1)}, u32[]{:S(2)}, u32[]{:S(2)}) async-start(bf16[16,128,512]{2,1,0:T(8,128)(2,1)} %bitcast.97), calls=%async_computation | async-start | bytes 4194304 | tf_op jit(solution)/shard_map/all_to_all | solution.py:38
  55.1 28.0 %all-to-all-done = bf16[16,128,512]{2,1,0:T(8,128)(2,1)S(1)} async-done(((bf16[16,128,512]{2,1,0:T(8,128)(2,1)}), bf16[16,128,512]{2,1,0:T(8,128)(2,1)S(1)}, u32[]{:S(2)}, u32[]{:S(2)}) %all-to-all-start) | async-done | bytes 2097184 | tf_op jit(solution)/shard_map/all_to_all | solution.py:38
  83.0 8.4 %convolution_convert_fusion = bf16[2048,2048]{1,0:T(8,128)(2,1)} fusion(bf16[2048,512]{1,0:T(8,128)(2,1)S(1)} %bitcast.94, bf16[2048,512]{1,0:T(8,128)(2,1)} %collective-permute-done.4, pred[]{:T(512)S(6)} %eq.6, bf16[1,2048,512]{2,1,0:T(8,128)(2,1)} %param.7), kind=kOutput, calls=%fused_computation.3 | convolution fusion | flops 4300210176 | bytes 14680065 | tf_op jit(solution)/shard_map/dot_general | solution.py:71
  95.7 82.1 %reduce-scatter.2.cloned.1.call-done = bf16[128,2048]{1,0:T(8,128)(2,1)} async-done(((bf16[2048,2048]{1,0:T(8,128)(2,1)}), bf16[128,2048]{1,0:T(8,128)(2,1)}) %reduce-scatter.2.cloned.1.call-update) | async-done | bytes 524304 | tf_op jit(solution)/shard_map/reduce_scatter | solution.py:74
  184.1 3.0 collective-permute-start.8
  188.3 3.1 fusion.31
  193.8 10.4 %collective-permute-done.6 = bf16[2,64,2048]{2,1,0:T(8,128)(2,1)} collective-permute-done((bf16[2,64,2048]{2,1,0:T(8,128)(2,1)S(1)}, bf16[2,64,2048]{2,1,0:T(8,128)(2,1)}, u32[]{:S(2)}, u32[]{:S(2)}) %collective-permute-start.6) | collective-permute-done | bytes 524320 | tf_op jit(solution)/shard_map/ppermute | solution.py:18
  205.1 2.7 fusion.32
  218.9 3.0 fusion.3
  221.9 4.2 %gather_fusion.1 = bf16[4,4,128,512]{3,2,1,0:T(8,128)(2,1)} fusion(bf16[4,4,128,512]{3,2,1,0:T(8,128)(2,1)} %fusion.3, s32[1024]{0:T(1024)S(1)} %pad_clamp_fusion), kind=kCustom, calls=%fused_computation.1.clone | custom fusion | bytes 4194320 | tf_op jit(solution)/shard_map/jit(_take)/gather | solution.py:37
  226.1 3.2 broadcast_select_fusion
  229.3 4.5 %all-to-all-start.1 = ((bf16[16,128,512]{2,1,0:T(8,128)(2,1)}), bf16[16,128,512]{2,1,0:T(8,128)(2,1)}, u32[]{:S(2)}, u32[]{:S(2)}) async-start(bf16[16,128,512]{2,1,0:T(8,128)(2,1)} %bitcast.98), calls=%async_computation.2 | async-start | bytes 4194304 | tf_op jit(solution)/shard_map/all_to_all | solution.py:38
  233.8 2.7 collective-permute-start.3
  236.4 47.8 %all-to-all-done.1 = bf16[16,128,512]{2,1,0:T(8,128)(2,1)} async-done(((bf16[16,128,512]{2,1,0:T(8,128)(2,1)}), bf16[16,128,512]{2,1,0:T(8,128)(2,1)}, u32[]{:S(2)}, u32[]{:S(2)}) %all-to-all-start.1) | async-done | bytes 2097184 | tf_op jit(solution)/shard_map/all_to_all | solution.py:38
  284.3 3.4 collective-permute-start.9
  287.6 4.0 %copy.78 = bf16[1,2048,512]{1,2,0:T(8,128)(2,1)} copy(bf16[1,2048,512]{2,1,0:T(8,128)(2,1)} %param.11) | data formatting | bytes 4194304 | tf_op args[4]
  292.9 18.9 %all-gather.1 = f32[16,2,2]{2,1,0:T(2,128)S(1)} all-gather(f32[1,2,2]{2,1,0:T(2,128)S(1)} %bitcast.110), channel_id=1, replica_groups=mesh['pipe'=2,'dp'=16,'tensor'=4] {'dp'}, dimensions={0}, use_global_device_ids=true | all-gather | bytes 272 | tf_op jit(solution)/shard_map/all_gather | solution.py:90
  312.6 7.8 %multiply_convert_fusion = bf16[2,16,2,64,512]{4,3,2,1,0:T(8,128)(2,1)} fusion(bf16[1,16,2,64,512]{4,3,2,1,0:T(8,128)(2,1)S(1)} %bitcast.96, bf16[1,16,2,64,512]{4,3,2,1,0:T(8,128)(2,1)} %bitcast.4, bf16[1,16,2,64,512]{4,3,2,1,0:T(8,128)(2,1)} %bitcast.33, bf16[1,16,2,64,512]{4,3,2,1,0:T(8,128)(2,1)} %bitcast.32, f32[2,16,2]{2,1,0:T(8,128)S(1)} %mul.52, ...), kind=kLoop, calls=%fused_computation.2 | loop fusion | flops 20971520 | bytes 12583169 | tf_op jit(solution)/shard_map/convert_element_type | solution.py:106
  320.3 15.3 %fusion.2 = f32[1,2048,512]{1,2,0:T(8,128)} fusion(bf16[1,2048,512]{1,2,0:T(8,128)(2,1)} %copy.78, bf16[4096,512]{1,0:T(8,128)(2,1)} %bitcast.99, bf16[4096,2048]{1,0:T(8,128)(2,1)} %bitcast.113, f32[]{:T(128)S(6)} %mul_shard_map.3), kind=kOutput, calls=%fused_computation.9 | convolution fusion | flops 8594128896 | bytes 27262980 | tf_op jit(solution)/shard_map/dot_general | solution.py:109
  335.7 5.4 %copy.79 = f32[1,2048,512]{2,1,0:T(8,128)} copy(f32[1,2048,512]{1,2,0:T(8,128)} %fusion.2) | data formatting | bytes 8388608
  (70 shorter events, 43.3 us)
Async XLA Ops:
  8.0 1.2 copy-start
  10.1 16.4 %collective-permute-start = (bf16[2,64,2048]{2,1,0:T(8,128)(2,1)}, bf16[2,64,2048]{2,1,0:T(8,128)(2,1)S(1)}, u32[]{:S(2)}, u32[]{:S(2)}) collective-permute-start(bf16[2,64,2048]{2,1,0:T(8,128)(2,1)} %fusion.46), channel_id=1, source_target_pairs={{0,1},{1,2},{2,3},{3,0},{4,5},{5,6},{6,7},{7,4},{8,9},{9,10},{10,1... | collective-permute-start | bytes 1572872 | tf_op jit(solution)/shard_map/ppermute | solution.py:18
  12.5 26.1 %collective-permute-start.1 = (bf16[2,64,2048]{2,1,0:T(8,128)(2,1)}, bf16[2,64,2048]{2,1,0:T(8,128)(2,1)S(1)}, u32[]{:S(2)}, u32[]{:S(2)}) collective-permute-start(bf16[2,64,2048]{2,1,0:T(8,128)(2,1)} %fusion.46), channel_id=1, source_target_pairs={{0,2},{1,3},{2,0},{3,1},{4,6},{5,7},{6,4},{7,5},{8,10},{9,11},{10,... | collective-permute-start | bytes 1572872 | tf_op jit(solution)/shard_map/ppermute | solution.py:18
  15.8 24.1 %collective-permute-start.2 = (bf16[2,64,2048]{2,1,0:T(8,128)(2,1)}, bf16[2,64,2048]{2,1,0:T(8,128)(2,1)}, u32[]{:S(2)}, u32[]{:S(2)}) collective-permute-start(bf16[2,64,2048]{2,1,0:T(8,128)(2,1)} %fusion.46), channel_id=1, source_target_pairs={{0,3},{1,0},{2,1},{3,2},{4,7},{5,4},{6,5},{7,6},{8,11},{9,8},{10,9... | collective-permute-start | bytes 1572872 | tf_op jit(solution)/shard_map/ppermute | solution.py:18
  16.6 38.5 %collective-permute-start.4 = (bf16[2048,512]{1,0:T(8,128)(2,1)}, bf16[2048,512]{1,0:T(8,128)(2,1)}, u32[]{:S(2)}, u32[]{:S(2)}) collective-permute-start(bf16[2048,512]{1,0:T(8,128)(2,1)} %bitcast.114), channel_id=1, source_target_pairs={{0,64},{64,0},{1,65},{65,1},{2,66},{66,2},{3,67},{67,3},{4,68},{68... | collective-permute-start | bytes 6291464 | tf_op jit(solution)/shard_map/ppermute | solution.py:9
  18.1 9.6 %copy-start.2 = (bf16[1,2,64,2048]{3,2,0,1:T(8,128)(2,1)}, bf16[1,2,64,2048]{3,2,0,1:T(8,128)(2,1)S(1)}, u32[]{:S(2)}) copy-start(bf16[1,2,64,2048]{3,2,0,1:T(8,128)(2,1)S(1)} %fusion.45) | copy-start | bytes 1572868
  26.5 13.4 %copy-start.3 = (bf16[2,64,2048]{2,1,0:T(8,128)(2,1)}, bf16[2,64,2048]{2,1,0:T(8,128)(2,1)S(1)}, u32[]{:S(2)}) copy-start(bf16[2,64,2048]{2,1,0:T(8,128)(2,1)S(1)} %collective-permute-done) | copy-start | bytes 1572868
  38.6 2.7 copy-start.4
  48.2 34.8 %all-to-all-start = ((bf16[16,128,512]{2,1,0:T(8,128)(2,1)}), bf16[16,128,512]{2,1,0:T(8,128)(2,1)S(1)}, u32[]{:S(2)}, u32[]{:S(2)}) async-start(bf16[16,128,512]{2,1,0:T(8,128)(2,1)} %bitcast.97), calls=%async_computation | async-start | bytes 4194304 | tf_op jit(solution)/shard_map/all_to_all | solution.py:38
  55.0 122.8 %reduce-scatter.2.cloned.1.call-start = ((), (), s32[]{:S(2)}) async-start(), calls=%async_computation.3 | async-start | bytes 8912896 | tf_op jit(solution)/shard_map/reduce_scatter | solution.py:74
  91.4 92.7 %all-reduce.2.cloned.1.call-start = ((), (), s32[]{:S(2)}) async-start(), calls=%async_computation.4 | async-start | bytes 262144 | tf_op jit(solution)/shard_map/psum | solution.py:62
  94.1 226.2 %all-gather.4.cloned.1.call-start = ((), (), s32[]{:S(2)}) async-start(), calls=%async_computation.5 | async-start | bytes 17825792 | tf_op jit(solution)/shard_map/all_gather | solution.py:61
  179.1 14.7 %collective-permute-start.5 = (bf16[2,64,2048]{2,1,0:T(8,128)(2,1)S(1)}, bf16[2,64,2048]{2,1,0:T(8,128)(2,1)}, u32[]{:S(2)}, u32[]{:S(2)}) collective-permute-start(bf16[2,64,2048]{2,1,0:T(8,128)(2,1)S(1)} %bitcast.100), channel_id=1, source_target_pairs={{0,1},{1,2},{2,3},{3,0},{4,5},{5,6},{6,7},{7,4},{8,9},{9,10},{10,1... | collective-permute-start | bytes 1572872 | tf_op jit(solution)/shard_map/ppermute | solution.py:18
  180.5 23.8 %collective-permute-start.6 = (bf16[2,64,2048]{2,1,0:T(8,128)(2,1)S(1)}, bf16[2,64,2048]{2,1,0:T(8,128)(2,1)}, u32[]{:S(2)}, u32[]{:S(2)}) collective-permute-start(bf16[2,64,2048]{2,1,0:T(8,128)(2,1)S(1)} %bitcast.101), channel_id=1, source_target_pairs={{0,2},{1,3},{2,0},{3,1},{4,6},{5,7},{6,4},{7,5},{8,10},{9,11},{10,... | collective-permute-start | bytes 1572872 | tf_op jit(solution)/shard_map/ppermute | solution.py:18
  183.0 22.1 %collective-permute-start.7 = (bf16[2,64,2048]{2,1,0:T(8,128)(2,1)S(1)}, bf16[2,64,2048]{2,1,0:T(8,128)(2,1)}, u32[]{:S(2)}, u32[]{:S(2)}) collective-permute-start(bf16[2,64,2048]{2,1,0:T(8,128)(2,1)S(1)} %bitcast.102), channel_id=1, source_target_pairs={{0,3},{1,0},{2,1},{3,2},{4,7},{5,4},{6,5},{7,6},{8,11},{9,8},{10,9... | collective-permute-start | bytes 1572872 | tf_op jit(solution)/shard_map/ppermute | solution.py:18
  184.1 4.2 %collective-permute-start.8 = (f32[2,2,64,64]{3,2,1,0:T(8,128)}, f32[2,2,64,64]{3,2,1,0:T(8,128)S(1)}, u32[]{:S(2)}, u32[]{:S(2)}) collective-permute-start(f32[2,2,64,64]{3,2,1,0:T(8,128)} %all-reduce.2.cloned.1.call-done), channel_id=1, source_target_pairs={{0,64},{64,0},{1,65},{65,1},{2,66},{66,2},{3,67},{67,3},{4,68},{68... | collective-permute-start | bytes 196616 | tf_op jit(solution)/shard_map/ppermute | solution.py:9
  191.4 13.7 %copy-start.5 = (f32[2,2,64,64]{3,2,1,0:T(8,128)S(1)}, f32[2,2,64,64]{3,2,1,0:T(8,128)}, u32[]{:S(2)}) copy-start(f32[2,2,64,64]{3,2,1,0:T(8,128)} %all-reduce.2.cloned.1.call-done) | copy-start | bytes 196612
  229.3 55.0 %all-to-all-start.1 = ((bf16[16,128,512]{2,1,0:T(8,128)(2,1)}), bf16[16,128,512]{2,1,0:T(8,128)(2,1)}, u32[]{:S(2)}, u32[]{:S(2)}) async-start(bf16[16,128,512]{2,1,0:T(8,128)(2,1)} %bitcast.98), calls=%async_computation.2 | async-start | bytes 4194304 | tf_op jit(solution)/shard_map/all_to_all | solution.py:38
  233.8 78.8 %collective-permute-start.3 = (bf16[2048,512]{1,0:T(8,128)(2,1)S(1)}, bf16[2048,512]{1,0:T(8,128)(2,1)}, u32[]{:S(2)}, u32[]{:S(2)}) collective-permute-start(bf16[2048,512]{1,0:T(8,128)(2,1)S(1)} %bitcast.95), channel_id=1, source_target_pairs={{0,64},{64,0},{1,65},{65,1},{2,66},{66,2},{3,67},{67,3},{4,68},{68... | collective-permute-start | bytes 6291464 | tf_op jit(solution)/shard_map/ppermute | solution.py:9
  284.3 28.3 %collective-permute-start.9 = (bf16[2048,512]{1,0:T(8,128)(2,1)}, bf16[2048,512]{1,0:T(8,128)(2,1)}, u32[]{:S(2)}, u32[]{:S(2)}) collective-permute-start(bf16[2048,512]{1,0:T(8,128)(2,1)} %bitcast.31), channel_id=1, source_target_pairs={{0,64},{64,0},{1,65},{65,1},{2,66},{66,2},{3,67},{67,3},{4,68},{68... | collective-permute-start | bytes 6291464 | tf_op jit(solution)/shard_map/ppermute | solution.py:9
  291.6 1.2 collective-permute-start.10
  335.7 5.4 %copy-start.1 = (bf16[2,2,64,2048]{3,2,1,0:T(8,128)(2,1)S(1)}, bf16[2,2,64,2048]{3,2,1,0:T(8,128)(2,1)}, u32[]{:S(2)}) copy-start(bf16[2,2,64,2048]{3,2,1,0:T(8,128)(2,1)} %param.9) | copy-start | bytes 3145732
Sparse Core Ops, SparseCore 0:
  91.5 86.2 reduce-scatter.1
  179.9 134.2 all-gather.3
Sparse Core Ops, SparseCore 1:
  94.2 41.5 all-reduce.1

commit v5 on v4

--- a/solution.py
+++ b/solution.py
@@ -58,7 +58,9 @@
     full_width = column_part * group_count
     is_last = section_index == 1
 
-    gathered_inputs = lax.all_gather(local_inputs, "dp", axis=1, tiled=True)
+    gathered_inputs = jnp.concatenate(
+        [lax.all_gather(local_inputs[m : m + 1], "dp", axis=1, tiled=True) for m in range(micro_count)], axis=0
+    )
     input_grams = lax.psum(token_grams(local_inputs), "tensor")
     other_input_grams = swapped(input_grams, "pipe")
 
@@ -71,7 +73,10 @@
     terms = lax.dot_general(
         last_blocks, last_weights, (((1,), (1,)), ((), ())), preferred_element_type=jnp.float32
     ).astype(jnp.bfloat16)
-    summed = lax.psum_scatter(terms, "dp", scatter_dimension=0, tiled=True).astype(jnp.float32)
+    halves = jnp.split(terms, 2, axis=1)
+    summed = jnp.concatenate(
+        [lax.psum_scatter(half, "dp", scatter_dimension=0, tiled=True) for half in halves], axis=1
+    ).astype(jnp.float32)
     renewed = (own_cotangent.reshape(token_count, width_part).astype(jnp.float32) + summed).astype(
         jnp.bfloat16
     ).reshape(example_count, length_count, width_part)

time: 351 us -> 450 us (1.28)
  waiting for transfers between devices: 189 us -> 295 us
  other arithmetic: 20.7 us -> 31.2 us
  matrix products: 32.2 us -> 23.7 us
    reduce_scatter x1 -> x2, waiting for transfers between devices: 82.1 us -> 151 us  [local(): lax.psum_scatter(half, 'dp', scatter_dimension=0, tiled=True)]
    all_gather x1 -> x2, waiting for transfers between devices: 0.01 us -> 38.2 us  [local(): lax.all_gather(local_inputs[m:m + 1], 'dp', axis=1, tiled=True)]
    concatenate x0 -> x1, other arithmetic: none -> 9.33 us  [local(): jnp.concatenate([lax.all_gather(local_inputs[m:m + 1], 'dp', axis=1, tile...]
    all_to_all x2, waiting for transfers between devices: 75.8 us -> 67.3 us  [column_blocks(): lax.all_to_all(chunks, 'dp', split_axis=0, concat_axis=1, tiled=True)]
    unnamed x16 -> x24, local copies, waits for them, and re-layouts: 10.8 us -> 2.5 us
    dot_general x1, matrix products: 15.3 us -> 10.4 us  [local(): lax.dot_general(flat_inputs, flat_grads, (((0,), (0,)), ((), ())), prefer...]
  transfers between devices with their start and end apart: 16 -> 18, of which waited for: 9 -> 11; matrix products, arithmetic and copies ran while one was open for 17% -> 15% of each run, Pallas kernels for 0% -> 0%
where the time goes in v5:
time: 450 us; the launch traced here: 449 us
  waiting for transfers between devices  295 us (66%)
  local copies, waits for them, and re-layouts  33.6 us (7%)
  other arithmetic  31.2 us (7%)
  starting transfers between devices  31.1 us (7%)
  matrix products  23.7 us (5%)
  blocking collectives  17.2 us (4%)
  between operations  16.6 us (4%)
    reduce_scatter x2, waiting for transfers between devices, local(): lax.psum_scatter(half, 'dp', scatter_dimension=0, tiled=True)  151 us
    all_to_all x2, waiting for transfers between devices, column_blocks(): lax.all_to_all(chunks, 'dp', split_axis=0, concat_axis=1, tiled=True)  67.3 us
    all_gather x2, waiting for transfers between devices, local(): lax.all_gather(local_inputs[m:m + 1], 'dp', axis=1, tiled=True)  38.2 us
    ppermute x6, waiting for transfers between devices, ring_pieces(): lax.ppermute(values, axis, [(source, (source + offset) % count) for sourc...  31.4 us
    another operation x16, local copies, waits for them, and re-layouts, ring_pieces(): stacked = jnp.stack(pieces)  18.4 us
    all_gather x1, blocking collectives, local(): all_scales = lax.all_gather(scale_terms, 'dp', axis=1, tiled=True)  17.2 us
    ppermute x6, starting transfers between devices, ring_pieces(): lax.ppermute(values, axis, [(source, (source + offset) % count) for sourc...  11.4 us
    all_to_all x2, starting transfers between devices, column_blocks(): lax.all_to_all(chunks, 'dp', split_axis=0, concat_axis=1, tiled=True)  11.3 us
  transfers between devices with their start and end apart: 18, of which 11 were waited for; matrix products, arithmetic and copies ran while one was open for 15% of the time, Pallas kernels for 0%

profile of v5, /device:TPU:1, one launch (start us, length us, event | category | flops | bytes accessed | tf_op | source)
XLA Modules:
  0.0 448.5 jit_solution(7313620353953771594)
XLA Ops:
  12.3 3.3 collective-permute-start.1
  19.5 6.8 %collective-permute-done = bf16[2,64,2048]{2,1,0:T(8,128)(2,1)S(1)} collective-permute-done((bf16[2,64,2048]{2,1,0:T(8,128)(2,1)}, bf16[2,64,2048]{2,1,0:T(8,128)(2,1)S(1)}, u32[]{:S(2)}, u32[]{:S(2)}) %collective-permute-start) | collective-permute-done | bytes 524320 | tf_op jit(solution)/shard_map/ppermute | solution.py:18
  26.8 11.6 %collective-permute-done.1 = bf16[2,64,2048]{2,1,0:T(8,128)(2,1)S(1)} collective-permute-done((bf16[2,64,2048]{2,1,0:T(8,128)(2,1)}, bf16[2,64,2048]{2,1,0:T(8,128)(2,1)S(1)}, u32[]{:S(2)}, u32[]{:S(2)}) %collective-permute-start.1) | collective-permute-done | bytes 524320 | tf_op jit(solution)/shard_map/ppermute | solution.py:18
  44.6 3.2 broadcast_select_fusion.1
  47.7 6.9 %all-to-all-start = ((bf16[16,128,512]{2,1,0:T(8,128)(2,1)}), bf16[16,128,512]{2,1,0:T(8,128)(2,1)S(1)}, u32[]{:S(2)}, u32[]{:S(2)}) async-start(bf16[16,128,512]{2,1,0:T(8,128)(2,1)} %bitcast.92), calls=%async_computation | async-start | bytes 4194304 | tf_op jit(solution)/shard_map/all_to_all | solution.py:38
  55.9 26.8 %all-to-all-done = bf16[16,128,512]{2,1,0:T(8,128)(2,1)S(1)} async-done(((bf16[16,128,512]{2,1,0:T(8,128)(2,1)}), bf16[16,128,512]{2,1,0:T(8,128)(2,1)S(1)}, u32[]{:S(2)}, u32[]{:S(2)}) %all-to-all-start) | async-done | bytes 2097184 | tf_op jit(solution)/shard_map/all_to_all | solution.py:38
  82.7 6.4 %convolution_convert_fusion = bf16[2048,2048]{1,0:T(8,128)(2,1)S(1)} fusion(bf16[2048,512]{1,0:T(8,128)(2,1)S(1)} %bitcast.89, bf16[2048,512]{1,0:T(8,128)(2,1)} %collective-permute-done.4, pred[]{:T(512)S(6)} %eq.6, bf16[1,2048,512]{2,1,0:T(8,128)(2,1)} %param.7), kind=kOutput, calls=%fused_computation.4 | convolution fusion | flops 4300210176 | bytes 14680065 | tf_op jit(solution)/shard_map/dot_general | solution.py:73
  89.1 3.8 fusion.40
  98.2 2.9 collective-permute-start.8
  101.1 70.5 %reduce-scatter.3.cloned.1.call-done = bf16[128,1024]{1,0:T(8,128)(2,1)} async-done(((bf16[2048,1024]{1,0:T(8,128)(2,1)}), bf16[128,1024]{1,0:T(8,128)(2,1)}) %reduce-scatter.3.cloned.1.call-update) | async-done | bytes 262160 | tf_op jit(solution)/shard_map/reduce_scatter | solution.py:78
  171.6 80.9 %reduce-scatter.5.cloned.1.call-done = bf16[128,1024]{1,0:T(8,128)(2,1)} async-done(((bf16[2048,1024]{1,0:T(8,128)(2,1)}), bf16[128,1024]{1,0:T(8,128)(2,1)}) %reduce-scatter.5.cloned.1.call-update) | async-done | bytes 262160 | tf_op jit(solution)/shard_map/reduce_scatter | solution.py:78
  260.1 3.1 fusion.30
  267.7 11.8 %collective-permute-done.6 = bf16[2,64,2048]{2,1,0:T(8,128)(2,1)} collective-permute-done((bf16[2,64,2048]{2,1,0:T(8,128)(2,1)}, bf16[2,64,2048]{2,1,0:T(8,128)(2,1)}, u32[]{:S(2)}, u32[]{:S(2)}) %collective-permute-start.6) | collective-permute-done | bytes 524320 | tf_op jit(solution)/shard_map/ppermute | solution.py:18
  294.7 2.9 fusion.3
  297.6 3.6 gather_fusion.1
  301.2 3.3 broadcast_select_fusion
  304.5 4.5 all-to-all-start.1
  311.3 40.5 %all-to-all-done.1 = bf16[16,128,512]{2,1,0:T(8,128)(2,1)} async-done(((bf16[16,128,512]{2,1,0:T(8,128)(2,1)}), bf16[16,128,512]{2,1,0:T(8,128)(2,1)}, u32[]{:S(2)}, u32[]{:S(2)}) %all-to-all-start.1) | async-done | bytes 2097184 | tf_op jit(solution)/shard_map/all_to_all | solution.py:38
  353.1 4.1 collective-permute-done.10
  357.3 17.2 %all-gather.2 = f32[16,2,2]{2,1,0:T(2,128)S(1)} all-gather(f32[1,2,2]{2,1,0:T(2,128)S(1)} %bitcast.108), channel_id=1, replica_groups=mesh['pipe'=2,'dp'=16,'tensor'=4] {'dp'}, dimensions={0}, use_global_device_ids=true | all-gather | bytes 272 | tf_op jit(solution)/shard_map/all_gather | solution.py:95
  375.3 7.7 %multiply_convert_fusion = bf16[2,16,2,64,512]{4,3,2,1,0:T(8,128)(2,1)} fusion(bf16[1,16,2,64,512]{4,3,2,1,0:T(8,128)(2,1)S(1)} %bitcast.91, bf16[1,16,2,64,512]{4,3,2,1,0:T(8,128)(2,1)} %bitcast.7, bf16[1,16,2,64,512]{4,3,2,1,0:T(8,128)(2,1)} %bitcast.34, bf16[1,16,2,64,512]{4,3,2,1,0:T(8,128)(2,1)} %bitcast.33, f32[2,16,2]{2,1,0:T(8,128)S(1)} %mul.52, ...), kind=kLoop, calls=%fused_computation.3 | loop fusion | flops 20971520 | bytes 12583169 | tf_op jit(solution)/shard_map/convert_element_type | solution.py:111
  382.9 38.2 %all-gather.8.cloned.1.call-done = bf16[1,1,32,64,2048]{4,3,1,0,2:T(8,128)(2,1)} async-done(((bf16[1,1,2,64,2048]{4,3,1,0,2:T(8,128)(2,1)}), bf16[1,1,32,64,2048]{4,3,1,0,2:T(8,128)(2,1)}) %all-gather.8.cloned.1.call-update) | async-done | bytes 8388624 | tf_op jit(solution)/shard_map/all_gather | solution.py:62
  421.1 9.3 %pad_maximum_fusion = bf16[2,32,64,2048]{3,2,1,0:T(8,128)(2,1)S(1)} fusion(bf16[1,32,64,2048]{3,2,1,0:T(8,128)(2,1)} %bitcast.95, bf16[1,32,64,2048]{3,2,1,0:T(8,128)(2,1)} %bitcast.94), kind=kLoop, calls=%fused_computation.2 | loop fusion | flops 8388608 | bytes 33554432 | tf_op jit(solution)/shard_map/concatenate | solution.py:61
  430.5 10.4 %fusion.2 = f32[1,2048,512]{2,1,0:T(8,128)} fusion(bf16[1,2048,512]{2,1,0:T(8,128)(2,1)S(1)} %copy-done.9, bf16[4096,2048]{1,0:T(8,128)(2,1)S(1)} %bitcast.88, bf16[4096,512]{1,0:T(8,128)(2,1)S(1)} %bitcast.96, f32[]{:T(128)S(6)} %mul_shard_map.3), kind=kOutput, calls=%fused_computation.10 | convolution fusion | flops 8594128896 | bytes 27262980 | tf_op jit(solution)/shard_map/dot_general | solution.py:114
  (87 shorter events, 52.3 us)
Async XLA Ops:
  9.9 16.4 %collective-permute-start = (bf16[2,64,2048]{2,1,0:T(8,128)(2,1)}, bf16[2,64,2048]{2,1,0:T(8,128)(2,1)S(1)}, u32[]{:S(2)}, u32[]{:S(2)}) collective-permute-start(bf16[2,64,2048]{2,1,0:T(8,128)(2,1)} %fusion.45), channel_id=1, source_target_pairs={{0,1},{1,2},{2,3},{3,0},{4,5},{5,6},{6,7},{7,4},{8,9},{9,10},{10,1... | collective-permute-start | bytes 1572872 | tf_op jit(solution)/shard_map/ppermute | solution.py:18
  12.3 26.1 %collective-permute-start.1 = (bf16[2,64,2048]{2,1,0:T(8,128)(2,1)}, bf16[2,64,2048]{2,1,0:T(8,128)(2,1)S(1)}, u32[]{:S(2)}, u32[]{:S(2)}) collective-permute-start(bf16[2,64,2048]{2,1,0:T(8,128)(2,1)} %fusion.45), channel_id=1, source_target_pairs={{0,2},{1,3},{2,0},{3,1},{4,6},{5,7},{6,4},{7,5},{8,10},{9,11},{10,... | collective-permute-start | bytes 1572872 | tf_op jit(solution)/shard_map/ppermute | solution.py:18
  15.6 24.1 %collective-permute-start.2 = (bf16[2,64,2048]{2,1,0:T(8,128)(2,1)}, bf16[2,64,2048]{2,1,0:T(8,128)(2,1)}, u32[]{:S(2)}, u32[]{:S(2)}) collective-permute-start(bf16[2,64,2048]{2,1,0:T(8,128)(2,1)} %fusion.45), channel_id=1, source_target_pairs={{0,3},{1,0},{2,1},{3,2},{4,7},{5,4},{6,5},{7,6},{8,11},{9,8},{10,9... | collective-permute-start | bytes 1572872 | tf_op jit(solution)/shard_map/ppermute | solution.py:18
  16.4 39.5 %collective-permute-start.4 = (bf16[2048,512]{1,0:T(8,128)(2,1)}, bf16[2048,512]{1,0:T(8,128)(2,1)}, u32[]{:S(2)}, u32[]{:S(2)}) collective-permute-start(bf16[2048,512]{1,0:T(8,128)(2,1)} %bitcast.111), channel_id=1, source_target_pairs={{0,64},{64,0},{1,65},{65,1},{2,66},{66,2},{3,67},{67,3},{4,68},{68... | collective-permute-start | bytes 6291464 | tf_op jit(solution)/shard_map/ppermute | solution.py:9
  26.3 13.4 %copy-start.7 = (bf16[2,64,2048]{2,1,0:T(8,128)(2,1)}, bf16[2,64,2048]{2,1,0:T(8,128)(2,1)S(1)}, u32[]{:S(2)}) copy-start(bf16[2,64,2048]{2,1,0:T(8,128)(2,1)S(1)} %collective-permute-done) | copy-start | bytes 1572868
  47.7 34.9 %all-to-all-start = ((bf16[16,128,512]{2,1,0:T(8,128)(2,1)}), bf16[16,128,512]{2,1,0:T(8,128)(2,1)S(1)}, u32[]{:S(2)}, u32[]{:S(2)}) async-start(bf16[16,128,512]{2,1,0:T(8,128)(2,1)} %bitcast.92), calls=%async_computation | async-start | bytes 4194304 | tf_op jit(solution)/shard_map/all_to_all | solution.py:38
  54.6 43.5 %all-reduce.2.cloned.1.call-start = ((), (), s32[]{:S(2)}) async-start(), calls=%async_computation.6 | async-start | bytes 262144 | tf_op jit(solution)/shard_map/psum | solution.py:64
  55.8 115.8 %reduce-scatter.3.cloned.1.call-start = ((), (), s32[]{:S(2)}) async-start(), calls=%async_computation.4 | async-start | bytes 4456448 | tf_op jit(solution)/shard_map/reduce_scatter | solution.py:78
  92.9 159.7 %reduce-scatter.5.cloned.1.call-start = ((), (), s32[]{:S(2)}) async-start(), calls=%async_computation.5 | async-start | bytes 4456448 | tf_op jit(solution)/shard_map/reduce_scatter | solution.py:78
  93.5 159.1 %copy-start.1 = (bf16[2,2,64,2048]{3,2,1,0:T(8,128)(2,1)S(1)}, bf16[2,2,64,2048]{3,2,1,0:T(8,128)(2,1)}, u32[]{:S(2)}) copy-start(bf16[2,2,64,2048]{3,2,1,0:T(8,128)(2,1)} %param.9) | copy-start | bytes 3145732
  93.5 289.5 %all-gather.6.cloned.1.call-start = ((), (), s32[]{:S(2)}) async-start(), calls=%async_computation.7 | async-start | bytes 8912896 | tf_op jit(solution)/shard_map/all_gather | solution.py:62
  95.9 325.2 %all-gather.8.cloned.1.call-start = ((), (), s32[]{:S(2)}) async-start(), calls=%async_computation.8 | async-start | bytes 8912896 | tf_op jit(solution)/shard_map/all_gather | solution.py:62
  98.2 161.9 %collective-permute-start.8 = (f32[2,2,64,64]{3,2,1,0:T(8,128)}, f32[2,2,64,64]{3,2,1,0:T(8,128)S(1)}, u32[]{:S(2)}, u32[]{:S(2)}) collective-permute-start(f32[2,2,64,64]{3,2,1,0:T(8,128)} %all-reduce.2.cloned.1.call-done), channel_id=1, source_target_pairs={{0,64},{64,0},{1,65},{65,1},{2,66},{66,2},{3,67},{67,3},{4,68},{68... | collective-permute-start | bytes 196616 | tf_op jit(solution)/shard_map/ppermute | solution.py:9
  254.5 13.2 %collective-permute-start.5 = (bf16[2,64,2048]{2,1,0:T(8,128)(2,1)}, bf16[2,64,2048]{2,1,0:T(8,128)(2,1)}, u32[]{:S(2)}, u32[]{:S(2)}) collective-permute-start(bf16[2,64,2048]{2,1,0:T(8,128)(2,1)} %add_convert_fusion), channel_id=1, source_target_pairs={{0,1},{1,2},{2,3},{3,0},{4,5},{5,6},{6,7},{7,4},{8,9},{9,10},{10,1... | collective-permute-start | bytes 1572872 | tf_op jit(solution)/shard_map/ppermute | solution.py:18
  255.7 23.8 %collective-permute-start.6 = (bf16[2,64,2048]{2,1,0:T(8,128)(2,1)}, bf16[2,64,2048]{2,1,0:T(8,128)(2,1)}, u32[]{:S(2)}, u32[]{:S(2)}) collective-permute-start(bf16[2,64,2048]{2,1,0:T(8,128)(2,1)} %add_convert_fusion), channel_id=1, source_target_pairs={{0,2},{1,3},{2,0},{3,1},{4,6},{5,7},{6,4},{7,5},{8,10},{9,11},{10,... | collective-permute-start | bytes 1572872 | tf_op jit(solution)/shard_map/ppermute | solution.py:18
  258.3 22.3 %collective-permute-start.7 = (bf16[2,64,2048]{2,1,0:T(8,128)(2,1)}, bf16[2,64,2048]{2,1,0:T(8,128)(2,1)}, u32[]{:S(2)}, u32[]{:S(2)}) collective-permute-start(bf16[2,64,2048]{2,1,0:T(8,128)(2,1)} %add_convert_fusion), channel_id=1, source_target_pairs={{0,3},{1,0},{2,1},{3,2},{4,7},{5,4},{6,5},{7,6},{8,11},{9,8},{10,9... | collective-permute-start | bytes 1572872 | tf_op jit(solution)/shard_map/ppermute | solution.py:18
  263.2 17.5 %copy-start.10 = (f32[2,2,64,64]{3,2,1,0:T(8,128)S(1)}, f32[2,2,64,64]{3,2,1,0:T(8,128)}, u32[]{:S(2)}) copy-start(f32[2,2,64,64]{3,2,1,0:T(8,128)} %all-reduce.2.cloned.1.call-done) | copy-start | bytes 196612
  264.1 16.6 %copy-start.3 = (bf16[1,2,64,2048]{3,2,1,0:T(8,128)(2,1)S(1)}, bf16[1,2,64,2048]{3,2,1,0:T(8,128)(2,1)}, u32[]{:S(2)}) copy-start(bf16[1,2,64,2048]{3,2,1,0:T(8,128)(2,1)} %add_convert_fusion.1) | copy-start | bytes 1572868
  304.5 47.3 %all-to-all-start.1 = ((bf16[16,128,512]{2,1,0:T(8,128)(2,1)}), bf16[16,128,512]{2,1,0:T(8,128)(2,1)}, u32[]{:S(2)}, u32[]{:S(2)}) async-start(bf16[16,128,512]{2,1,0:T(8,128)(2,1)} %bitcast.93), calls=%async_computation.3 | async-start | bytes 4194304 | tf_op jit(solution)/shard_map/all_to_all | solution.py:38
  308.9 66.3 %collective-permute-start.3 = (bf16[2048,512]{1,0:T(8,128)(2,1)S(1)}, bf16[2048,512]{1,0:T(8,128)(2,1)}, u32[]{:S(2)}, u32[]{:S(2)}) collective-permute-start(bf16[2048,512]{1,0:T(8,128)(2,1)S(1)} %bitcast.90), channel_id=1, source_target_pairs={{0,64},{64,0},{1,65},{65,1},{2,66},{66,2},{3,67},{67,3},{4,68},{68... | collective-permute-start | bytes 6291464 | tf_op jit(solution)/shard_map/ppermute | solution.py:9
  351.8 23.5 %collective-permute-start.9 = (bf16[2048,512]{1,0:T(8,128)(2,1)}, bf16[2048,512]{1,0:T(8,128)(2,1)}, u32[]{:S(2)}, u32[]{:S(2)}) collective-permute-start(bf16[2048,512]{1,0:T(8,128)(2,1)} %bitcast.32), channel_id=1, source_target_pairs={{0,64},{64,0},{1,65},{65,1},{2,66},{66,2},{3,67},{67,3},{4,68},{68... | collective-permute-start | bytes 6291464 | tf_op jit(solution)/shard_map/ppermute | solution.py:9
  353.1 4.1 collective-permute-start.10
  421.1 9.3 %copy-start = (bf16[2,16,2,64,512]{4,3,2,1,0:T(8,128)(2,1)S(1)}, bf16[2,16,2,64,512]{4,3,2,1,0:T(8,128)(2,1)}, u32[]{:S(2)}) copy-start(bf16[2,16,2,64,512]{4,3,2,1,0:T(8,128)(2,1)} %multiply_convert_fusion) | copy-start | bytes 12582916
  421.1 9.4 %copy-start.9 = (bf16[1,2048,512]{2,1,0:T(8,128)(2,1)S(1)}, bf16[1,2048,512]{2,1,0:T(8,128)(2,1)}, u32[]{:S(2)}) copy-start(bf16[1,2048,512]{2,1,0:T(8,128)(2,1)} %param.11) | copy-start | bytes 6291460
  (5 other events, 23.7 us)
Sparse Core Ops, SparseCore 0:
  57.8 40.3 all-reduce.1
Sparse Core Ops, SparseCore 1:
  93.0 78.6 reduce-scatter.2
  174.8 77.7 reduce-scatter.4
  254.5 92.7 all-gather.5
  349.5 71.6 all-gather.7

commit v6 on v4

--- a/solution.py
+++ b/solution.py
@@ -35,8 +35,26 @@
     per_piece = width_part // column_part
     chunks = stacked.reshape(pieces, token_count, per_piece, column_part).transpose(0, 2, 1, 3)
     chunks = jnp.take(chunks, order, axis=0).reshape(pieces * per_piece, token_count, column_part)
+    extra = 0
+    if row_scales is not None:
+        parts = []
+        rest = row_scales
+        for _ in range(3):
+            part = rest.astype(jnp.bfloat16)
+            parts.append(part)
+            rest = rest - part.astype(jnp.float32)
+        extra = 16
+        rows = jnp.zeros((extra, column_part), jnp.bfloat16)
+        rows = rows.at[: len(parts), :example_count].set(jnp.stack(parts))
+        rows = jnp.broadcast_to(rows[None], (pieces * per_piece, extra, column_part))
+        chunks = jnp.concatenate([chunks, rows], axis=1)
     moved = lax.all_to_all(chunks, "dp", split_axis=0, concat_axis=1, tiled=True)
-    return moved.reshape(group_count * token_count, column_part)
+    moved = moved.reshape(group_count, token_count + extra, column_part)
+    blocks = moved[:, :token_count].reshape(group_count * token_count, column_part)
+    if row_scales is None:
+        return blocks
+    received = moved[:, token_count : token_count + 3, :example_count].astype(jnp.float32)
+    return blocks, (received[:, 2] + received[:, 1]) + received[:, 0]
 
 
 def token_grams(values):
@@ -87,10 +105,10 @@
     bound = clip_norm[0]
     own_scales = bound / jnp.maximum(jnp.sqrt(norm_square), bound)
     scale_terms = by_micro(is_last, own_scales, swapped(own_scales, "pipe"))
-    all_scales = lax.all_gather(scale_terms, "dp", axis=1, tiled=True)
 
-    first_blocks = column_blocks(first_pieces, first_order, group_count, column_part, own_scales)
+    first_blocks, group_scales = column_blocks(first_pieces, first_order, group_count, column_part, own_scales)
     first_blocks_other = swapped(first_blocks, "pipe")
+    all_scales = by_micro(is_last, group_scales, swapped(group_scales, "pipe"))
 
     grad_blocks = jnp.where(
         is_last,

time: 351 us -> 347 us (0.989)
  waiting for transfers between devices: 189 us -> 217 us
  blocking collectives: 18.9 us -> 0 us
  local copies, waits for them, and re-layouts: 37.6 us -> 29.3 us
    all_gather x1 -> x0, blocking collectives: 18.9 us -> none  [local(): all_scales = lax.all_gather(scale_terms, 'dp', axis=1, tiled=True)]
    all_gather x1, waiting for transfers between devices: 0.01 us -> 16.3 us  [local(): gathered_inputs = lax.all_gather(local_inputs, 'dp', axis=1, tiled=True)]
    another operation x16, local copies, waits for them, and re-layouts: 18.6 us -> 10.4 us  [ring_pieces(): stacked = jnp.stack(pieces)]
    all_to_all x2, waiting for transfers between devices: 75.8 us -> 81.7 us  [column_blocks(): lax.all_to_all(chunks, 'dp', split_axis=0, concat_axis=1, tiled=True)]
    unnamed x16 -> x28, local copies, waits for them, and re-layouts: 10.8 us -> 12 us
    ppermute x5 -> x6, starting transfers between devices: 10.6 us -> 10.3 us  [swapped(): lax.ppermute(value, axis, [(source, count - 1 - source) for source in ran...]
  transfers between devices with their start and end apart: 16 -> 17, of which waited for: 9 -> 12; matrix products, arithmetic and copies ran while one was open for 17% -> 13% of each run, Pallas kernels for 0% -> 0%
where the time goes in v6:
time: 347 us; the launch traced here: 346 us
  waiting for transfers between devices  217 us (63%)
  starting transfers between devices  33.4 us (10%)
  matrix products  29.9 us (9%)
  local copies, waits for them, and re-layouts  29.3 us (8%)
  other arithmetic  19.6 us (6%)
  between operations  16.4 us (5%)
    reduce_scatter x1, waiting for transfers between devices, local(): lax.psum_scatter(terms, 'dp', scatter_dimension=0, tiled=True)  83.5 us
    all_to_all x2, waiting for transfers between devices, column_blocks(): lax.all_to_all(chunks, 'dp', split_axis=0, concat_axis=1, tiled=True)  81.7 us
    ppermute x6, waiting for transfers between devices, ring_pieces(): lax.ppermute(values, axis, [(source, (source + offset) % count) for sourc...  32.3 us
    all_gather x1, waiting for transfers between devices, local(): gathered_inputs = lax.all_gather(local_inputs, 'dp', axis=1, tiled=True)  16.3 us
    dot_general x1, matrix products, local(): lax.dot_general(flat_inputs, flat_grads, (((0,), (0,)), ((), ())), prefer...  15 us
    unnamed x28, local copies, waits for them, and re-layouts  12 us
    ppermute x6, starting transfers between devices, ring_pieces(): lax.ppermute(values, axis, [(source, (source + offset) % count) for sourc...  11.5 us
    all_to_all x2, starting transfers between devices, column_blocks(): lax.all_to_all(chunks, 'dp', split_axis=0, concat_axis=1, tiled=True)  11.4 us
  transfers between devices with their start and end apart: 17, of which 12 were waited for; matrix products, arithmetic and copies ran while one was open for 13% of the time, Pallas kernels for 0%

profile of v6, /device:TPU:1, one launch (start us, length us, event | category | flops | bytes accessed | tf_op | source)
XLA Modules:
  0.0 345.8 jit_solution(638347614685283321)
XLA Ops:
  10.1 2.5 collective-permute-start
  12.5 3.3 collective-permute-start.1
  19.4 7.0 %collective-permute-done = bf16[2,64,2048]{2,1,0:T(8,128)(2,1)S(1)} collective-permute-done((bf16[2,64,2048]{2,1,0:T(8,128)(2,1)}, bf16[2,64,2048]{2,1,0:T(8,128)(2,1)S(1)}, u32[]{:S(2)}, u32[]{:S(2)}) %collective-permute-start) | collective-permute-done | bytes 524320 | tf_op jit(solution)/shard_map/ppermute | solution.py:18
  27.8 10.9 %collective-permute-done.1 = bf16[2,64,2048]{2,1,0:T(8,128)(2,1)S(1)} collective-permute-done((bf16[2,64,2048]{2,1,0:T(8,128)(2,1)}, bf16[2,64,2048]{2,1,0:T(8,128)(2,1)S(1)}, u32[]{:S(2)}, u32[]{:S(2)}) %collective-permute-start.1) | collective-permute-done | bytes 524320 | tf_op jit(solution)/shard_map/ppermute | solution.py:18
  43.1 2.0 gather_fusion
  45.1 3.2 broadcast_select_fusion.1
  48.2 6.8 %all-to-all-start = ((bf16[16,128,512]{2,1,0:T(8,128)(2,1)}), bf16[16,128,512]{2,1,0:T(8,128)(2,1)S(1)}, u32[]{:S(2)}, u32[]{:S(2)}) async-start(bf16[16,128,512]{2,1,0:T(8,128)(2,1)} %bitcast.100), calls=%async_computation | async-start | bytes 4194304 | tf_op jit(solution)/shard_map/all_to_all | solution.py:51
  55.1 28.0 %all-to-all-done = bf16[16,128,512]{2,1,0:T(8,128)(2,1)S(1)} async-done(((bf16[16,128,512]{2,1,0:T(8,128)(2,1)}), bf16[16,128,512]{2,1,0:T(8,128)(2,1)S(1)}, u32[]{:S(2)}, u32[]{:S(2)}) %all-to-all-start) | async-done | bytes 2097184 | tf_op jit(solution)/shard_map/all_to_all | solution.py:51
  83.0 9.1 %convolution_convert_fusion = bf16[2048,2048]{1,0:T(8,128)(2,1)} fusion(bf16[2048,512]{1,0:T(8,128)(2,1)S(1)} %bitcast.97, bf16[2048,512]{1,0:T(8,128)(2,1)} %collective-permute-done.4, pred[]{:T(512)S(6)} %eq.6, bf16[1,2048,512]{2,1,0:T(8,128)(2,1)} %param.9), kind=kOutput, calls=%fused_computation.3 | convolution fusion | flops 4300210176 | bytes 14680065 | tf_op jit(solution)/shard_map/dot_general | solution.py:89
  95.3 83.5 %reduce-scatter.2.cloned.1.call-done = bf16[128,2048]{1,0:T(8,128)(2,1)} async-done(((bf16[2048,2048]{1,0:T(8,128)(2,1)}), bf16[128,2048]{1,0:T(8,128)(2,1)}) %reduce-scatter.2.cloned.1.call-update) | async-done | bytes 524304 | tf_op jit(solution)/shard_map/reduce_scatter | solution.py:92
  181.3 2.6 collective-permute-start.6
  185.0 2.9 collective-permute-start.8
  192.7 12.4 %collective-permute-done.6 = bf16[2,64,2048]{2,1,0:T(8,128)(2,1)} collective-permute-done((bf16[2,64,2048]{2,1,0:T(8,128)(2,1)S(1)}, bf16[2,64,2048]{2,1,0:T(8,128)(2,1)}, u32[]{:S(2)}, u32[]{:S(2)}) %collective-permute-start.6) | collective-permute-done | bytes 524320 | tf_op jit(solution)/shard_map/ppermute | solution.py:18
  205.9 2.8 fusion.32
  215.4 2.3 gather_fusion.1
  219.6 4.7 %all-to-all-start.1 = ((bf16[16,144,512]{2,1,0:T(8,128)(2,1)}), bf16[16,144,512]{2,1,0:T(8,128)(2,1)S(1)}, u32[]{:S(2)}, u32[]{:S(2)}) async-start(bf16[16,144,512]{2,1,0:T(8,128)(2,1)} %pad_maximum_fusion), calls=%async_computation.2 | async-start | bytes 4718592 | tf_op jit(solution)/shard_map/all_to_all | solution.py:51
  224.3 2.5 collective-permute-start.3
  226.8 53.7 %all-to-all-done.1 = bf16[16,144,512]{2,1,0:T(8,128)(2,1)S(1)} async-done(((bf16[16,144,512]{2,1,0:T(8,128)(2,1)}), bf16[16,144,512]{2,1,0:T(8,128)(2,1)S(1)}, u32[]{:S(2)}, u32[]{:S(2)}) %all-to-all-start.1) | async-done | bytes 2359328 | tf_op jit(solution)/shard_map/all_to_all | solution.py:51
  282.0 3.1 collective-permute-start.9
  285.2 4.0 %copy.101 = bf16[1,2048,512]{1,2,0:T(8,128)(2,1)} copy(bf16[1,2048,512]{2,1,0:T(8,128)(2,1)} %param.13) | data formatting | bytes 4194304 | tf_op args[4]
  292.4 9.3 %multiply_convert_fusion = bf16[2,16,2,64,512]{4,3,2,1,0:T(8,128)(2,1)} fusion(bf16[1,16,2,64,512]{4,3,2,1,0:T(8,128)(2,1)} %bitcast.99, bf16[1,16,2,64,512]{4,3,2,1,0:T(8,128)(2,1)} %bitcast.4, bf16[1,16,2,64,512]{4,3,2,1,0:T(8,128)(2,1)} %bitcast.34, bf16[1,16,2,64,512]{4,3,2,1,0:T(8,128)(2,1)} %bitcast.33, f32[2,16,2]{2,1,0:T(8,128)S(1)} %copy.100, pred[]{:T(512)S(6)} %eq.6), kind=kLoop, calls=%fused_computation.2 | loop fusion | flops 20971520 | bytes 12583169 | tf_op jit(solution)/shard_map/convert_element_type | solution.py:124
  301.7 16.3 %all-gather.3.cloned.1.call-done = bf16[1,2,32,64,2048]{4,3,2,1,0:T(8,128)(2,1)} async-done(((bf16[1,2,2,64,2048]{4,3,2,1,0:T(8,128)(2,1)}), bf16[1,2,32,64,2048]{4,3,2,1,0:T(8,128)(2,1)}) %all-gather.3.cloned.1.call-update) | async-done | bytes 16777232 | tf_op jit(solution)/shard_map/all_gather | solution.py:79
  318.0 15.0 %fusion.2 = f32[1,2048,512]{1,2,0:T(8,128)} fusion(bf16[1,2048,512]{1,2,0:T(8,128)(2,1)S(1)} %copy-done.3, bf16[4096,512]{1,0:T(8,128)(2,1)} %bitcast.102, bf16[4096,2048]{1,0:T(8,128)(2,1)} %bitcast.112, f32[]{:T(128)S(6)} %mul_shard_map.3), kind=kOutput, calls=%fused_computation.9 | convolution fusion | flops 8594128896 | bytes 27262980 | tf_op jit(solution)/shard_map/dot_general | solution.py:127
  332.9 5.4 %copy.102 = f32[1,2048,512]{2,1,0:T(8,128)} copy(f32[1,2048,512]{1,2,0:T(8,128)} %fusion.2) | data formatting | bytes 8388608
  (90 shorter events, 36.4 us)
Async XLA Ops:
  10.1 16.4 %collective-permute-start = (bf16[2,64,2048]{2,1,0:T(8,128)(2,1)}, bf16[2,64,2048]{2,1,0:T(8,128)(2,1)S(1)}, u32[]{:S(2)}, u32[]{:S(2)}) collective-permute-start(bf16[2,64,2048]{2,1,0:T(8,128)(2,1)} %fusion.58), channel_id=1, source_target_pairs={{0,1},{1,2},{2,3},{3,0},{4,5},{5,6},{6,7},{7,4},{8,9},{9,10},{10,1... | collective-permute-start | bytes 1572872 | tf_op jit(solution)/shard_map/ppermute | solution.py:18
  12.5 26.1 %collective-permute-start.1 = (bf16[2,64,2048]{2,1,0:T(8,128)(2,1)}, bf16[2,64,2048]{2,1,0:T(8,128)(2,1)S(1)}, u32[]{:S(2)}, u32[]{:S(2)}) collective-permute-start(bf16[2,64,2048]{2,1,0:T(8,128)(2,1)} %fusion.58), channel_id=1, source_target_pairs={{0,2},{1,3},{2,0},{3,1},{4,6},{5,7},{6,4},{7,5},{8,10},{9,11},{10,... | collective-permute-start | bytes 1572872 | tf_op jit(solution)/shard_map/ppermute | solution.py:18
  15.8 24.1 %collective-permute-start.2 = (bf16[2,64,2048]{2,1,0:T(8,128)(2,1)}, bf16[2,64,2048]{2,1,0:T(8,128)(2,1)}, u32[]{:S(2)}, u32[]{:S(2)}) collective-permute-start(bf16[2,64,2048]{2,1,0:T(8,128)(2,1)} %fusion.58), channel_id=1, source_target_pairs={{0,3},{1,0},{2,1},{3,2},{4,7},{5,4},{6,5},{7,6},{8,11},{9,8},{10,9... | collective-permute-start | bytes 1572872 | tf_op jit(solution)/shard_map/ppermute | solution.py:18
  16.6 38.5 %collective-permute-start.4 = (bf16[2048,512]{1,0:T(8,128)(2,1)}, bf16[2048,512]{1,0:T(8,128)(2,1)}, u32[]{:S(2)}, u32[]{:S(2)}) collective-permute-start(bf16[2048,512]{1,0:T(8,128)(2,1)} %bitcast.113), channel_id=1, source_target_pairs={{0,64},{64,0},{1,65},{65,1},{2,66},{66,2},{3,67},{67,3},{4,68},{68... | collective-permute-start | bytes 6291464 | tf_op jit(solution)/shard_map/ppermute | solution.py:9
  18.1 9.6 %copy-start.4 = (bf16[1,2,64,2048]{3,2,0,1:T(8,128)(2,1)}, bf16[1,2,64,2048]{3,2,0,1:T(8,128)(2,1)S(1)}, u32[]{:S(2)}) copy-start(bf16[1,2,64,2048]{3,2,0,1:T(8,128)(2,1)S(1)} %fusion.57) | copy-start | bytes 1572868
  26.5 13.4 %copy-start.7 = (bf16[2,64,2048]{2,1,0:T(8,128)(2,1)}, bf16[2,64,2048]{2,1,0:T(8,128)(2,1)S(1)}, u32[]{:S(2)}) copy-start(bf16[2,64,2048]{2,1,0:T(8,128)(2,1)S(1)} %collective-permute-done) | copy-start | bytes 1572868
  48.2 34.8 %all-to-all-start = ((bf16[16,128,512]{2,1,0:T(8,128)(2,1)}), bf16[16,128,512]{2,1,0:T(8,128)(2,1)S(1)}, u32[]{:S(2)}, u32[]{:S(2)}) async-start(bf16[16,128,512]{2,1,0:T(8,128)(2,1)} %bitcast.100), calls=%async_computation | async-start | bytes 4194304 | tf_op jit(solution)/shard_map/all_to_all | solution.py:51
  55.0 123.8 %reduce-scatter.2.cloned.1.call-start = ((), (), s32[]{:S(2)}) async-start(), calls=%async_computation.3 | async-start | bytes 8912896 | tf_op jit(solution)/shard_map/reduce_scatter | solution.py:92
  92.2 92.8 %all-reduce.3.cloned.1.call-start = ((), (), s32[]{:S(2)}) async-start(), calls=%async_computation.4 | async-start | bytes 262144 | tf_op jit(solution)/shard_map/psum | solution.py:80
  94.5 94.6 %copy-start.5 = (bf16[1,2,64,2048]{3,2,0,1:T(8,128)(2,1)S(1)}, bf16[1,2,64,2048]{3,2,0,1:T(8,128)(2,1)}, u32[]{:S(2)}) copy-start(bf16[1,2,64,2048]{3,2,0,1:T(8,128)(2,1)} %copy-done.4) | copy-start | bytes 1572868
  94.5 94.6 %copy-start.8 = (bf16[2,64,2048]{2,1,0:T(8,128)(2,1)S(1)}, bf16[2,64,2048]{2,1,0:T(8,128)(2,1)}, u32[]{:S(2)}) copy-start(bf16[2,64,2048]{2,1,0:T(8,128)(2,1)} %copy-done.7) | copy-start | bytes 1572868
  94.5 94.6 %copy-start.10 = (bf16[2,64,2048]{2,1,0:T(8,128)(2,1)S(1)}, bf16[2,64,2048]{2,1,0:T(8,128)(2,1)}, u32[]{:S(2)}) copy-start(bf16[2,64,2048]{2,1,0:T(8,128)(2,1)} %copy-done.9) | copy-start | bytes 1572868
  94.5 223.5 %all-gather.3.cloned.1.call-start = ((), (), s32[]{:S(2)}) async-start(), calls=%async_computation.5 | async-start | bytes 17825792 | tf_op jit(solution)/shard_map/all_gather | solution.py:79
  179.9 12.7 %collective-permute-start.5 = (bf16[2,64,2048]{2,1,0:T(8,128)(2,1)S(1)}, bf16[2,64,2048]{2,1,0:T(8,128)(2,1)}, u32[]{:S(2)}, u32[]{:S(2)}) collective-permute-start(bf16[2,64,2048]{2,1,0:T(8,128)(2,1)S(1)} %bitcast.103), channel_id=1, source_target_pairs={{0,1},{1,2},{2,3},{3,0},{4,5},{5,6},{6,7},{7,4},{8,9},{9,10},{10,1... | collective-permute-start | bytes 1572872 | tf_op jit(solution)/shard_map/ppermute | solution.py:18
  181.3 23.8 %collective-permute-start.6 = (bf16[2,64,2048]{2,1,0:T(8,128)(2,1)S(1)}, bf16[2,64,2048]{2,1,0:T(8,128)(2,1)}, u32[]{:S(2)}, u32[]{:S(2)}) collective-permute-start(bf16[2,64,2048]{2,1,0:T(8,128)(2,1)S(1)} %bitcast.104), channel_id=1, source_target_pairs={{0,2},{1,3},{2,0},{3,1},{4,6},{5,7},{6,4},{7,5},{8,10},{9,11},{10,... | collective-permute-start | bytes 1572872 | tf_op jit(solution)/shard_map/ppermute | solution.py:18
  183.9 22.1 %collective-permute-start.7 = (bf16[2,64,2048]{2,1,0:T(8,128)(2,1)S(1)}, bf16[2,64,2048]{2,1,0:T(8,128)(2,1)}, u32[]{:S(2)}, u32[]{:S(2)}) collective-permute-start(bf16[2,64,2048]{2,1,0:T(8,128)(2,1)S(1)} %bitcast.105), channel_id=1, source_target_pairs={{0,3},{1,0},{2,1},{3,2},{4,7},{5,4},{6,5},{7,6},{8,11},{9,8},{10,9... | collective-permute-start | bytes 1572872 | tf_op jit(solution)/shard_map/ppermute | solution.py:18
  185.0 4.1 %collective-permute-start.8 = (f32[2,2,64,64]{3,2,1,0:T(8,128)}, f32[2,2,64,64]{3,2,1,0:T(8,128)S(1)}, u32[]{:S(2)}, u32[]{:S(2)}) collective-permute-start(f32[2,2,64,64]{3,2,1,0:T(8,128)} %all-reduce.3.cloned.1.call-done), channel_id=1, source_target_pairs={{0,64},{64,0},{1,65},{65,1},{2,66},{66,2},{3,67},{67,3},{4,68},{68... | collective-permute-start | bytes 196616 | tf_op jit(solution)/shard_map/ppermute | solution.py:9
  191.1 14.8 %copy-start.11 = (f32[2,2,64,64]{3,2,1,0:T(8,128)S(1)}, f32[2,2,64,64]{3,2,1,0:T(8,128)}, u32[]{:S(2)}) copy-start(f32[2,2,64,64]{3,2,1,0:T(8,128)} %all-reduce.3.cloned.1.call-done) | copy-start | bytes 196612
  219.6 60.9 %all-to-all-start.1 = ((bf16[16,144,512]{2,1,0:T(8,128)(2,1)}), bf16[16,144,512]{2,1,0:T(8,128)(2,1)S(1)}, u32[]{:S(2)}, u32[]{:S(2)}) async-start(bf16[16,144,512]{2,1,0:T(8,128)(2,1)} %pad_maximum_fusion), calls=%async_computation.2 | async-start | bytes 4718592 | tf_op jit(solution)/shard_map/all_to_all | solution.py:51
  224.3 68.1 %collective-permute-start.3 = (bf16[2048,512]{1,0:T(8,128)(2,1)}, bf16[2048,512]{1,0:T(8,128)(2,1)}, u32[]{:S(2)}, u32[]{:S(2)}) collective-permute-start(bf16[2048,512]{1,0:T(8,128)(2,1)} %bitcast.98), channel_id=1, source_target_pairs={{0,64},{64,0},{1,65},{65,1},{2,66},{66,2},{3,67},{67,3},{4,68},{68... | collective-permute-start | bytes 6291464 | tf_op jit(solution)/shard_map/ppermute | solution.py:9
  282.0 10.4 %collective-permute-start.9 = (bf16[2048,512]{1,0:T(8,128)(2,1)}, bf16[2048,512]{1,0:T(8,128)(2,1)}, u32[]{:S(2)}, u32[]{:S(2)}) collective-permute-start(bf16[2048,512]{1,0:T(8,128)(2,1)} %bitcast.32), channel_id=1, source_target_pairs={{0,64},{64,0},{1,65},{65,1},{2,66},{66,2},{3,67},{67,3},{4,68},{68... | collective-permute-start | bytes 6291464 | tf_op jit(solution)/shard_map/ppermute | solution.py:9
  289.2 1.2 collective-permute-start.11
  291.1 1.2 collective-permute-start.10
  292.4 25.6 %copy-start.3 = (bf16[1,2048,512]{1,2,0:T(8,128)(2,1)S(1)}, bf16[1,2048,512]{1,2,0:T(8,128)(2,1)}, u32[]{:S(2)}) copy-start(bf16[1,2048,512]{1,2,0:T(8,128)(2,1)} %copy.101) | copy-start | bytes 6291460
  (5 other events, 19.7 us)
Sparse Core Ops, SparseCore 0:
  92.3 86.4 reduce-scatter.1
  180.9 137.0 all-gather.2
Sparse Core Ops, SparseCore 1:
  95.6 41.5 all-reduce.2

commit v7 on v6

--- a/solution.py
+++ b/solution.py
@@ -40,7 +40,7 @@
         parts = []
         rest = row_scales
         for _ in range(3):
-            part = rest.astype(jnp.bfloat16)
+            part = lax.optimization_barrier(rest.astype(jnp.bfloat16))
             parts.append(part)
             rest = rest - part.astype(jnp.float32)
         extra = 16
@@ -78,7 +78,6 @@
 
     gathered_inputs = lax.all_gather(local_inputs, "dp", axis=1, tiled=True)
     input_grams = lax.psum(token_grams(local_inputs), "tensor")
-    other_input_grams = swapped(input_grams, "pipe")
 
     own_cotangent = lax.dynamic_index_in_dim(cotangent, section_index, 0, keepdims=False)
     last_pieces, last_order, last_grams = feature_pieces(own_cotangent)
@@ -89,7 +88,9 @@
     terms = lax.dot_general(
         last_blocks, last_weights, (((1,), (1,)), ((), ())), preferred_element_type=jnp.float32
     ).astype(jnp.bfloat16)
+    terms, gathered_inputs, input_grams = lax.optimization_barrier((terms, gathered_inputs, input_grams))
     summed = lax.psum_scatter(terms, "dp", scatter_dimension=0, tiled=True).astype(jnp.float32)
+    other_input_grams = swapped(input_grams, "pipe")
     renewed = (own_cotangent.reshape(token_count, width_part).astype(jnp.float32) + summed).astype(
         jnp.bfloat16
     ).reshape(example_count, length_count, width_part)

time: 347 us -> 358 us (1.032)
  waiting for transfers between devices: 217 us -> 237 us
  local copies, waits for them, and re-layouts: 29.3 us -> 18.1 us
    all_gather x1, waiting for transfers between devices: 16.3 us -> 32 us  [local(): gathered_inputs = lax.all_gather(local_inputs, 'dp', axis=1, tiled=True)]
    unnamed x28 -> x24, local copies, waits for them, and re-layouts: 12 us -> 0.2 us
    reduce_scatter x1, waiting for transfers between devices: 83.5 us -> 87.4 us  [local(): lax.psum_scatter(terms, 'dp', scatter_dimension=0, tiled=True)]
  transfers between devices with their start and end apart: 17 -> 17, of which waited for: 12 -> 12; matrix products, arithmetic and copies ran while one was open for 13% -> 8% of each run, Pallas kernels for 0% -> 0%
where the time goes in v7:
time: 358 us; the launch traced here: 356 us
  waiting for transfers between devices  237 us (66%)
  starting transfers between devices  35.2 us (10%)
  matrix products  30.3 us (8%)
  other arithmetic  19.3 us (5%)
  local copies, waits for them, and re-layouts  18.1 us (5%)
  between operations  16.4 us (5%)
    reduce_scatter x1, waiting for transfers between devices, local(): lax.psum_scatter(terms, 'dp', scatter_dimension=0, tiled=True)  87.4 us
    all_to_all x2, waiting for transfers between devices, column_blocks(): lax.all_to_all(chunks, 'dp', split_axis=0, concat_axis=1, tiled=True)  78.2 us
    ppermute x6, waiting for transfers between devices, ring_pieces(): lax.ppermute(values, axis, [(source, (source + offset) % count) for sourc...  33.2 us
    all_gather x1, waiting for transfers between devices, local(): gathered_inputs = lax.all_gather(local_inputs, 'dp', axis=1, tiled=True)  32 us
    dot_general x1, matrix products, local(): lax.dot_general(flat_inputs, flat_grads, (((0,), (0,)), ((), ())), prefer...  13.9 us
    ppermute x6, starting transfers between devices, swapped(): lax.ppermute(value, axis, [(source, count - 1 - source) for source in ran...  12.2 us
    ppermute x6, starting transfers between devices, ring_pieces(): lax.ppermute(values, axis, [(source, (source + offset) % count) for sourc...  11.5 us
    all_to_all x2, starting transfers between devices, column_blocks(): lax.all_to_all(chunks, 'dp', split_axis=0, concat_axis=1, tiled=True)  11.4 us
  transfers between devices with their start and end apart: 17, of which 12 were waited for; matrix products, arithmetic and copies ran while one was open for 8% of the time, Pallas kernels for 0%

profile of v7, /device:TPU:1, one launch (start us, length us, event | category | flops | bytes accessed | tf_op | source)
XLA Modules:
  0.0 356.1 jit_solution(5764984294672538421)
XLA Ops:
  8.1 2.7 fusion.29
  12.2 2.5 collective-permute-start
  14.7 3.3 collective-permute-start.1
  21.6 7.4 %collective-permute-done = bf16[2,64,2048]{2,1,0:T(8,128)(2,1)S(1)} collective-permute-done((bf16[2,64,2048]{2,1,0:T(8,128)(2,1)}, bf16[2,64,2048]{2,1,0:T(8,128)(2,1)S(1)}, u32[]{:S(2)}, u32[]{:S(2)}) %collective-permute-start) | collective-permute-done | bytes 524320 | tf_op jit(solution)/shard_map/ppermute | solution.py:18
  30.3 11.3 %collective-permute-done.1 = bf16[2,64,2048]{2,1,0:T(8,128)(2,1)S(1)} collective-permute-done((bf16[2,64,2048]{2,1,0:T(8,128)(2,1)}, bf16[2,64,2048]{2,1,0:T(8,128)(2,1)S(1)}, u32[]{:S(2)}, u32[]{:S(2)}) %collective-permute-start.1) | collective-permute-done | bytes 524320 | tf_op jit(solution)/shard_map/ppermute | solution.py:18
  46.1 2.0 gather_fusion
  48.1 3.2 broadcast_select_fusion.1
  51.2 6.7 %all-to-all-start = ((bf16[16,128,512]{2,1,0:T(8,128)(2,1)}), bf16[16,128,512]{2,1,0:T(8,128)(2,1)S(1)}, u32[]{:S(2)}, u32[]{:S(2)}) async-start(bf16[16,128,512]{2,1,0:T(8,128)(2,1)} %bitcast.99), calls=%async_computation | async-start | bytes 4194304 | tf_op jit(solution)/shard_map/all_to_all | solution.py:51
  58.0 50.7 %all-to-all-done = bf16[16,128,512]{2,1,0:T(8,128)(2,1)S(1)} async-done(((bf16[16,128,512]{2,1,0:T(8,128)(2,1)}), bf16[16,128,512]{2,1,0:T(8,128)(2,1)S(1)}, u32[]{:S(2)}, u32[]{:S(2)}) %all-to-all-start) | async-done | bytes 2097184 | tf_op jit(solution)/shard_map/all_to_all | solution.py:51
  108.7 9.1 %convolution_convert_fusion = bf16[2048,2048]{1,0:T(8,128)(2,1)} fusion(bf16[2048,512]{1,0:T(8,128)(2,1)S(1)} %bitcast.96, bf16[2048,512]{1,0:T(8,128)(2,1)} %collective-permute-done.3, pred[]{:T(512)S(6)} %eq.6, bf16[1,2048,512]{2,1,0:T(8,128)(2,1)} %param.9), kind=kOutput, calls=%fused_computation.3 | convolution fusion | flops 4300210176 | bytes 14680065 | tf_op jit(solution)/shard_map/dot_general | solution.py:88
  117.8 32.0 %all-gather.3.cloned.1.call-done = bf16[1,2,32,64,2048]{4,3,2,1,0:T(8,128)(2,1)} async-done(((bf16[1,2,2,64,2048]{4,3,2,1,0:T(8,128)(2,1)}), bf16[1,2,32,64,2048]{4,3,2,1,0:T(8,128)(2,1)}) %all-gather.3.cloned.1.call-update) | async-done | bytes 16777232 | tf_op jit(solution)/shard_map/all_gather | solution.py:79
  149.9 87.4 %reduce-scatter.2.cloned.1.call-done = bf16[128,2048]{1,0:T(8,128)(2,1)} async-done(((bf16[2048,2048]{1,0:T(8,128)(2,1)}), bf16[128,2048]{1,0:T(8,128)(2,1)}) %reduce-scatter.2.cloned.1.call-update) | async-done | bytes 524304 | tf_op jit(solution)/shard_map/reduce_scatter | solution.py:92
  239.9 2.6 collective-permute-start.6
  243.5 3.0 collective-permute-start.8
  251.2 12.4 %collective-permute-done.6 = bf16[2,64,2048]{2,1,0:T(8,128)(2,1)} collective-permute-done((bf16[2,64,2048]{2,1,0:T(8,128)(2,1)S(1)}, bf16[2,64,2048]{2,1,0:T(8,128)(2,1)}, u32[]{:S(2)}, u32[]{:S(2)}) %collective-permute-start.6) | collective-permute-done | bytes 524320 | tf_op jit(solution)/shard_map/ppermute | solution.py:18
  264.5 2.7 fusion.32
  274.4 2.0 gather_fusion.1
  279.9 4.7 %all-to-all-start.1 = ((bf16[16,144,512]{2,1,0:T(8,128)(2,1)}), bf16[16,144,512]{2,1,0:T(8,128)(2,1)S(1)}, u32[]{:S(2)}, u32[]{:S(2)}) async-start(bf16[16,144,512]{2,1,0:T(8,128)(2,1)} %pad_maximum_fusion), calls=%async_computation.2 | async-start | bytes 4718592 | tf_op jit(solution)/shard_map/all_to_all | solution.py:51
  284.6 2.5 collective-permute-start.4
  287.1 27.5 %all-to-all-done.1 = bf16[16,144,512]{2,1,0:T(8,128)(2,1)S(1)} async-done(((bf16[16,144,512]{2,1,0:T(8,128)(2,1)}), bf16[16,144,512]{2,1,0:T(8,128)(2,1)S(1)}, u32[]{:S(2)}, u32[]{:S(2)}) %all-to-all-start.1) | async-done | bytes 2359328 | tf_op jit(solution)/shard_map/all_to_all | solution.py:51
  316.1 4.8 %collective-permute-start.9 = (bf16[2048,512]{1,0:T(8,128)(2,1)}, bf16[2048,512]{1,0:T(8,128)(2,1)}, u32[]{:S(2)}, u32[]{:S(2)}) collective-permute-start(bf16[2048,512]{1,0:T(8,128)(2,1)} %bitcast.36), channel_id=1, source_target_pairs={{0,64},{64,0},{1,65},{65,1},{2,66},{66,2},{3,67},{67,3},{4,68},{68... | collective-permute-start | bytes 6291464 | tf_op jit(solution)/shard_map/ppermute | solution.py:9
  320.9 4.1 %collective-permute-done.11 = f32[2]{0:T(128)S(1)} collective-permute-done((f32[2]{0:T(128)S(1)}, f32[2]{0:T(128)S(1)}, u32[]{:S(2)}, u32[]{:S(2)}) %collective-permute-start.11) | collective-permute-done | bytes 40 | tf_op jit(solution)/shard_map/ppermute | solution.py:9
  327.1 7.6 %multiply_convert_fusion = bf16[2,16,2,64,512]{4,3,2,1,0:T(8,128)(2,1)S(1)} fusion(bf16[1,16,2,64,512]{4,3,2,1,0:T(8,128)(2,1)} %bitcast.98, bf16[1,16,2,64,512]{4,3,2,1,0:T(8,128)(2,1)} %bitcast.8, bf16[1,16,2,64,512]{4,3,2,1,0:T(8,128)(2,1)} %bitcast.38, bf16[1,16,2,64,512]{4,3,2,1,0:T(8,128)(2,1)} %bitcast.37, f32[2,16,2]{2,1,0:T(8,128)S(1)} %copy.90, ...), kind=kLoop, calls=%fused_computation.2 | loop fusion | flops 20971520 | bytes 12583169 | tf_op jit(solution)/shard_map/convert_element_type | solution.py:125
  334.8 13.9 %fusion.2 = f32[1,2048,512]{2,1,0:T(8,128)} fusion(bf16[1,2048,512]{2,1,0:T(8,128)(2,1)S(1)} %copy-done.9, bf16[4096,2048]{1,0:T(8,128)(2,1)} %bitcast.114, bf16[4096,512]{1,0:T(8,128)(2,1)S(1)} %bitcast.101, f32[]{:T(128)S(6)} %mul_shard_map.3), kind=kOutput, calls=%fused_computation.9 | convolution fusion | flops 8594128896 | bytes 27262980 | tf_op jit(solution)/shard_map/dot_general | solution.py:128
  (87 shorter events, 33.7 us)
Async XLA Ops:
  8.0 109.8 %all-reduce.3.cloned.1.call-start = ((), (), s32[]{:S(2)}) async-start(), calls=%async_computation.3 | async-start | bytes 262144 | tf_op jit(solution)/shard_map/psum | solution.py:80
  10.8 139.0 %all-gather.3.cloned.1.call-start = ((), (), s32[]{:S(2)}) async-start(), calls=%async_computation.5 | async-start | bytes 17825792 | tf_op jit(solution)/shard_map/all_gather | solution.py:79
  12.2 16.8 %collective-permute-start = (bf16[2,64,2048]{2,1,0:T(8,128)(2,1)}, bf16[2,64,2048]{2,1,0:T(8,128)(2,1)S(1)}, u32[]{:S(2)}, u32[]{:S(2)}) collective-permute-start(bf16[2,64,2048]{2,1,0:T(8,128)(2,1)} %fusion.59), channel_id=1, source_target_pairs={{0,1},{1,2},{2,3},{3,0},{4,5},{5,6},{6,7},{7,4},{8,9},{9,10},{10,1... | collective-permute-start | bytes 1572872 | tf_op jit(solution)/shard_map/ppermute | solution.py:18
  14.7 26.9 %collective-permute-start.1 = (bf16[2,64,2048]{2,1,0:T(8,128)(2,1)}, bf16[2,64,2048]{2,1,0:T(8,128)(2,1)S(1)}, u32[]{:S(2)}, u32[]{:S(2)}) collective-permute-start(bf16[2,64,2048]{2,1,0:T(8,128)(2,1)} %fusion.59), channel_id=1, source_target_pairs={{0,2},{1,3},{2,0},{3,1},{4,6},{5,7},{6,4},{7,5},{8,10},{9,11},{10,... | collective-permute-start | bytes 1572872 | tf_op jit(solution)/shard_map/ppermute | solution.py:18
  18.0 24.9 %collective-permute-start.2 = (bf16[2,64,2048]{2,1,0:T(8,128)(2,1)}, bf16[2,64,2048]{2,1,0:T(8,128)(2,1)}, u32[]{:S(2)}, u32[]{:S(2)}) collective-permute-start(bf16[2,64,2048]{2,1,0:T(8,128)(2,1)} %fusion.59), channel_id=1, source_target_pairs={{0,3},{1,0},{2,1},{3,2},{4,7},{5,4},{6,5},{7,6},{8,11},{9,8},{10,9... | collective-permute-start | bytes 1572872 | tf_op jit(solution)/shard_map/ppermute | solution.py:18
  18.7 39.3 %collective-permute-start.3 = (bf16[2048,512]{1,0:T(8,128)(2,1)}, bf16[2048,512]{1,0:T(8,128)(2,1)}, u32[]{:S(2)}, u32[]{:S(2)}) collective-permute-start(bf16[2048,512]{1,0:T(8,128)(2,1)} %bitcast.115), channel_id=1, source_target_pairs={{0,64},{64,0},{1,65},{65,1},{2,66},{66,2},{3,67},{67,3},{4,68},{68... | collective-permute-start | bytes 6291464 | tf_op jit(solution)/shard_map/ppermute | solution.py:9
  20.3 10.0 %copy-start.3 = (bf16[1,2,64,2048]{3,2,0,1:T(8,128)(2,1)}, bf16[1,2,64,2048]{3,2,0,1:T(8,128)(2,1)S(1)}, u32[]{:S(2)}) copy-start(bf16[1,2,64,2048]{3,2,0,1:T(8,128)(2,1)S(1)} %fusion.58) | copy-start | bytes 1572868
  29.0 13.9 %copy-start.5 = (bf16[2,64,2048]{2,1,0:T(8,128)(2,1)}, bf16[2,64,2048]{2,1,0:T(8,128)(2,1)S(1)}, u32[]{:S(2)}) copy-start(bf16[2,64,2048]{2,1,0:T(8,128)(2,1)S(1)} %collective-permute-done) | copy-start | bytes 1572868
  51.2 57.4 %all-to-all-start = ((bf16[16,128,512]{2,1,0:T(8,128)(2,1)}), bf16[16,128,512]{2,1,0:T(8,128)(2,1)S(1)}, u32[]{:S(2)}, u32[]{:S(2)}) async-start(bf16[16,128,512]{2,1,0:T(8,128)(2,1)} %bitcast.99), calls=%async_computation | async-start | bytes 4194304 | tf_op jit(solution)/shard_map/all_to_all | solution.py:51
  57.9 179.4 %reduce-scatter.2.cloned.1.call-start = ((), (), s32[]{:S(2)}) async-start(), calls=%async_computation.4 | async-start | bytes 8912896 | tf_op jit(solution)/shard_map/reduce_scatter | solution.py:92
  149.9 93.7 %copy-start.10 = (f32[2,2,64,64]{3,2,1,0:T(8,128)S(1)}, f32[2,2,64,64]{3,2,1,0:T(8,128)}, u32[]{:S(2)}) copy-start(f32[2,2,64,64]{3,2,1,0:T(8,128)} %all-reduce.3.cloned.1.call-done) | copy-start | bytes 196612
  149.9 97.7 %copy-start.4 = (bf16[1,2,64,2048]{3,2,0,1:T(8,128)(2,1)S(1)}, bf16[1,2,64,2048]{3,2,0,1:T(8,128)(2,1)}, u32[]{:S(2)}) copy-start(bf16[1,2,64,2048]{3,2,0,1:T(8,128)(2,1)} %copy-done.3) | copy-start | bytes 1572868
  149.9 97.7 %copy-start.6 = (bf16[2,64,2048]{2,1,0:T(8,128)(2,1)S(1)}, bf16[2,64,2048]{2,1,0:T(8,128)(2,1)}, u32[]{:S(2)}) copy-start(bf16[2,64,2048]{2,1,0:T(8,128)(2,1)} %copy-done.5) | copy-start | bytes 1572868
  149.9 97.7 %copy-start.8 = (bf16[2,64,2048]{2,1,0:T(8,128)(2,1)S(1)}, bf16[2,64,2048]{2,1,0:T(8,128)(2,1)}, u32[]{:S(2)}) copy-start(bf16[2,64,2048]{2,1,0:T(8,128)(2,1)} %copy-done.7) | copy-start | bytes 1572868
  238.5 12.7 %collective-permute-start.5 = (bf16[2,64,2048]{2,1,0:T(8,128)(2,1)S(1)}, bf16[2,64,2048]{2,1,0:T(8,128)(2,1)}, u32[]{:S(2)}, u32[]{:S(2)}) collective-permute-start(bf16[2,64,2048]{2,1,0:T(8,128)(2,1)S(1)} %bitcast.102), channel_id=1, source_target_pairs={{0,1},{1,2},{2,3},{3,0},{4,5},{5,6},{6,7},{7,4},{8,9},{9,10},{10,1... | collective-permute-start | bytes 1572872 | tf_op jit(solution)/shard_map/ppermute | solution.py:18
  239.9 23.7 %collective-permute-start.6 = (bf16[2,64,2048]{2,1,0:T(8,128)(2,1)S(1)}, bf16[2,64,2048]{2,1,0:T(8,128)(2,1)}, u32[]{:S(2)}, u32[]{:S(2)}) collective-permute-start(bf16[2,64,2048]{2,1,0:T(8,128)(2,1)S(1)} %bitcast.103), channel_id=1, source_target_pairs={{0,2},{1,3},{2,0},{3,1},{4,6},{5,7},{6,4},{7,5},{8,10},{9,11},{10,... | collective-permute-start | bytes 1572872 | tf_op jit(solution)/shard_map/ppermute | solution.py:18
  242.4 22.1 %collective-permute-start.7 = (bf16[2,64,2048]{2,1,0:T(8,128)(2,1)S(1)}, bf16[2,64,2048]{2,1,0:T(8,128)(2,1)}, u32[]{:S(2)}, u32[]{:S(2)}) collective-permute-start(bf16[2,64,2048]{2,1,0:T(8,128)(2,1)S(1)} %bitcast.104), channel_id=1, source_target_pairs={{0,3},{1,0},{2,1},{3,2},{4,7},{5,4},{6,5},{7,6},{8,11},{9,8},{10,9... | collective-permute-start | bytes 1572872 | tf_op jit(solution)/shard_map/ppermute | solution.py:18
  243.5 4.0 %collective-permute-start.8 = (f32[2,2,64,64]{3,2,1,0:T(8,128)S(1)}, f32[2,2,64,64]{3,2,1,0:T(8,128)S(1)}, u32[]{:S(2)}, u32[]{:S(2)}) collective-permute-start(f32[2,2,64,64]{3,2,1,0:T(8,128)S(1)} %copy-done.10), channel_id=1, source_target_pairs={{0,64},{64,0},{1,65},{65,1},{2,66},{66,2},{3,67},{67,3},{4,68},{68... | collective-permute-start | bytes 196616 | tf_op jit(solution)/shard_map/ppermute | solution.py:9
  279.9 34.7 %all-to-all-start.1 = ((bf16[16,144,512]{2,1,0:T(8,128)(2,1)}), bf16[16,144,512]{2,1,0:T(8,128)(2,1)S(1)}, u32[]{:S(2)}, u32[]{:S(2)}) async-start(bf16[16,144,512]{2,1,0:T(8,128)(2,1)} %pad_maximum_fusion), calls=%async_computation.2 | async-start | bytes 4718592 | tf_op jit(solution)/shard_map/all_to_all | solution.py:51
  284.6 42.5 %collective-permute-start.4 = (bf16[2048,512]{1,0:T(8,128)(2,1)}, bf16[2048,512]{1,0:T(8,128)(2,1)}, u32[]{:S(2)}, u32[]{:S(2)}) collective-permute-start(bf16[2048,512]{1,0:T(8,128)(2,1)} %bitcast.97), channel_id=1, source_target_pairs={{0,64},{64,0},{1,65},{65,1},{2,66},{66,2},{3,67},{67,3},{4,68},{68... | collective-permute-start | bytes 6291464 | tf_op jit(solution)/shard_map/ppermute | solution.py:9
  316.1 11.0 %collective-permute-start.9 = (bf16[2048,512]{1,0:T(8,128)(2,1)}, bf16[2048,512]{1,0:T(8,128)(2,1)}, u32[]{:S(2)}, u32[]{:S(2)}) collective-permute-start(bf16[2048,512]{1,0:T(8,128)(2,1)} %bitcast.36), channel_id=1, source_target_pairs={{0,64},{64,0},{1,65},{65,1},{2,66},{66,2},{3,67},{67,3},{4,68},{68... | collective-permute-start | bytes 6291464 | tf_op jit(solution)/shard_map/ppermute | solution.py:9
  320.9 4.1 %collective-permute-start.11 = (f32[2]{0:T(128)S(1)}, f32[2]{0:T(128)S(1)}, u32[]{:S(2)}, u32[]{:S(2)}) collective-permute-start(f32[2]{0:T(128)S(1)} %get-tuple-element.22), channel_id=1, source_target_pairs={{0,64},{64,0},{1,65},{65,1},{2,66},{66,2},{3,67},{67,3},{4,68},{68... | collective-permute-start | bytes 32 | tf_op jit(solution)/shard_map/ppermute | solution.py:9
  325.7 1.3 collective-permute-start.10
  334.8 13.9 %copy-start.1 = (bf16[2,2,64,2048]{3,2,1,0:T(8,128)(2,1)S(1)}, bf16[2,2,64,2048]{3,2,1,0:T(8,128)(2,1)}, u32[]{:S(2)}) copy-start(bf16[2,2,64,2048]{3,2,1,0:T(8,128)(2,1)} %param.11) | copy-start | bytes 3145732
  (4 other events, 22.9 us)
Sparse Core Ops, SparseCore 0:
  11.1 56.3 all-reduce.2
Sparse Core Ops, SparseCore 1:
  13.4 136.4 all-gather.2
  153.1 84.2 reduce-scatter.1

commit v8 on v7

--- a/solution.py
+++ b/solution.py
@@ -88,7 +88,7 @@
     terms = lax.dot_general(
         last_blocks, last_weights, (((1,), (1,)), ((), ())), preferred_element_type=jnp.float32
     ).astype(jnp.bfloat16)
-    terms, gathered_inputs, input_grams = lax.optimization_barrier((terms, gathered_inputs, input_grams))
+    terms, input_grams = lax.optimization_barrier((terms, input_grams))
     summed = lax.psum_scatter(terms, "dp", scatter_dimension=0, tiled=True).astype(jnp.float32)
     other_input_grams = swapped(input_grams, "pipe")
     renewed = (own_cotangent.reshape(token_count, width_part).astype(jnp.float32) + summed).astype(

time: 358 us -> 355 us (level)
  local copies, waits for them, and re-layouts: 18.1 us -> 28.2 us
  waiting for transfers between devices: 237 us -> 227 us
    all_gather x1, waiting for transfers between devices: 32 us -> 16.3 us  [local(): gathered_inputs = lax.all_gather(local_inputs, 'dp', axis=1, tiled=True)]
    unnamed x24 -> x26, local copies, waits for them, and re-layouts: 0.2 us -> 10.8 us
    psum x1, waiting for transfers between devices: 0.01 us -> 6.95 us  [local(): input_grams = lax.psum(token_grams(local_inputs), 'tensor')]
  transfers between devices with their start and end apart: 17 -> 17, of which waited for: 12 -> 13; matrix products, arithmetic and copies ran while one was open for 8% -> 16% of each run, Pallas kernels for 0% -> 0%
where the time goes in v8:
time: 355 us
  waiting for transfers between devices  227 us (64%)
  starting transfers between devices  33.3 us (9%)
  matrix products  31.5 us (9%)
  local copies, waits for them, and re-layouts  28.2 us (8%)
  other arithmetic  19.7 us (6%)
  between operations  14.7 us (4%)
    reduce_scatter x1, waiting for transfers between devices, local(): lax.psum_scatter(terms, 'dp', scatter_dimension=0, tiled=True)  89.3 us
    all_to_all x2, waiting for transfers between devices, column_blocks(): lax.all_to_all(chunks, 'dp', split_axis=0, concat_axis=1, tiled=True)  79 us
    ppermute x6, waiting for transfers between devices, ring_pieces(): lax.ppermute(values, axis, [(source, (source + offset) % count) for sourc...  32.5 us
    all_gather x1, waiting for transfers between devices, local(): gathered_inputs = lax.all_gather(local_inputs, 'dp', axis=1, tiled=True)  16.3 us
    dot_general x1, matrix products, local(): lax.dot_general(flat_inputs, flat_grads, (((0,), (0,)), ((), ())), prefer...  15 us
    ppermute x6, starting transfers between devices, ring_pieces(): lax.ppermute(values, axis, [(source, (source + offset) % count) for sourc...  11.5 us
    all_to_all x2, starting transfers between devices, column_blocks(): lax.all_to_all(chunks, 'dp', split_axis=0, concat_axis=1, tiled=True)  11.4 us
    unnamed x26, local copies, waits for them, and re-layouts  10.8 us
  transfers between devices with their start and end apart: 17, of which 13 were waited for; matrix products, arithmetic and copies ran while one was open for 16% of the time, Pallas kernels for 0%

profile of v8, /device:TPU:1, one launch (start us, length us, event | category | flops | bytes accessed | tf_op | source)
XLA Modules:
  0.0 354.5 jit_solution(970468313639926576)
XLA Ops:
  9.2 2.5 collective-permute-start
  11.7 3.3 collective-permute-start.1
  18.6 7.0 %collective-permute-done = bf16[2,64,2048]{2,1,0:T(8,128)(2,1)S(1)} collective-permute-done((bf16[2,64,2048]{2,1,0:T(8,128)(2,1)}, bf16[2,64,2048]{2,1,0:T(8,128)(2,1)S(1)}, u32[]{:S(2)}, u32[]{:S(2)}) %collective-permute-start) | collective-permute-done | bytes 524320 | tf_op jit(solution)/shard_map/ppermute | solution.py:18
  26.9 10.9 %collective-permute-done.1 = bf16[2,64,2048]{2,1,0:T(8,128)(2,1)S(1)} collective-permute-done((bf16[2,64,2048]{2,1,0:T(8,128)(2,1)}, bf16[2,64,2048]{2,1,0:T(8,128)(2,1)S(1)}, u32[]{:S(2)}, u32[]{:S(2)}) %collective-permute-start.1) | collective-permute-done | bytes 524320 | tf_op jit(solution)/shard_map/ppermute | solution.py:18
  44.2 3.2 broadcast_select_fusion.1
  47.4 6.8 %all-to-all-start = ((bf16[16,128,512]{2,1,0:T(8,128)(2,1)}), bf16[16,128,512]{2,1,0:T(8,128)(2,1)S(1)}, u32[]{:S(2)}, u32[]{:S(2)}) async-start(bf16[16,128,512]{2,1,0:T(8,128)(2,1)} %bitcast.100), calls=%async_computation | async-start | bytes 4194304 | tf_op jit(solution)/shard_map/all_to_all | solution.py:51
  54.2 2.6 fusion.29
  56.9 25.2 %all-to-all-done = bf16[16,128,512]{2,1,0:T(8,128)(2,1)S(1)} async-done(((bf16[16,128,512]{2,1,0:T(8,128)(2,1)}), bf16[16,128,512]{2,1,0:T(8,128)(2,1)S(1)}, u32[]{:S(2)}, u32[]{:S(2)}) %all-to-all-start) | async-done | bytes 2097184 | tf_op jit(solution)/shard_map/all_to_all | solution.py:51
  82.2 9.1 %convolution_convert_fusion = bf16[2048,2048]{1,0:T(8,128)(2,1)} fusion(bf16[2048,512]{1,0:T(8,128)(2,1)S(1)} %bitcast.97, bf16[2048,512]{1,0:T(8,128)(2,1)} %collective-permute-done.4, pred[]{:T(512)S(6)} %eq.6, bf16[1,2048,512]{2,1,0:T(8,128)(2,1)} %param.9), kind=kOutput, calls=%fused_computation.3 | convolution fusion | flops 4300210176 | bytes 14680065 | tf_op jit(solution)/shard_map/dot_general | solution.py:88
  91.3 6.9 %all-reduce.3.cloned.1.call-done = f32[2,2,64,64]{3,2,1,0:T(8,128)} async-done(((f32[2,2,64,64]{3,2,1,0:T(8,128)}), f32[2,2,64,64]{3,2,1,0:T(8,128)}) %all-reduce.3.cloned.1.call-update) | async-done | bytes 65552 | tf_op jit(solution)/shard_map/psum | solution.py:80
  99.1 89.3 %reduce-scatter.2.cloned.1.call-done = bf16[128,2048]{1,0:T(8,128)(2,1)} async-done(((bf16[2048,2048]{1,0:T(8,128)(2,1)}), bf16[128,2048]{1,0:T(8,128)(2,1)}) %reduce-scatter.2.cloned.1.call-update) | async-done | bytes 524304 | tf_op jit(solution)/shard_map/reduce_scatter | solution.py:92
  190.9 2.6 collective-permute-start.6
  194.6 2.9 collective-permute-start.8
  202.4 12.3 %collective-permute-done.6 = bf16[2,64,2048]{2,1,0:T(8,128)(2,1)} collective-permute-done((bf16[2,64,2048]{2,1,0:T(8,128)(2,1)S(1)}, bf16[2,64,2048]{2,1,0:T(8,128)(2,1)}, u32[]{:S(2)}, u32[]{:S(2)}) %collective-permute-start.6) | collective-permute-done | bytes 524320 | tf_op jit(solution)/shard_map/ppermute | solution.py:18
  215.6 2.7 fusion.32
  229.2 4.6 %all-to-all-start.1 = ((bf16[16,144,512]{2,1,0:T(8,128)(2,1)}), bf16[16,144,512]{2,1,0:T(8,128)(2,1)S(1)}, u32[]{:S(2)}, u32[]{:S(2)}) async-start(bf16[16,144,512]{2,1,0:T(8,128)(2,1)} %pad_maximum_fusion), calls=%async_computation.2 | async-start | bytes 4718592 | tf_op jit(solution)/shard_map/all_to_all | solution.py:51
  233.9 2.5 collective-permute-start.3
  236.4 53.7 %all-to-all-done.1 = bf16[16,144,512]{2,1,0:T(8,128)(2,1)S(1)} async-done(((bf16[16,144,512]{2,1,0:T(8,128)(2,1)}), bf16[16,144,512]{2,1,0:T(8,128)(2,1)S(1)}, u32[]{:S(2)}, u32[]{:S(2)}) %all-to-all-start.1) | async-done | bytes 2359328 | tf_op jit(solution)/shard_map/all_to_all | solution.py:51
  291.6 3.1 collective-permute-start.9
  294.8 4.0 %copy.101 = bf16[1,2048,512]{1,2,0:T(8,128)(2,1)} copy(bf16[1,2048,512]{2,1,0:T(8,128)(2,1)} %param.13) | data formatting | bytes 4194304 | tf_op args[4]
  302.0 9.3 %multiply_convert_fusion = bf16[2,16,2,64,512]{4,3,2,1,0:T(8,128)(2,1)} fusion(bf16[1,16,2,64,512]{4,3,2,1,0:T(8,128)(2,1)} %bitcast.99, bf16[1,16,2,64,512]{4,3,2,1,0:T(8,128)(2,1)} %bitcast.4, bf16[1,16,2,64,512]{4,3,2,1,0:T(8,128)(2,1)} %bitcast.36, bf16[1,16,2,64,512]{4,3,2,1,0:T(8,128)(2,1)} %bitcast.35, f32[2,16,2]{2,1,0:T(8,128)S(1)} %copy.100, pred[]{:T(512)S(6)} %eq.6), kind=kLoop, calls=%fused_computation.2 | loop fusion | flops 20971520 | bytes 12583169 | tf_op jit(solution)/shard_map/convert_element_type | solution.py:125
  311.2 16.3 %all-gather.3.cloned.1.call-done = bf16[1,2,32,64,2048]{4,3,2,1,0:T(8,128)(2,1)} async-done(((bf16[1,2,2,64,2048]{4,3,2,1,0:T(8,128)(2,1)}), bf16[1,2,32,64,2048]{4,3,2,1,0:T(8,128)(2,1)}) %all-gather.3.cloned.1.call-update) | async-done | bytes 16777232 | tf_op jit(solution)/shard_map/all_gather | solution.py:79
  327.6 15.0 %fusion.2 = f32[1,2048,512]{1,2,0:T(8,128)} fusion(bf16[1,2048,512]{1,2,0:T(8,128)(2,1)S(1)} %copy-done.3, bf16[4096,512]{1,0:T(8,128)(2,1)} %bitcast.102, bf16[4096,2048]{1,0:T(8,128)(2,1)} %bitcast.115, f32[]{:T(128)S(6)} %mul_shard_map.3), kind=kOutput, calls=%fused_computation.9 | convolution fusion | flops 8594128896 | bytes 27262980 | tf_op jit(solution)/shard_map/dot_general | solution.py:128
  342.5 5.4 %copy.102 = f32[1,2048,512]{2,1,0:T(8,128)} copy(f32[1,2048,512]{1,2,0:T(8,128)} %fusion.2) | data formatting | bytes 8388608
  (89 shorter events, 38.5 us)
Async XLA Ops:
  9.2 16.4 %collective-permute-start = (bf16[2,64,2048]{2,1,0:T(8,128)(2,1)}, bf16[2,64,2048]{2,1,0:T(8,128)(2,1)S(1)}, u32[]{:S(2)}, u32[]{:S(2)}) collective-permute-start(bf16[2,64,2048]{2,1,0:T(8,128)(2,1)} %fusion.59), channel_id=1, source_target_pairs={{0,1},{1,2},{2,3},{3,0},{4,5},{5,6},{6,7},{7,4},{8,9},{9,10},{10,1... | collective-permute-start | bytes 1572872 | tf_op jit(solution)/shard_map/ppermute | solution.py:18
  11.7 26.1 %collective-permute-start.1 = (bf16[2,64,2048]{2,1,0:T(8,128)(2,1)}, bf16[2,64,2048]{2,1,0:T(8,128)(2,1)S(1)}, u32[]{:S(2)}, u32[]{:S(2)}) collective-permute-start(bf16[2,64,2048]{2,1,0:T(8,128)(2,1)} %fusion.59), channel_id=1, source_target_pairs={{0,2},{1,3},{2,0},{3,1},{4,6},{5,7},{6,4},{7,5},{8,10},{9,11},{10,... | collective-permute-start | bytes 1572872 | tf_op jit(solution)/shard_map/ppermute | solution.py:18
  15.0 24.1 %collective-permute-start.2 = (bf16[2,64,2048]{2,1,0:T(8,128)(2,1)}, bf16[2,64,2048]{2,1,0:T(8,128)(2,1)}, u32[]{:S(2)}, u32[]{:S(2)}) collective-permute-start(bf16[2,64,2048]{2,1,0:T(8,128)(2,1)} %fusion.59), channel_id=1, source_target_pairs={{0,3},{1,0},{2,1},{3,2},{4,7},{5,4},{6,5},{7,6},{8,11},{9,8},{10,9... | collective-permute-start | bytes 1572872 | tf_op jit(solution)/shard_map/ppermute | solution.py:18
  15.7 41.2 %collective-permute-start.4 = (bf16[2048,512]{1,0:T(8,128)(2,1)}, bf16[2048,512]{1,0:T(8,128)(2,1)}, u32[]{:S(2)}, u32[]{:S(2)}) collective-permute-start(bf16[2048,512]{1,0:T(8,128)(2,1)} %bitcast.116), channel_id=1, source_target_pairs={{0,64},{64,0},{1,65},{65,1},{2,66},{66,2},{3,67},{67,3},{4,68},{68... | collective-permute-start | bytes 6291464 | tf_op jit(solution)/shard_map/ppermute | solution.py:9
  17.3 9.6 %copy-start.4 = (bf16[1,2,64,2048]{3,2,0,1:T(8,128)(2,1)}, bf16[1,2,64,2048]{3,2,0,1:T(8,128)(2,1)S(1)}, u32[]{:S(2)}) copy-start(bf16[1,2,64,2048]{3,2,0,1:T(8,128)(2,1)S(1)} %fusion.58) | copy-start | bytes 1572868
  25.6 13.4 %copy-start.6 = (bf16[2,64,2048]{2,1,0:T(8,128)(2,1)}, bf16[2,64,2048]{2,1,0:T(8,128)(2,1)S(1)}, u32[]{:S(2)}) copy-start(bf16[2,64,2048]{2,1,0:T(8,128)(2,1)S(1)} %collective-permute-done) | copy-start | bytes 1572868
  47.4 34.8 %all-to-all-start = ((bf16[16,128,512]{2,1,0:T(8,128)(2,1)}), bf16[16,128,512]{2,1,0:T(8,128)(2,1)S(1)}, u32[]{:S(2)}, u32[]{:S(2)}) async-start(bf16[16,128,512]{2,1,0:T(8,128)(2,1)} %bitcast.100), calls=%async_computation | async-start | bytes 4194304 | tf_op jit(solution)/shard_map/all_to_all | solution.py:51
  54.2 44.1 %all-reduce.3.cloned.1.call-start = ((), (), s32[]{:S(2)}) async-start(), calls=%async_computation.3 | async-start | bytes 262144 | tf_op jit(solution)/shard_map/psum | solution.py:80
  56.9 131.5 %reduce-scatter.2.cloned.1.call-start = ((), (), s32[]{:S(2)}) async-start(), calls=%async_computation.4 | async-start | bytes 8912896 | tf_op jit(solution)/shard_map/reduce_scatter | solution.py:92
  98.3 96.3 %copy-start.10 = (f32[2,2,64,64]{3,2,1,0:T(8,128)S(1)}, f32[2,2,64,64]{3,2,1,0:T(8,128)}, u32[]{:S(2)}) copy-start(f32[2,2,64,64]{3,2,1,0:T(8,128)} %all-reduce.3.cloned.1.call-done) | copy-start | bytes 196612
  98.3 100.2 %copy-start.5 = (bf16[1,2,64,2048]{3,2,0,1:T(8,128)(2,1)S(1)}, bf16[1,2,64,2048]{3,2,0,1:T(8,128)(2,1)}, u32[]{:S(2)}) copy-start(bf16[1,2,64,2048]{3,2,0,1:T(8,128)(2,1)} %copy-done.4) | copy-start | bytes 1572868
  98.3 100.2 %copy-start.7 = (bf16[2,64,2048]{2,1,0:T(8,128)(2,1)S(1)}, bf16[2,64,2048]{2,1,0:T(8,128)(2,1)}, u32[]{:S(2)}) copy-start(bf16[2,64,2048]{2,1,0:T(8,128)(2,1)} %copy-done.6) | copy-start | bytes 1572868
  98.3 100.2 %copy-start.9 = (bf16[2,64,2048]{2,1,0:T(8,128)(2,1)S(1)}, bf16[2,64,2048]{2,1,0:T(8,128)(2,1)}, u32[]{:S(2)}) copy-start(bf16[2,64,2048]{2,1,0:T(8,128)(2,1)} %copy-done.8) | copy-start | bytes 1572868
  98.3 229.3 %all-gather.3.cloned.1.call-start = ((), (), s32[]{:S(2)}) async-start(), calls=%async_computation.5 | async-start | bytes 17825792 | tf_op jit(solution)/shard_map/all_gather | solution.py:79
  189.6 12.8 %collective-permute-start.5 = (bf16[2,64,2048]{2,1,0:T(8,128)(2,1)S(1)}, bf16[2,64,2048]{2,1,0:T(8,128)(2,1)}, u32[]{:S(2)}, u32[]{:S(2)}) collective-permute-start(bf16[2,64,2048]{2,1,0:T(8,128)(2,1)S(1)} %bitcast.103), channel_id=1, source_target_pairs={{0,1},{1,2},{2,3},{3,0},{4,5},{5,6},{6,7},{7,4},{8,9},{9,10},{10,1... | collective-permute-start | bytes 1572872 | tf_op jit(solution)/shard_map/ppermute | solution.py:18
  190.9 23.8 %collective-permute-start.6 = (bf16[2,64,2048]{2,1,0:T(8,128)(2,1)S(1)}, bf16[2,64,2048]{2,1,0:T(8,128)(2,1)}, u32[]{:S(2)}, u32[]{:S(2)}) collective-permute-start(bf16[2,64,2048]{2,1,0:T(8,128)(2,1)S(1)} %bitcast.104), channel_id=1, source_target_pairs={{0,2},{1,3},{2,0},{3,1},{4,6},{5,7},{6,4},{7,5},{8,10},{9,11},{10,... | collective-permute-start | bytes 1572872 | tf_op jit(solution)/shard_map/ppermute | solution.py:18
  193.5 22.1 %collective-permute-start.7 = (bf16[2,64,2048]{2,1,0:T(8,128)(2,1)S(1)}, bf16[2,64,2048]{2,1,0:T(8,128)(2,1)}, u32[]{:S(2)}, u32[]{:S(2)}) collective-permute-start(bf16[2,64,2048]{2,1,0:T(8,128)(2,1)S(1)} %bitcast.105), channel_id=1, source_target_pairs={{0,3},{1,0},{2,1},{3,2},{4,7},{5,4},{6,5},{7,6},{8,11},{9,8},{10,9... | collective-permute-start | bytes 1572872 | tf_op jit(solution)/shard_map/ppermute | solution.py:18
  194.6 3.9 %collective-permute-start.8 = (f32[2,2,64,64]{3,2,1,0:T(8,128)S(1)}, f32[2,2,64,64]{3,2,1,0:T(8,128)S(1)}, u32[]{:S(2)}, u32[]{:S(2)}) collective-permute-start(f32[2,2,64,64]{3,2,1,0:T(8,128)S(1)} %copy-done.10), channel_id=1, source_target_pairs={{0,64},{64,0},{1,65},{65,1},{2,66},{66,2},{3,67},{67,3},{4,68},{68... | collective-permute-start | bytes 196616 | tf_op jit(solution)/shard_map/ppermute | solution.py:9
  229.2 60.9 %all-to-all-start.1 = ((bf16[16,144,512]{2,1,0:T(8,128)(2,1)}), bf16[16,144,512]{2,1,0:T(8,128)(2,1)S(1)}, u32[]{:S(2)}, u32[]{:S(2)}) async-start(bf16[16,144,512]{2,1,0:T(8,128)(2,1)} %pad_maximum_fusion), calls=%async_computation.2 | async-start | bytes 4718592 | tf_op jit(solution)/shard_map/all_to_all | solution.py:51
  233.9 68.1 %collective-permute-start.3 = (bf16[2048,512]{1,0:T(8,128)(2,1)}, bf16[2048,512]{1,0:T(8,128)(2,1)}, u32[]{:S(2)}, u32[]{:S(2)}) collective-permute-start(bf16[2048,512]{1,0:T(8,128)(2,1)} %bitcast.98), channel_id=1, source_target_pairs={{0,64},{64,0},{1,65},{65,1},{2,66},{66,2},{3,67},{67,3},{4,68},{68... | collective-permute-start | bytes 6291464 | tf_op jit(solution)/shard_map/ppermute | solution.py:9
  291.6 10.4 %collective-permute-start.9 = (bf16[2048,512]{1,0:T(8,128)(2,1)}, bf16[2048,512]{1,0:T(8,128)(2,1)}, u32[]{:S(2)}, u32[]{:S(2)}) collective-permute-start(bf16[2048,512]{1,0:T(8,128)(2,1)} %bitcast.34), channel_id=1, source_target_pairs={{0,64},{64,0},{1,65},{65,1},{2,66},{66,2},{3,67},{67,3},{4,68},{68... | collective-permute-start | bytes 6291464 | tf_op jit(solution)/shard_map/ppermute | solution.py:9
  298.8 1.2 collective-permute-start.11
  300.6 1.2 collective-permute-start.10
  302.0 25.6 %copy-start.3 = (bf16[1,2048,512]{1,2,0:T(8,128)(2,1)S(1)}, bf16[1,2048,512]{1,2,0:T(8,128)(2,1)}, u32[]{:S(2)}) copy-start(bf16[1,2048,512]{1,2,0:T(8,128)(2,1)} %copy.101) | copy-start | bytes 6291460
  (4 other events, 18.5 us)
Sparse Core Ops, SparseCore 0:
  57.3 40.9 all-reduce.2
  101.7 86.6 reduce-scatter.1
  190.6 136.9 all-gather.2

commit v9 on v8

--- a/solution.py
+++ b/solution.py
@@ -88,8 +88,10 @@
     terms = lax.dot_general(
         last_blocks, last_weights, (((1,), (1,)), ((), ())), preferred_element_type=jnp.float32
     ).astype(jnp.bfloat16)
-    terms, input_grams = lax.optimization_barrier((terms, input_grams))
-    summed = lax.psum_scatter(terms, "dp", scatter_dimension=0, tiled=True).astype(jnp.float32)
+    arrived = lax.all_to_all(
+        terms.reshape(group_count, token_count, width_part), "dp", split_axis=0, concat_axis=0, tiled=True
+    )
+    summed = jnp.sum(arrived.astype(jnp.float32), axis=0)
     other_input_grams = swapped(input_grams, "pipe")
     renewed = (own_cotangent.reshape(token_count, width_part).astype(jnp.float32) + summed).astype(
         jnp.bfloat16

time: 355 us -> 399 us (1.12)
  waiting for transfers between devices: 227 us -> 257 us
  starting transfers between devices: 33.3 us -> 40.8 us
  other arithmetic: 19.7 us -> 23.7 us
    all_to_all x0 -> x1, waiting for transfers between devices: none -> 138 us  [local(): lax.all_to_all(terms.reshape(group_count, token_count, width_part), 'dp',...]
    reduce_scatter x1 -> x0, waiting for transfers between devices: 89.3 us -> none  [local(): lax.psum_scatter(terms, 'dp', scatter_dimension=0, tiled=True)]
    all_gather x1, waiting for transfers between devices: 16.3 us -> 0.01 us  [local(): gathered_inputs = lax.all_gather(local_inputs, 'dp', axis=1, tiled=True)]
    psum x1, waiting for transfers between devices: 6.95 us -> 0.02 us  [local(): input_grams = lax.psum(token_grams(local_inputs), 'tensor')]
    ppermute x6, waiting for transfers between devices: 32.5 us -> 38.1 us  [ring_pieces(): lax.ppermute(values, axis, [(source, (source + offset) % count) for sourc...]
    reduce_sum x0 -> x1, other arithmetic: none -> 5.34 us  [local(): summed = jnp.sum(arrived.astype(jnp.float32), axis=0)]
    all_to_all x0 -> x1, starting transfers between devices: none -> 4.8 us  [local(): lax.all_to_all(terms.reshape(group_count, token_count, width_part), 'dp',...]
    unnamed x26 -> x23, local copies, waits for them, and re-layouts: 10.8 us -> 9.45 us
  transfers between devices with their start and end apart: 17 -> 17, of which waited for: 13 -> 9; matrix products, arithmetic and copies ran while one was open for 16% -> 15% of each run, Pallas kernels for 0% -> 0%
where the time goes in v9:
time: 399 us; the launch traced here: 396 us
  waiting for transfers between devices  257 us (64%)
  starting transfers between devices  40.8 us (10%)
  matrix products  31.6 us (8%)
  local copies, waits for them, and re-layouts  26.8 us (7%)
  other arithmetic  23.7 us (6%)
  between operations  16.5 us (4%)
    all_to_all x1, waiting for transfers between devices, local(): lax.all_to_all(terms.reshape(group_count, token_count, width_part), 'dp',...  138 us
    all_to_all x2, waiting for transfers between devices, column_blocks(): lax.all_to_all(chunks, 'dp', split_axis=0, concat_axis=1, tiled=True)  78.2 us
    ppermute x6, waiting for transfers between devices, ring_pieces(): lax.ppermute(values, axis, [(source, (source + offset) % count) for sourc...  38.1 us
    dot_general x1, matrix products, local(): lax.dot_general(flat_inputs, flat_grads, (((0,), (0,)), ((), ())), prefer...  15 us
    ppermute x6, starting transfers between devices, swapped(): lax.ppermute(value, axis, [(source, count - 1 - source) for source in ran...  12.5 us
    ppermute x6, starting transfers between devices, ring_pieces(): lax.ppermute(values, axis, [(source, (source + offset) % count) for sourc...  11.7 us
    all_to_all x2, starting transfers between devices, column_blocks(): lax.all_to_all(chunks, 'dp', split_axis=0, concat_axis=1, tiled=True)  11.7 us
    another operation x16, local copies, waits for them, and re-layouts, ring_pieces(): stacked = jnp.stack(pieces)  10.4 us
  transfers between devices with their start and end apart: 17, of which 9 were waited for; matrix products, arithmetic and copies ran while one was open for 15% of the time, Pallas kernels for 0%

profile of v9, /device:TPU:1, one launch (start us, length us, event | category | flops | bytes accessed | tf_op | source)
XLA Modules:
  0.0 395.9 jit_solution(9453215195351911873)
XLA Ops:
  8.1 2.7 fusion.28
  14.6 3.3 collective-permute-start.1
  21.6 7.4 %collective-permute-done = bf16[2,64,2048]{2,1,0:T(8,128)(2,1)S(1)} collective-permute-done((bf16[2,64,2048]{2,1,0:T(8,128)(2,1)}, bf16[2,64,2048]{2,1,0:T(8,128)(2,1)S(1)}, u32[]{:S(2)}, u32[]{:S(2)}) %collective-permute-start) | collective-permute-done | bytes 524320 | tf_op jit(solution)/shard_map/ppermute | solution.py:18
  30.2 11.3 %collective-permute-done.1 = bf16[2,64,2048]{2,1,0:T(8,128)(2,1)S(1)} collective-permute-done((bf16[2,64,2048]{2,1,0:T(8,128)(2,1)}, bf16[2,64,2048]{2,1,0:T(8,128)(2,1)S(1)}, u32[]{:S(2)}, u32[]{:S(2)}) %collective-permute-start.1) | collective-permute-done | bytes 524320 | tf_op jit(solution)/shard_map/ppermute | solution.py:18
  48.0 3.2 broadcast_select_fusion.1
  51.2 6.7 %all-to-all-start = ((bf16[16,128,512]{2,1,0:T(8,128)(2,1)}), bf16[16,128,512]{2,1,0:T(8,128)(2,1)S(1)}, u32[]{:S(2)}, u32[]{:S(2)}) async-start(bf16[16,128,512]{2,1,0:T(8,128)(2,1)} %bitcast.92), calls=%async_computation | async-start | bytes 4194304 | tf_op jit(solution)/shard_map/all_to_all | solution.py:51
  57.9 50.7 %all-to-all-done = bf16[16,128,512]{2,1,0:T(8,128)(2,1)S(1)} async-done(((bf16[16,128,512]{2,1,0:T(8,128)(2,1)}), bf16[16,128,512]{2,1,0:T(8,128)(2,1)S(1)}, u32[]{:S(2)}, u32[]{:S(2)}) %all-to-all-start) | async-done | bytes 2097184 | tf_op jit(solution)/shard_map/all_to_all | solution.py:51
  108.7 9.1 %convolution_convert_fusion = bf16[2048,2048]{1,0:T(8,128)(2,1)} fusion(bf16[2048,512]{1,0:T(8,128)(2,1)S(1)} %bitcast.88, bf16[2048,512]{1,0:T(8,128)(2,1)} %collective-permute-done.4, pred[]{:T(512)S(6)} %eq.6, bf16[1,2048,512]{2,1,0:T(8,128)(2,1)} %param.9), kind=kOutput, calls=%fused_computation.4 | convolution fusion | flops 4300210176 | bytes 14680065 | tf_op jit(solution)/shard_map/dot_general | solution.py:88
  117.8 4.8 %all-to-all-start.1 = ((bf16[16,128,2048]{2,1,0:T(8,128)(2,1)}), bf16[16,128,2048]{2,1,0:T(8,128)(2,1)}, u32[]{:S(2)}, u32[]{:S(2)}) async-start(bf16[16,128,2048]{2,1,0:T(8,128)(2,1)} %bitcast.91), calls=%async_computation.1 | async-start | bytes 16777216 | tf_op jit(solution)/shard_map/all_to_all | solution.py:91
  123.3 3.5 collective-permute-start.8
  126.8 137.5 %all-to-all-done.1 = bf16[16,128,2048]{2,1,0:T(8,128)(2,1)} async-done(((bf16[16,128,2048]{2,1,0:T(8,128)(2,1)}), bf16[16,128,2048]{2,1,0:T(8,128)(2,1)}, u32[]{:S(2)}, u32[]{:S(2)}) %all-to-all-start.1) | async-done | bytes 8388640 | tf_op jit(solution)/shard_map/all_to_all | solution.py:91
  264.3 5.3 %convert_reduce_fusion = f32[128,2048]{1,0:T(8,128)S(1)} fusion(bf16[16,128,2048]{2,1,0:T(8,128)(2,1)} %all-to-all-done.1), kind=kLoop, calls=%fused_computation.2 | loop fusion | flops 8126464 | bytes 9437184 | tf_op jit(solution)/shard_map/reduce_sum | solution.py:94
  271.7 3.4 collective-permute-start.6
  277.8 7.2 %collective-permute-done.5 = bf16[2,64,2048]{2,1,0:T(8,128)(2,1)} collective-permute-done((bf16[2,64,2048]{2,1,0:T(8,128)(2,1)S(1)}, bf16[2,64,2048]{2,1,0:T(8,128)(2,1)}, u32[]{:S(2)}, u32[]{:S(2)}) %collective-permute-start.5) | collective-permute-done | bytes 524320 | tf_op jit(solution)/shard_map/ppermute | solution.py:18
  285.0 12.1 %collective-permute-done.6 = bf16[2,64,2048]{2,1,0:T(8,128)(2,1)} collective-permute-done((bf16[2,64,2048]{2,1,0:T(8,128)(2,1)S(1)}, bf16[2,64,2048]{2,1,0:T(8,128)(2,1)}, u32[]{:S(2)}, u32[]{:S(2)}) %collective-permute-start.6) | collective-permute-done | bytes 524320 | tf_op jit(solution)/shard_map/ppermute | solution.py:18
  297.2 2.8 fusion.31
  310.8 5.0 %all-to-all-start.2 = ((bf16[16,144,512]{2,1,0:T(8,128)(2,1)}), bf16[16,144,512]{2,1,0:T(8,128)(2,1)S(1)}, u32[]{:S(2)}, u32[]{:S(2)}) async-start(bf16[16,144,512]{2,1,0:T(8,128)(2,1)} %pad_maximum_fusion), calls=%async_computation.2 | async-start | bytes 4718592 | tf_op jit(solution)/shard_map/all_to_all | solution.py:51
  315.8 2.5 collective-permute-start.3
  318.3 27.5 %all-to-all-done.2 = bf16[16,144,512]{2,1,0:T(8,128)(2,1)S(1)} async-done(((bf16[16,144,512]{2,1,0:T(8,128)(2,1)}), bf16[16,144,512]{2,1,0:T(8,128)(2,1)S(1)}, u32[]{:S(2)}, u32[]{:S(2)}) %all-to-all-start.2) | async-done | bytes 2359328 | tf_op jit(solution)/shard_map/all_to_all | solution.py:51
  347.3 4.8 %collective-permute-start.9 = (bf16[2048,512]{1,0:T(8,128)(2,1)}, bf16[2048,512]{1,0:T(8,128)(2,1)}, u32[]{:S(2)}, u32[]{:S(2)}) collective-permute-start(bf16[2048,512]{1,0:T(8,128)(2,1)} %bitcast.31), channel_id=1, source_target_pairs={{0,64},{64,0},{1,65},{65,1},{2,66},{66,2},{3,67},{67,3},{4,68},{68... | collective-permute-start | bytes 6291464 | tf_op jit(solution)/shard_map/ppermute | solution.py:9
  352.1 4.0 copy.87
  359.3 8.9 %multiply_convert_fusion = bf16[2,16,2,64,512]{4,3,2,1,0:T(8,128)(2,1)} fusion(bf16[1,16,2,64,512]{4,3,2,1,0:T(8,128)(2,1)} %bitcast.90, bf16[1,16,2,64,512]{4,3,2,1,0:T(8,128)(2,1)} %bitcast.4, bf16[1,16,2,64,512]{4,3,2,1,0:T(8,128)(2,1)} %bitcast.33, bf16[1,16,2,64,512]{4,3,2,1,0:T(8,128)(2,1)} %bitcast.32, f32[2,16,2]{2,1,0:T(8,128)S(1)} %copy.86, pred[]{:T(512)S(6)} %eq.6), kind=kLoop, calls=%fused_computation.3 | loop fusion | flops 20971520 | bytes 12583169 | tf_op jit(solution)/shard_map/convert_element_type | solution.py:127
  368.2 15.0 %fusion.2 = f32[1,2048,512]{1,2,0:T(8,128)} fusion(bf16[1,2048,512]{1,2,0:T(8,128)(2,1)S(1)} %copy-done.2, bf16[4096,512]{1,0:T(8,128)(2,1)} %bitcast.94, bf16[4096,2048]{1,0:T(8,128)(2,1)} %bitcast.104, f32[]{:T(128)S(6)} %mul_shard_map.3), kind=kOutput, calls=%fused_computation.10 | convolution fusion | flops 8594128896 | bytes 27262980 | tf_op jit(solution)/shard_map/dot_general | solution.py:130
  383.2 5.3 %copy.88 = f32[1,2048,512]{2,1,0:T(8,128)} copy(f32[1,2048,512]{1,2,0:T(8,128)} %fusion.2) | data formatting | bytes 8388608
  (87 shorter events, 35.5 us)
Async XLA Ops:
  8.0 115.3 %all-reduce.3.cloned.1.call-start = ((), (), s32[]{:S(2)}) async-start(), calls=%async_computation.3 | async-start | bytes 262144 | tf_op jit(solution)/shard_map/psum | solution.py:80
  10.8 357.4 %all-gather.3.cloned.1.call-start = ((), (), s32[]{:S(2)}) async-start(), calls=%async_computation.4 | async-start | bytes 17825792 | tf_op jit(solution)/shard_map/all_gather | solution.py:79
  12.2 16.8 %collective-permute-start = (bf16[2,64,2048]{2,1,0:T(8,128)(2,1)}, bf16[2,64,2048]{2,1,0:T(8,128)(2,1)S(1)}, u32[]{:S(2)}, u32[]{:S(2)}) collective-permute-start(bf16[2,64,2048]{2,1,0:T(8,128)(2,1)} %fusion.57), channel_id=1, source_target_pairs={{0,1},{1,2},{2,3},{3,0},{4,5},{5,6},{6,7},{7,4},{8,9},{9,10},{10,1... | collective-permute-start | bytes 1572872 | tf_op jit(solution)/shard_map/ppermute | solution.py:18
  14.6 26.9 %collective-permute-start.1 = (bf16[2,64,2048]{2,1,0:T(8,128)(2,1)}, bf16[2,64,2048]{2,1,0:T(8,128)(2,1)S(1)}, u32[]{:S(2)}, u32[]{:S(2)}) collective-permute-start(bf16[2,64,2048]{2,1,0:T(8,128)(2,1)} %fusion.57), channel_id=1, source_target_pairs={{0,2},{1,3},{2,0},{3,1},{4,6},{5,7},{6,4},{7,5},{8,10},{9,11},{10,... | collective-permute-start | bytes 1572872 | tf_op jit(solution)/shard_map/ppermute | solution.py:18
  17.9 24.9 %collective-permute-start.2 = (bf16[2,64,2048]{2,1,0:T(8,128)(2,1)}, bf16[2,64,2048]{2,1,0:T(8,128)(2,1)}, u32[]{:S(2)}, u32[]{:S(2)}) collective-permute-start(bf16[2,64,2048]{2,1,0:T(8,128)(2,1)} %fusion.57), channel_id=1, source_target_pairs={{0,3},{1,0},{2,1},{3,2},{4,7},{5,4},{6,5},{7,6},{8,11},{9,8},{10,9... | collective-permute-start | bytes 1572872 | tf_op jit(solution)/shard_map/ppermute | solution.py:18
  18.7 39.2 %collective-permute-start.4 = (bf16[2048,512]{1,0:T(8,128)(2,1)}, bf16[2048,512]{1,0:T(8,128)(2,1)}, u32[]{:S(2)}, u32[]{:S(2)}) collective-permute-start(bf16[2048,512]{1,0:T(8,128)(2,1)} %bitcast.105), channel_id=1, source_target_pairs={{0,64},{64,0},{1,65},{65,1},{2,66},{66,2},{3,67},{67,3},{4,68},{68... | collective-permute-start | bytes 6291464 | tf_op jit(solution)/shard_map/ppermute | solution.py:9
  20.2 10.0 %copy-start.3 = (bf16[1,2,64,2048]{3,2,1,0:T(8,128)(2,1)}, bf16[1,2,64,2048]{3,2,1,0:T(8,128)(2,1)S(1)}, u32[]{:S(2)}) copy-start(bf16[1,2,64,2048]{3,2,1,0:T(8,128)(2,1)S(1)} %constant_dynamic-slice_fusion) | copy-start | bytes 1572868
  29.0 13.9 %copy-start.5 = (bf16[2,64,2048]{2,1,0:T(8,128)(2,1)}, bf16[2,64,2048]{2,1,0:T(8,128)(2,1)S(1)}, u32[]{:S(2)}) copy-start(bf16[2,64,2048]{2,1,0:T(8,128)(2,1)S(1)} %collective-permute-done) | copy-start | bytes 1572868
  51.2 57.5 %all-to-all-start = ((bf16[16,128,512]{2,1,0:T(8,128)(2,1)}), bf16[16,128,512]{2,1,0:T(8,128)(2,1)S(1)}, u32[]{:S(2)}, u32[]{:S(2)}) async-start(bf16[16,128,512]{2,1,0:T(8,128)(2,1)} %bitcast.92), calls=%async_computation | async-start | bytes 4194304 | tf_op jit(solution)/shard_map/all_to_all | solution.py:51
  108.7 9.1 %copy-start = (bf16[16,128,512]{2,1,0:T(8,128)(2,1)}, bf16[16,128,512]{2,1,0:T(8,128)(2,1)S(1)}, u32[]{:S(2)}) copy-start(bf16[16,128,512]{2,1,0:T(8,128)(2,1)S(1)} %all-to-all-done) | copy-start | bytes 6291460
  117.8 146.5 %all-to-all-start.1 = ((bf16[16,128,2048]{2,1,0:T(8,128)(2,1)}), bf16[16,128,2048]{2,1,0:T(8,128)(2,1)}, u32[]{:S(2)}, u32[]{:S(2)}) async-start(bf16[16,128,2048]{2,1,0:T(8,128)(2,1)} %bitcast.91), calls=%async_computation.1 | async-start | bytes 16777216 | tf_op jit(solution)/shard_map/all_to_all | solution.py:91
  123.3 151.8 %collective-permute-start.8 = (f32[2,2,64,64]{3,2,1,0:T(8,128)}, f32[2,2,64,64]{3,2,1,0:T(8,128)S(1)}, u32[]{:S(2)}, u32[]{:S(2)}) collective-permute-start(f32[2,2,64,64]{3,2,1,0:T(8,128)} %all-reduce.3.cloned.1.call-done), channel_id=1, source_target_pairs={{0,64},{64,0},{1,65},{65,1},{2,66},{66,2},{3,67},{67,3},{4,68},{68... | collective-permute-start | bytes 196616 | tf_op jit(solution)/shard_map/ppermute | solution.py:9
  269.7 5.4 %copy-start.4 = (bf16[1,2,64,2048]{3,2,1,0:T(8,128)(2,1)S(1)}, bf16[1,2,64,2048]{3,2,1,0:T(8,128)(2,1)}, u32[]{:S(2)}) copy-start(bf16[1,2,64,2048]{3,2,1,0:T(8,128)(2,1)} %copy-done.3) | copy-start | bytes 1572868
  269.7 5.4 %copy-start.6 = (bf16[2,64,2048]{2,1,0:T(8,128)(2,1)S(1)}, bf16[2,64,2048]{2,1,0:T(8,128)(2,1)}, u32[]{:S(2)}) copy-start(bf16[2,64,2048]{2,1,0:T(8,128)(2,1)} %copy-done.5) | copy-start | bytes 1572868
  269.7 5.4 %copy-start.8 = (bf16[2,64,2048]{2,1,0:T(8,128)(2,1)S(1)}, bf16[2,64,2048]{2,1,0:T(8,128)(2,1)}, u32[]{:S(2)}) copy-start(bf16[2,64,2048]{2,1,0:T(8,128)(2,1)} %copy-done.7) | copy-start | bytes 1572868
  269.9 15.2 %collective-permute-start.5 = (bf16[2,64,2048]{2,1,0:T(8,128)(2,1)S(1)}, bf16[2,64,2048]{2,1,0:T(8,128)(2,1)}, u32[]{:S(2)}, u32[]{:S(2)}) collective-permute-start(bf16[2,64,2048]{2,1,0:T(8,128)(2,1)S(1)} %add_convert_fusion), channel_id=1, source_target_pairs={{0,1},{1,2},{2,3},{3,0},{4,5},{5,6},{6,7},{7,4},{8,9},{9,10},{10,1... | collective-permute-start | bytes 1572872 | tf_op jit(solution)/shard_map/ppermute | solution.py:18
  271.7 25.5 %collective-permute-start.6 = (bf16[2,64,2048]{2,1,0:T(8,128)(2,1)S(1)}, bf16[2,64,2048]{2,1,0:T(8,128)(2,1)}, u32[]{:S(2)}, u32[]{:S(2)}) collective-permute-start(bf16[2,64,2048]{2,1,0:T(8,128)(2,1)S(1)} %add_convert_fusion), channel_id=1, source_target_pairs={{0,2},{1,3},{2,0},{3,1},{4,6},{5,7},{6,4},{7,5},{8,10},{9,11},{10,... | collective-permute-start | bytes 1572872 | tf_op jit(solution)/shard_map/ppermute | solution.py:18
  275.1 22.1 %collective-permute-start.7 = (bf16[2,64,2048]{2,1,0:T(8,128)(2,1)S(1)}, bf16[2,64,2048]{2,1,0:T(8,128)(2,1)}, u32[]{:S(2)}, u32[]{:S(2)}) collective-permute-start(bf16[2,64,2048]{2,1,0:T(8,128)(2,1)S(1)} %add_convert_fusion), channel_id=1, source_target_pairs={{0,3},{1,0},{2,1},{3,2},{4,7},{5,4},{6,5},{7,6},{8,11},{9,8},{10,9... | collective-permute-start | bytes 1572872 | tf_op jit(solution)/shard_map/ppermute | solution.py:18
  310.8 34.9 %all-to-all-start.2 = ((bf16[16,144,512]{2,1,0:T(8,128)(2,1)}), bf16[16,144,512]{2,1,0:T(8,128)(2,1)S(1)}, u32[]{:S(2)}, u32[]{:S(2)}) async-start(bf16[16,144,512]{2,1,0:T(8,128)(2,1)} %pad_maximum_fusion), calls=%async_computation.2 | async-start | bytes 4718592 | tf_op jit(solution)/shard_map/all_to_all | solution.py:51
  315.8 43.5 %collective-permute-start.3 = (bf16[2048,512]{1,0:T(8,128)(2,1)}, bf16[2048,512]{1,0:T(8,128)(2,1)}, u32[]{:S(2)}, u32[]{:S(2)}) collective-permute-start(bf16[2048,512]{1,0:T(8,128)(2,1)} %bitcast.89), channel_id=1, source_target_pairs={{0,64},{64,0},{1,65},{65,1},{2,66},{66,2},{3,67},{67,3},{4,68},{68... | collective-permute-start | bytes 6291464 | tf_op jit(solution)/shard_map/ppermute | solution.py:9
  347.3 12.0 %collective-permute-start.9 = (bf16[2048,512]{1,0:T(8,128)(2,1)}, bf16[2048,512]{1,0:T(8,128)(2,1)}, u32[]{:S(2)}, u32[]{:S(2)}) collective-permute-start(bf16[2048,512]{1,0:T(8,128)(2,1)} %bitcast.31), channel_id=1, source_target_pairs={{0,64},{64,0},{1,65},{65,1},{2,66},{66,2},{3,67},{67,3},{4,68},{68... | collective-permute-start | bytes 6291464 | tf_op jit(solution)/shard_map/ppermute | solution.py:9
  356.1 1.2 collective-permute-start.11
  357.9 1.2 collective-permute-start.10
  359.3 8.9 %copy-start.2 = (bf16[1,2048,512]{1,2,0:T(8,128)(2,1)S(1)}, bf16[1,2048,512]{1,2,0:T(8,128)(2,1)}, u32[]{:S(2)}) copy-start(bf16[1,2048,512]{1,2,0:T(8,128)(2,1)} %copy.87) | copy-start | bytes 6291460
  (3 other events, 11.5 us)
Sparse Core Ops, SparseCore 0:
  11.1 56.3 all-reduce.2
Sparse Core Ops, SparseCore 1:
  13.4 223.0 all-gather.2

commit v10 on v8

--- a/solution.py
+++ b/solution.py
@@ -2,6 +2,9 @@
 import jax.numpy as jnp
 from jax import lax
 from jax.sharding import PartitionSpec as P
+
+
+DATA = ("dy", "dx")
 
 
 def swapped(value, axis):
@@ -48,7 +51,7 @@
         rows = rows.at[: len(parts), :example_count].set(jnp.stack(parts))
         rows = jnp.broadcast_to(rows[None], (pieces * per_piece, extra, column_part))
         chunks = jnp.concatenate([chunks, rows], axis=1)
-    moved = lax.all_to_all(chunks, "dp", split_axis=0, concat_axis=1, tiled=True)
+    moved = lax.all_to_all(chunks, DATA, split_axis=0, concat_axis=1, tiled=True)
     moved = moved.reshape(group_count, token_count + extra, column_part)
     blocks = moved[:, :token_count].reshape(group_count * token_count, column_part)
     if row_scales is None:
@@ -67,7 +70,7 @@
 
 def local(weights, inputs, cotangent, clip_norm, noise):
     section_index = lax.axis_index("pipe")
-    group_count = lax.axis_size("dp")
+    group_count = lax.axis_size("dy") * lax.axis_size("dx")
     weight_block = weights[0]
     local_inputs = inputs[0]
     micro_count, example_count, length_count, width_part = local_inputs.shape
@@ -76,7 +79,9 @@
     full_width = column_part * group_count
     is_last = section_index == 1
 
-    gathered_inputs = lax.all_gather(local_inputs, "dp", axis=1, tiled=True)
+    gathered_inputs = lax.all_gather(
+        lax.all_gather(local_inputs, "dx", axis=1, tiled=True), "dy", axis=1, tiled=True
+    )
     input_grams = lax.psum(token_grams(local_inputs), "tensor")
 
     own_cotangent = lax.dynamic_index_in_dim(cotangent, section_index, 0, keepdims=False)
@@ -89,7 +94,7 @@
         last_blocks, last_weights, (((1,), (1,)), ((), ())), preferred_element_type=jnp.float32
     ).astype(jnp.bfloat16)
     terms, input_grams = lax.optimization_barrier((terms, input_grams))
-    summed = lax.psum_scatter(terms, "dp", scatter_dimension=0, tiled=True).astype(jnp.float32)
+    summed = lax.psum_scatter(terms, DATA, scatter_dimension=0, tiled=True).astype(jnp.float32)
     other_input_grams = swapped(input_grams, "pipe")
     renewed = (own_cotangent.reshape(token_count, width_part).astype(jnp.float32) + summed).astype(
         jnp.bfloat16
@@ -137,12 +142,18 @@
 
 
 def solution(mesh):
+    sizes = dict(zip(mesh.axis_names, mesh.devices.shape))
+    rows = 4 if sizes["dp"] % 4 == 0 else 1
+    split_mesh = jax.sharding.Mesh(
+        mesh.devices.reshape(sizes["pipe"], rows, sizes["dp"] // rows, sizes["tensor"]),
+        ("pipe", "dy", "dx", "tensor"),
+    )
     in_specs = (
-        P("pipe", "tensor", "dp"),
-        P("pipe", None, "dp", None, "tensor"),
-        P(None, "dp", None, "tensor"),
+        P("pipe", "tensor", DATA),
+        P("pipe", None, DATA, None, "tensor"),
+        P(None, DATA, None, "tensor"),
         P(),
-        P("pipe", "tensor", "dp"),
+        P("pipe", "tensor", DATA),
     )
-    out_specs = (P("pipe", "tensor", "dp"), P(None, "dp"))
-    return jax.shard_map(local, mesh=mesh, in_specs=in_specs, out_specs=out_specs, check_vma=False)
+    out_specs = (P("pipe", "tensor", DATA), P(None, DATA))
+    return jax.shard_map(local, mesh=split_mesh, in_specs=in_specs, out_specs=out_specs, check_vma=False)

time: 355 us -> 447 us (1.26)
  waiting for transfers between devices: 227 us -> 315 us
    reduce_scatter x1, waiting for transfers between devices: 89.3 us -> 215 us  [local(): lax.psum_scatter(terms, DATA, scatter_dimension=0, tiled=True)]
    all_gather x1 -> x2, waiting for transfers between devices: 16.3 us -> 0.02 us  [the longest x1 0.02 us: local(): lax.all_gather(local_inputs, 'dx', axis=1, tiled=True)]
    all_to_all x2, waiting for transfers between devices: 79 us -> 62.7 us  [column_blocks(): lax.all_to_all(chunks, DATA, split_axis=0, concat_axis=1, tiled=True)]
    psum x1, waiting for transfers between devices: 6.95 us -> 0.01 us  [local(): input_grams = lax.psum(token_grams(local_inputs), 'tensor')]
  transfers between devices with their start and end apart: 17 -> 18, of which waited for: 13 -> 11; matrix products, arithmetic and copies ran while one was open for 16% -> 12% of each run, Pallas kernels for 0% -> 0%
where the time goes in v10:
time: 447 us; the launch traced here: 444 us
  waiting for transfers between devices  315 us (70%)
  starting transfers between devices  35 us (8%)
  matrix products  31.7 us (7%)
  local copies, waits for them, and re-layouts  27 us (6%)
  other arithmetic  19.3 us (4%)
  between operations  16.4 us (4%)
    reduce_scatter x1, waiting for transfers between devices, local(): lax.psum_scatter(terms, DATA, scatter_dimension=0, tiled=True)  215 us
    all_to_all x2, waiting for transfers between devices, column_blocks(): lax.all_to_all(chunks, DATA, split_axis=0, concat_axis=1, tiled=True)  62.7 us
    ppermute x6, waiting for transfers between devices, ring_pieces(): lax.ppermute(values, axis, [(source, (source + offset) % count) for sourc...  33.2 us
    dot_general x1, matrix products, local(): lax.dot_general(flat_inputs, flat_grads, (((0,), (0,)), ((), ())), prefer...  15.1 us
    ppermute x6, starting transfers between devices, swapped(): lax.ppermute(value, axis, [(source, count - 1 - source) for source in ran...  12 us
    ppermute x6, starting transfers between devices, ring_pieces(): lax.ppermute(values, axis, [(source, (source + offset) % count) for sourc...  11.5 us
    all_to_all x2, starting transfers between devices, column_blocks(): lax.all_to_all(chunks, DATA, split_axis=0, concat_axis=1, tiled=True)  11.3 us
    another operation x16, local copies, waits for them, and re-layouts, ring_pieces(): stacked = jnp.stack(pieces)  10.4 us
  transfers between devices with their start and end apart: 18, of which 11 were waited for; matrix products, arithmetic and copies ran while one was open for 12% of the time, Pallas kernels for 0%

profile of v10, /device:TPU:1, one launch (start us, length us, event | category | flops | bytes accessed | tf_op | source)
XLA Modules:
  0.0 444.3 jit_solution(1024902779790389394)
XLA Ops:
  8.1 2.7 fusion.29
  12.2 2.5 collective-permute-start
  14.7 3.3 collective-permute-start.1
  21.7 7.4 %collective-permute-done = bf16[2,64,2048]{2,1,0:T(8,128)(2,1)S(1)} collective-permute-done((bf16[2,64,2048]{2,1,0:T(8,128)(2,1)}, bf16[2,64,2048]{2,1,0:T(8,128)(2,1)S(1)}, u32[]{:S(2)}, u32[]{:S(2)}) %collective-permute-start) | collective-permute-done | bytes 524320 | tf_op jit(solution)/shard_map/ppermute | solution.py:21
  30.3 11.3 %collective-permute-done.1 = bf16[2,64,2048]{2,1,0:T(8,128)(2,1)S(1)} collective-permute-done((bf16[2,64,2048]{2,1,0:T(8,128)(2,1)}, bf16[2,64,2048]{2,1,0:T(8,128)(2,1)S(1)}, u32[]{:S(2)}, u32[]{:S(2)}) %collective-permute-start.1) | collective-permute-done | bytes 524320 | tf_op jit(solution)/shard_map/ppermute | solution.py:21
  46.1 2.0 gather_fusion
  48.1 3.2 broadcast_select_fusion.1
  51.3 6.7 %all-to-all-start = ((bf16[16,128,512]{2,1,0:T(8,128)(2,1)}), bf16[16,128,512]{2,1,0:T(8,128)(2,1)S(1)}, u32[]{:S(2)}, u32[]{:S(2)}) async-start(bf16[16,128,512]{2,1,0:T(8,128)(2,1)} %bitcast.100), calls=%async_computation | async-start | bytes 4194304 | tf_op jit(solution)/shard_map/all_to_all | solution.py:54
  58.0 35.2 %all-to-all-done = bf16[16,128,512]{2,1,0:T(8,128)(2,1)S(1)} async-done(((bf16[16,128,512]{2,1,0:T(8,128)(2,1)}), bf16[16,128,512]{2,1,0:T(8,128)(2,1)S(1)}, u32[]{:S(2)}, u32[]{:S(2)}) %all-to-all-start) | async-done | bytes 2097184 | tf_op jit(solution)/shard_map/all_to_all | solution.py:54
  93.3 9.2 %convolution_convert_fusion = bf16[2048,2048]{1,0:T(8,128)(2,1)} fusion(bf16[2048,512]{1,0:T(8,128)(2,1)S(1)} %bitcast.97, bf16[2048,512]{1,0:T(8,128)(2,1)} %collective-permute-done.4, pred[]{:T(512)S(6)} %eq.6, bf16[1,2048,512]{2,1,0:T(8,128)(2,1)} %param.9), kind=kOutput, calls=%fused_computation.3 | convolution fusion | flops 4300210176 | bytes 14680065 | tf_op jit(solution)/shard_map/dot_general | solution.py:93
  103.1 215.4 %reduce-scatter.2.cloned.1.call-done = bf16[128,2048]{1,0:T(8,128)(2,1)} async-done(((bf16[2048,2048]{1,0:T(8,128)(2,1)}), bf16[128,2048]{1,0:T(8,128)(2,1)}) %reduce-scatter.2.cloned.1.call-update) | async-done | bytes 524304 | tf_op jit(solution)/shard_map/reduce_scatter | solution.py:97
  321.1 2.6 collective-permute-start.6
  324.8 3.0 collective-permute-start.8
  332.5 12.5 %collective-permute-done.6 = bf16[2,64,2048]{2,1,0:T(8,128)(2,1)} collective-permute-done((bf16[2,64,2048]{2,1,0:T(8,128)(2,1)S(1)}, bf16[2,64,2048]{2,1,0:T(8,128)(2,1)}, u32[]{:S(2)}, u32[]{:S(2)}) %collective-permute-start.6) | collective-permute-done | bytes 524320 | tf_op jit(solution)/shard_map/ppermute | solution.py:21
  345.7 2.8 fusion.32
  355.2 2.3 gather_fusion.1
  359.4 4.7 %all-to-all-start.1 = ((bf16[16,144,512]{2,1,0:T(8,128)(2,1)}), bf16[16,144,512]{2,1,0:T(8,128)(2,1)S(1)}, u32[]{:S(2)}, u32[]{:S(2)}) async-start(bf16[16,144,512]{2,1,0:T(8,128)(2,1)} %pad_maximum_fusion), calls=%async_computation.2 | async-start | bytes 4718592 | tf_op jit(solution)/shard_map/all_to_all | solution.py:54
  364.1 2.5 collective-permute-start.3
  366.6 27.5 %all-to-all-done.1 = bf16[16,144,512]{2,1,0:T(8,128)(2,1)S(1)} async-done(((bf16[16,144,512]{2,1,0:T(8,128)(2,1)}), bf16[16,144,512]{2,1,0:T(8,128)(2,1)S(1)}, u32[]{:S(2)}, u32[]{:S(2)}) %all-to-all-start.1) | async-done | bytes 2359328 | tf_op jit(solution)/shard_map/all_to_all | solution.py:54
  395.6 4.8 %collective-permute-start.9 = (bf16[2048,512]{1,0:T(8,128)(2,1)}, bf16[2048,512]{1,0:T(8,128)(2,1)}, u32[]{:S(2)}, u32[]{:S(2)}) collective-permute-start(bf16[2048,512]{1,0:T(8,128)(2,1)} %bitcast.34), channel_id=1, source_target_pairs={{0,64},{64,0},{1,65},{65,1},{2,66},{66,2},{3,67},{67,3},{4,68},{68... | collective-permute-start | bytes 6291464 | tf_op jit(solution)/shard_map/ppermute | solution.py:12
  400.4 4.0 copy.101
  407.6 8.8 %multiply_convert_fusion = bf16[2,16,2,64,512]{4,3,2,1,0:T(8,128)(2,1)} fusion(bf16[1,16,2,64,512]{4,3,2,1,0:T(8,128)(2,1)} %bitcast.99, bf16[1,16,2,64,512]{4,3,2,1,0:T(8,128)(2,1)} %bitcast.4, bf16[1,16,2,64,512]{4,3,2,1,0:T(8,128)(2,1)} %bitcast.36, bf16[1,16,2,64,512]{4,3,2,1,0:T(8,128)(2,1)} %bitcast.35, f32[2,16,2]{2,1,0:T(8,128)S(1)} %copy.100, pred[]{:T(512)S(6)} %eq.6), kind=kLoop, calls=%fused_computation.2 | loop fusion | flops 20971520 | bytes 12583169 | tf_op jit(solution)/shard_map/convert_element_type | solution.py:130
  416.4 15.1 %fusion.2 = f32[1,2048,512]{1,2,0:T(8,128)} fusion(bf16[1,2048,512]{1,2,0:T(8,128)(2,1)S(1)} %copy-done.3, bf16[4096,512]{1,0:T(8,128)(2,1)} %bitcast.102, bf16[4096,2048]{1,0:T(8,128)(2,1)} %bitcast.115, f32[]{:T(128)S(6)} %mul_shard_map.3), kind=kOutput, calls=%fused_computation.9 | convolution fusion | flops 8594128896 | bytes 27262980 | tf_op jit(solution)/shard_map/dot_general | solution.py:133
  431.5 5.4 %copy.102 = f32[1,2048,512]{2,1,0:T(8,128)} copy(f32[1,2048,512]{1,2,0:T(8,128)} %fusion.2) | data formatting | bytes 8388608
  (92 shorter events, 33.3 us)
Async XLA Ops:
  8.0 94.4 %all-reduce.3.cloned.1.call-start = ((), (), s32[]{:S(2)}) async-start(), calls=%async_computation.3 | async-start | bytes 262144 | tf_op jit(solution)/shard_map/psum | solution.py:85
  10.8 91.8 %all-gather.5.cloned.1.call-start = ((), (), s32[]{:S(2)}) async-start(), calls=%async_computation.5 | async-start | bytes 5242880 | tf_op jit(solution)/shard_map/all_gather | solution.py:83
  12.2 16.8 %collective-permute-start = (bf16[2,64,2048]{2,1,0:T(8,128)(2,1)}, bf16[2,64,2048]{2,1,0:T(8,128)(2,1)S(1)}, u32[]{:S(2)}, u32[]{:S(2)}) collective-permute-start(bf16[2,64,2048]{2,1,0:T(8,128)(2,1)} %fusion.59), channel_id=1, source_target_pairs={{0,1},{1,2},{2,3},{3,0},{4,5},{5,6},{6,7},{7,4},{8,9},{9,10},{10,1... | collective-permute-start | bytes 1572872 | tf_op jit(solution)/shard_map/ppermute | solution.py:21
  14.7 26.9 %collective-permute-start.1 = (bf16[2,64,2048]{2,1,0:T(8,128)(2,1)}, bf16[2,64,2048]{2,1,0:T(8,128)(2,1)S(1)}, u32[]{:S(2)}, u32[]{:S(2)}) collective-permute-start(bf16[2,64,2048]{2,1,0:T(8,128)(2,1)} %fusion.59), channel_id=1, source_target_pairs={{0,2},{1,3},{2,0},{3,1},{4,6},{5,7},{6,4},{7,5},{8,10},{9,11},{10,... | collective-permute-start | bytes 1572872 | tf_op jit(solution)/shard_map/ppermute | solution.py:21
  18.0 24.9 %collective-permute-start.2 = (bf16[2,64,2048]{2,1,0:T(8,128)(2,1)}, bf16[2,64,2048]{2,1,0:T(8,128)(2,1)}, u32[]{:S(2)}, u32[]{:S(2)}) collective-permute-start(bf16[2,64,2048]{2,1,0:T(8,128)(2,1)} %fusion.59), channel_id=1, source_target_pairs={{0,3},{1,0},{2,1},{3,2},{4,7},{5,4},{6,5},{7,6},{8,11},{9,8},{10,9... | collective-permute-start | bytes 1572872 | tf_op jit(solution)/shard_map/ppermute | solution.py:21
  18.7 39.3 %collective-permute-start.4 = (bf16[2048,512]{1,0:T(8,128)(2,1)}, bf16[2048,512]{1,0:T(8,128)(2,1)}, u32[]{:S(2)}, u32[]{:S(2)}) collective-permute-start(bf16[2048,512]{1,0:T(8,128)(2,1)} %bitcast.116), channel_id=1, source_target_pairs={{0,64},{64,0},{1,65},{65,1},{2,66},{66,2},{3,67},{67,3},{4,68},{68... | collective-permute-start | bytes 6291464 | tf_op jit(solution)/shard_map/ppermute | solution.py:12
  20.3 10.0 %copy-start.4 = (bf16[1,2,64,2048]{3,2,0,1:T(8,128)(2,1)}, bf16[1,2,64,2048]{3,2,0,1:T(8,128)(2,1)S(1)}, u32[]{:S(2)}) copy-start(bf16[1,2,64,2048]{3,2,0,1:T(8,128)(2,1)S(1)} %fusion.58) | copy-start | bytes 1572868
  29.0 13.9 %copy-start.6 = (bf16[2,64,2048]{2,1,0:T(8,128)(2,1)}, bf16[2,64,2048]{2,1,0:T(8,128)(2,1)S(1)}, u32[]{:S(2)}) copy-start(bf16[2,64,2048]{2,1,0:T(8,128)(2,1)S(1)} %collective-permute-done) | copy-start | bytes 1572868
  51.3 42.0 %all-to-all-start = ((bf16[16,128,512]{2,1,0:T(8,128)(2,1)}), bf16[16,128,512]{2,1,0:T(8,128)(2,1)S(1)}, u32[]{:S(2)}, u32[]{:S(2)}) async-start(bf16[16,128,512]{2,1,0:T(8,128)(2,1)} %bitcast.100), calls=%async_computation | async-start | bytes 4194304 | tf_op jit(solution)/shard_map/all_to_all | solution.py:54
  58.0 260.6 %reduce-scatter.2.cloned.1.call-start = ((), (), s32[]{:S(2)}) async-start(), calls=%async_computation.4 | async-start | bytes 8912896 | tf_op jit(solution)/shard_map/reduce_scatter | solution.py:97
  102.5 314.0 %all-gather.7.cloned.1.call-start = ((), (), s32[]{:S(2)}) async-start(), calls=%async_computation.6 | async-start | bytes 20971520 | tf_op jit(solution)/shard_map/all_gather | solution.py:82
  103.1 221.7 %copy-start.10 = (f32[2,2,64,64]{3,2,1,0:T(8,128)S(1)}, f32[2,2,64,64]{3,2,1,0:T(8,128)}, u32[]{:S(2)}) copy-start(f32[2,2,64,64]{3,2,1,0:T(8,128)} %all-reduce.3.cloned.1.call-done) | copy-start | bytes 196612
  103.1 225.7 %copy-start.5 = (bf16[1,2,64,2048]{3,2,0,1:T(8,128)(2,1)S(1)}, bf16[1,2,64,2048]{3,2,0,1:T(8,128)(2,1)}, u32[]{:S(2)}) copy-start(bf16[1,2,64,2048]{3,2,0,1:T(8,128)(2,1)} %copy-done.4) | copy-start | bytes 1572868
  103.1 225.7 %copy-start.7 = (bf16[2,64,2048]{2,1,0:T(8,128)(2,1)S(1)}, bf16[2,64,2048]{2,1,0:T(8,128)(2,1)}, u32[]{:S(2)}) copy-start(bf16[2,64,2048]{2,1,0:T(8,128)(2,1)} %copy-done.6) | copy-start | bytes 1572868
  103.1 225.6 %copy-start.9 = (bf16[2,64,2048]{2,1,0:T(8,128)(2,1)S(1)}, bf16[2,64,2048]{2,1,0:T(8,128)(2,1)}, u32[]{:S(2)}) copy-start(bf16[2,64,2048]{2,1,0:T(8,128)(2,1)} %copy-done.8) | copy-start | bytes 1572868
  319.7 12.7 %collective-permute-start.5 = (bf16[2,64,2048]{2,1,0:T(8,128)(2,1)S(1)}, bf16[2,64,2048]{2,1,0:T(8,128)(2,1)}, u32[]{:S(2)}, u32[]{:S(2)}) collective-permute-start(bf16[2,64,2048]{2,1,0:T(8,128)(2,1)S(1)} %bitcast.103), channel_id=1, source_target_pairs={{0,1},{1,2},{2,3},{3,0},{4,5},{5,6},{6,7},{7,4},{8,9},{9,10},{10,1... | collective-permute-start | bytes 1572872 | tf_op jit(solution)/shard_map/ppermute | solution.py:21
  321.1 23.8 %collective-permute-start.6 = (bf16[2,64,2048]{2,1,0:T(8,128)(2,1)S(1)}, bf16[2,64,2048]{2,1,0:T(8,128)(2,1)}, u32[]{:S(2)}, u32[]{:S(2)}) collective-permute-start(bf16[2,64,2048]{2,1,0:T(8,128)(2,1)S(1)} %bitcast.104), channel_id=1, source_target_pairs={{0,2},{1,3},{2,0},{3,1},{4,6},{5,7},{6,4},{7,5},{8,10},{9,11},{10,... | collective-permute-start | bytes 1572872 | tf_op jit(solution)/shard_map/ppermute | solution.py:21
  323.7 22.1 %collective-permute-start.7 = (bf16[2,64,2048]{2,1,0:T(8,128)(2,1)S(1)}, bf16[2,64,2048]{2,1,0:T(8,128)(2,1)}, u32[]{:S(2)}, u32[]{:S(2)}) collective-permute-start(bf16[2,64,2048]{2,1,0:T(8,128)(2,1)S(1)} %bitcast.105), channel_id=1, source_target_pairs={{0,3},{1,0},{2,1},{3,2},{4,7},{5,4},{6,5},{7,6},{8,11},{9,8},{10,9... | collective-permute-start | bytes 1572872 | tf_op jit(solution)/shard_map/ppermute | solution.py:21
  324.8 4.0 collective-permute-start.8
  359.4 34.6 %all-to-all-start.1 = ((bf16[16,144,512]{2,1,0:T(8,128)(2,1)}), bf16[16,144,512]{2,1,0:T(8,128)(2,1)S(1)}, u32[]{:S(2)}, u32[]{:S(2)}) async-start(bf16[16,144,512]{2,1,0:T(8,128)(2,1)} %pad_maximum_fusion), calls=%async_computation.2 | async-start | bytes 4718592 | tf_op jit(solution)/shard_map/all_to_all | solution.py:54
  364.1 43.5 %collective-permute-start.3 = (bf16[2048,512]{1,0:T(8,128)(2,1)}, bf16[2048,512]{1,0:T(8,128)(2,1)}, u32[]{:S(2)}, u32[]{:S(2)}) collective-permute-start(bf16[2048,512]{1,0:T(8,128)(2,1)} %bitcast.98), channel_id=1, source_target_pairs={{0,64},{64,0},{1,65},{65,1},{2,66},{66,2},{3,67},{67,3},{4,68},{68... | collective-permute-start | bytes 6291464 | tf_op jit(solution)/shard_map/ppermute | solution.py:12
  395.6 12.0 %collective-permute-start.9 = (bf16[2048,512]{1,0:T(8,128)(2,1)}, bf16[2048,512]{1,0:T(8,128)(2,1)}, u32[]{:S(2)}, u32[]{:S(2)}) collective-permute-start(bf16[2048,512]{1,0:T(8,128)(2,1)} %bitcast.34), channel_id=1, source_target_pairs={{0,64},{64,0},{1,65},{65,1},{2,66},{66,2},{3,67},{67,3},{4,68},{68... | collective-permute-start | bytes 6291464 | tf_op jit(solution)/shard_map/ppermute | solution.py:12
  404.4 1.2 collective-permute-start.11
  406.2 1.2 collective-permute-start.10
  (5 other events, 29.6 us)
Sparse Core Ops, SparseCore 0:
  11.1 56.3 all-reduce.2
  102.6 215.9 reduce-scatter.1
Sparse Core Ops, SparseCore 1:
  12.9 60.2 all-gather.4
  104.6 160.6 all-gather.6

commit v11 on v8

--- a/solution.py
+++ b/solution.py
@@ -76,7 +76,7 @@
     full_width = column_part * group_count
     is_last = section_index == 1
 
-    gathered_inputs = lax.all_gather(local_inputs, "dp", axis=1, tiled=True)
+    early_inputs = lax.all_gather(local_inputs[:1], "dp", axis=1, tiled=True)
     input_grams = lax.psum(token_grams(local_inputs), "tensor")
 
     own_cotangent = lax.dynamic_index_in_dim(cotangent, section_index, 0, keepdims=False)
@@ -88,8 +88,10 @@
     terms = lax.dot_general(
         last_blocks, last_weights, (((1,), (1,)), ((), ())), preferred_element_type=jnp.float32
     ).astype(jnp.bfloat16)
-    terms, input_grams = lax.optimization_barrier((terms, input_grams))
+    terms, input_grams, early_inputs = lax.optimization_barrier((terms, input_grams, early_inputs))
     summed = lax.psum_scatter(terms, "dp", scatter_dimension=0, tiled=True).astype(jnp.float32)
+    late_inputs = lax.all_gather(local_inputs[1:], "dp", axis=1, tiled=True)
+    gathered_inputs = jnp.concatenate([early_inputs, late_inputs], axis=0)
     other_input_grams = swapped(input_grams, "pipe")
     renewed = (own_cotangent.reshape(token_count, width_part).astype(jnp.float32) + summed).astype(
         jnp.bfloat16

time: 355 us -> 353 us (level)
  other arithmetic: 19.7 us -> 31.8 us
  local copies, waits for them, and re-layouts: 28.2 us -> 19 us
  waiting for transfers between devices: 227 us -> 222 us
    all_to_all x2, waiting for transfers between devices: 79 us -> 99.9 us  [column_blocks(): lax.all_to_all(chunks, 'dp', split_axis=0, concat_axis=1, tiled=True)]
    all_gather x1 -> x2, waiting for transfers between devices: 16.3 us -> 0.01 us  [the longest x1 0.01 us: local(): early_inputs = lax.all_gather(local_inputs[:1], 'dp', axis=1, tiled=True)]
    concatenate x0 -> x1, other arithmetic: none -> 13.8 us  [local(): gathered_inputs = jnp.concatenate([early_inputs, late_inputs], axis=0)]
    unnamed x26 -> x27, local copies, waits for them, and re-layouts: 10.8 us -> 1.27 us
    psum x1, waiting for transfers between devices: 6.95 us -> 0.01 us  [local(): input_grams = lax.psum(token_grams(local_inputs), 'tensor')]
    reduce_scatter x1, waiting for transfers between devices: 89.3 us -> 85.4 us  [local(): lax.psum_scatter(terms, 'dp', scatter_dimension=0, tiled=True)]
  transfers between devices with their start and end apart: 17 -> 18, of which waited for: 13 -> 10; matrix products, arithmetic and copies ran while one was open for 16% -> 16% of each run, Pallas kernels for 0% -> 0%
where the time goes in v11:
time: 353 us; the launch traced here: 352 us
  waiting for transfers between devices  222 us (63%)
  starting transfers between devices  32.3 us (9%)
  other arithmetic  31.8 us (9%)
  matrix products  30.5 us (9%)
  local copies, waits for them, and re-layouts  19 us (5%)
  between operations  16.6 us (5%)
    all_to_all x2, waiting for transfers between devices, column_blocks(): lax.all_to_all(chunks, 'dp', split_axis=0, concat_axis=1, tiled=True)  99.9 us
    reduce_scatter x1, waiting for transfers between devices, local(): lax.psum_scatter(terms, 'dp', scatter_dimension=0, tiled=True)  85.4 us
    ppermute x6, waiting for transfers between devices, ring_pieces(): lax.ppermute(values, axis, [(source, (source + offset) % count) for sourc...  33.4 us
    dot_general x1, matrix products, local(): lax.dot_general(flat_inputs, flat_grads, (((0,), (0,)), ((), ())), prefer...  13.9 us
    concatenate x1, other arithmetic, local(): gathered_inputs = jnp.concatenate([early_inputs, late_inputs], axis=0)  13.8 us
    all_to_all x2, starting transfers between devices, column_blocks(): lax.all_to_all(chunks, 'dp', split_axis=0, concat_axis=1, tiled=True)  11.1 us
    ppermute x6, starting transfers between devices, ring_pieces(): lax.ppermute(values, axis, [(source, (source + offset) % count) for sourc...  10.9 us
    another operation x16, local copies, waits for them, and re-layouts, ring_pieces(): stacked = jnp.stack(pieces)  10.4 us
  transfers between devices with their start and end apart: 18, of which 10 were waited for; matrix products, arithmetic and copies ran while one was open for 16% of the time, Pallas kernels for 0%

profile of v11, /device:TPU:1, one launch (start us, length us, event | category | flops | bytes accessed | tf_op | source)
XLA Modules:
  0.0 351.9 jit_solution(4870838533020098014)
XLA Ops:
  8.1 2.8 fusion.29
  12.9 4.6 %collective-permute-start.2 = (bf16[2,64,2048]{2,1,0:T(8,128)(2,1)}, bf16[2,64,2048]{2,1,0:T(8,128)(2,1)S(1)}, u32[]{:S(2)}, u32[]{:S(2)}) collective-permute-start(bf16[2,64,2048]{2,1,0:T(8,128)(2,1)} %fusion.59), channel_id=1, source_target_pairs={{0,3},{1,0},{2,1},{3,2},{4,7},{5,4},{6,5},{7,6},{8,11},{9,8},{10,9... | collective-permute-start | bytes 1572872 | tf_op jit(solution)/shard_map/ppermute | solution.py:18
  21.6 18.9 %collective-permute-done.2 = bf16[2,64,2048]{2,1,0:T(8,128)(2,1)S(1)} collective-permute-done((bf16[2,64,2048]{2,1,0:T(8,128)(2,1)}, bf16[2,64,2048]{2,1,0:T(8,128)(2,1)S(1)}, u32[]{:S(2)}, u32[]{:S(2)}) %collective-permute-start.2) | collective-permute-done | bytes 524320 | tf_op jit(solution)/shard_map/ppermute | solution.py:18
  46.3 2.0 gather_fusion
  48.3 3.2 broadcast_select_fusion.1
  51.4 6.8 %all-to-all-start = ((bf16[16,128,512]{2,1,0:T(8,128)(2,1)}), bf16[16,128,512]{2,1,0:T(8,128)(2,1)S(1)}, u32[]{:S(2)}, u32[]{:S(2)}) async-start(bf16[16,128,512]{2,1,0:T(8,128)(2,1)} %bitcast.105), calls=%async_computation | async-start | bytes 4194304 | tf_op jit(solution)/shard_map/all_to_all | solution.py:51
  58.3 49.3 %all-to-all-done = bf16[16,128,512]{2,1,0:T(8,128)(2,1)S(1)} async-done(((bf16[16,128,512]{2,1,0:T(8,128)(2,1)}), bf16[16,128,512]{2,1,0:T(8,128)(2,1)S(1)}, u32[]{:S(2)}, u32[]{:S(2)}) %all-to-all-start) | async-done | bytes 2097184 | tf_op jit(solution)/shard_map/all_to_all | solution.py:51
  107.5 9.1 %convolution_convert_fusion = bf16[2048,2048]{1,0:T(8,128)(2,1)} fusion(bf16[2048,512]{1,0:T(8,128)(2,1)S(1)} %bitcast.102, bf16[2048,512]{1,0:T(8,128)(2,1)} %collective-permute-done.3, pred[]{:T(512)S(6)} %eq.6, bf16[1,2048,512]{2,1,0:T(8,128)(2,1)} %param.9), kind=kOutput, calls=%fused_computation.4 | convolution fusion | flops 4300210176 | bytes 14680065 | tf_op jit(solution)/shard_map/dot_general | solution.py:88
  117.4 85.4 %reduce-scatter.2.cloned.1.call-done = bf16[128,2048]{1,0:T(8,128)(2,1)} async-done(((bf16[2048,2048]{1,0:T(8,128)(2,1)}), bf16[128,2048]{1,0:T(8,128)(2,1)}) %reduce-scatter.2.cloned.1.call-update) | async-done | bytes 524304 | tf_op jit(solution)/shard_map/reduce_scatter | solution.py:92
  205.3 2.6 collective-permute-start.6
  209.0 3.0 collective-permute-start.8
  213.0 2.0 fusion.31
  216.7 12.4 %collective-permute-done.6 = bf16[2,64,2048]{2,1,0:T(8,128)(2,1)} collective-permute-done((bf16[2,64,2048]{2,1,0:T(8,128)(2,1)S(1)}, bf16[2,64,2048]{2,1,0:T(8,128)(2,1)}, u32[]{:S(2)}, u32[]{:S(2)}) %collective-permute-start.6) | collective-permute-done | bytes 524320 | tf_op jit(solution)/shard_map/ppermute | solution.py:18
  230.0 2.7 fusion.32
  237.5 1.9 fusion.3
  239.3 2.6 gather_fusion.1
  242.3 1.6 pad_maximum_fusion.1
  244.0 4.3 %all-to-all-start.1 = ((bf16[16,144,512]{2,1,0:T(8,128)(2,1)}), bf16[16,144,512]{2,1,0:T(8,128)(2,1)S(1)}, u32[]{:S(2)}, u32[]{:S(2)}) async-start(bf16[16,144,512]{2,1,0:T(8,128)(2,1)} %pad_maximum_fusion.1), calls=%async_computation.2 | async-start | bytes 4718592 | tf_op jit(solution)/shard_map/all_to_all | solution.py:51
  248.3 3.0 collective-permute-start.4
  251.3 50.7 %all-to-all-done.1 = bf16[16,144,512]{2,1,0:T(8,128)(2,1)S(1)} async-done(((bf16[16,144,512]{2,1,0:T(8,128)(2,1)}), bf16[16,144,512]{2,1,0:T(8,128)(2,1)S(1)}, u32[]{:S(2)}, u32[]{:S(2)}) %all-to-all-start.1) | async-done | bytes 2359328 | tf_op jit(solution)/shard_map/all_to_all | solution.py:51
  303.5 2.4 collective-permute-start.9
  305.8 13.8 %pad_maximum_fusion = bf16[2,32,64,2048]{3,2,1,0:T(8,128)(2,1)} fusion(bf16[1,32,64,2048]{3,2,1,0:T(8,128)(2,1)} %bitcast.108, bf16[1,32,64,2048]{3,2,1,0:T(8,128)(2,1)} %bitcast.107), kind=kLoop, calls=%fused_computation.2 | loop fusion | flops 8388608 | bytes 33554432 | tf_op jit(solution)/shard_map/concatenate | solution.py:94
  322.8 7.6 %multiply_convert_fusion = bf16[2,16,2,64,512]{4,3,2,1,0:T(8,128)(2,1)S(1)} fusion(bf16[1,16,2,64,512]{4,3,2,1,0:T(8,128)(2,1)} %bitcast.104, bf16[1,16,2,64,512]{4,3,2,1,0:T(8,128)(2,1)} %bitcast.9, bf16[1,16,2,64,512]{4,3,2,1,0:T(8,128)(2,1)} %bitcast.39, bf16[1,16,2,64,512]{4,3,2,1,0:T(8,128)(2,1)} %bitcast.38, f32[2,16,2]{2,1,0:T(8,128)S(1)} %copy.113, ...), kind=kLoop, calls=%fused_computation.3 | loop fusion | flops 20971520 | bytes 12583169 | tf_op jit(solution)/shard_map/convert_element_type | solution.py:127
  330.5 13.9 %fusion.2 = f32[1,2048,512]{2,1,0:T(8,128)} fusion(bf16[1,2048,512]{2,1,0:T(8,128)(2,1)S(1)} %copy-done.10, bf16[4096,2048]{1,0:T(8,128)(2,1)} %bitcast.101, bf16[4096,512]{1,0:T(8,128)(2,1)S(1)} %bitcast.109, f32[]{:T(128)S(6)} %mul_shard_map.3), kind=kOutput, calls=%fused_computation.10 | convolution fusion | flops 8594128896 | bytes 27262980 | tf_op jit(solution)/shard_map/dot_general | solution.py:130
  (94 shorter events, 28.9 us)
Async XLA Ops:
  8.0 108.7 %all-reduce.3.cloned.1.call-start = ((), (), s32[]{:S(2)}) async-start(), calls=%async_computation.3 | async-start | bytes 262144 | tf_op jit(solution)/shard_map/psum | solution.py:80
  10.8 105.9 %all-gather.5.cloned.1.call-start = ((), (), s32[]{:S(2)}) async-start(), calls=%async_computation.5 | async-start | bytes 8912896 | tf_op jit(solution)/shard_map/all_gather | solution.py:79
  12.9 27.6 %collective-permute-start.2 = (bf16[2,64,2048]{2,1,0:T(8,128)(2,1)}, bf16[2,64,2048]{2,1,0:T(8,128)(2,1)S(1)}, u32[]{:S(2)}, u32[]{:S(2)}) collective-permute-start(bf16[2,64,2048]{2,1,0:T(8,128)(2,1)} %fusion.59), channel_id=1, source_target_pairs={{0,3},{1,0},{2,1},{3,2},{4,7},{5,4},{6,5},{7,6},{8,11},{9,8},{10,9... | collective-permute-start | bytes 1572872 | tf_op jit(solution)/shard_map/ppermute | solution.py:18
  17.4 24.4 %collective-permute-start = (bf16[2,64,2048]{2,1,0:T(8,128)(2,1)}, bf16[2,64,2048]{2,1,0:T(8,128)(2,1)S(1)}, u32[]{:S(2)}, u32[]{:S(2)}) collective-permute-start(bf16[2,64,2048]{2,1,0:T(8,128)(2,1)} %fusion.59), channel_id=1, source_target_pairs={{0,1},{1,2},{2,3},{3,0},{4,5},{5,6},{6,7},{7,4},{8,9},{9,10},{10,1... | collective-permute-start | bytes 1572872 | tf_op jit(solution)/shard_map/ppermute | solution.py:18
  17.4 25.7 %collective-permute-start.1 = (bf16[2,64,2048]{2,1,0:T(8,128)(2,1)}, bf16[2,64,2048]{2,1,0:T(8,128)(2,1)}, u32[]{:S(2)}, u32[]{:S(2)}) collective-permute-start(bf16[2,64,2048]{2,1,0:T(8,128)(2,1)} %fusion.59), channel_id=1, source_target_pairs={{0,2},{1,3},{2,0},{3,1},{4,6},{5,7},{6,4},{7,5},{8,10},{9,11},{10,... | collective-permute-start | bytes 1572872 | tf_op jit(solution)/shard_map/ppermute | solution.py:18
  18.7 39.5 %collective-permute-start.3 = (bf16[2048,512]{1,0:T(8,128)(2,1)}, bf16[2048,512]{1,0:T(8,128)(2,1)}, u32[]{:S(2)}, u32[]{:S(2)}) collective-permute-start(bf16[2048,512]{1,0:T(8,128)(2,1)} %bitcast.122), channel_id=1, source_target_pairs={{0,64},{64,0},{1,65},{65,1},{2,66},{66,2},{3,67},{67,3},{4,68},{68... | collective-permute-start | bytes 6291464 | tf_op jit(solution)/shard_map/ppermute | solution.py:9
  20.3 21.5 %copy-start.3 = (bf16[1,2,64,2048]{3,2,0,1:T(8,128)(2,1)}, bf16[1,2,64,2048]{3,2,0,1:T(8,128)(2,1)S(1)}, u32[]{:S(2)}) copy-start(bf16[1,2,64,2048]{3,2,0,1:T(8,128)(2,1)S(1)} %fusion.58) | copy-start | bytes 1572868
  51.4 56.1 %all-to-all-start = ((bf16[16,128,512]{2,1,0:T(8,128)(2,1)}), bf16[16,128,512]{2,1,0:T(8,128)(2,1)S(1)}, u32[]{:S(2)}, u32[]{:S(2)}) async-start(bf16[16,128,512]{2,1,0:T(8,128)(2,1)} %bitcast.105), calls=%async_computation | async-start | bytes 4194304 | tf_op jit(solution)/shard_map/all_to_all | solution.py:51
  58.2 144.6 %reduce-scatter.2.cloned.1.call-start = ((), (), s32[]{:S(2)}) async-start(), calls=%async_computation.4 | async-start | bytes 8912896 | tf_op jit(solution)/shard_map/reduce_scatter | solution.py:92
  116.7 92.2 %copy-start.11 = (f32[2,2,64,64]{3,2,1,0:T(8,128)S(1)}, f32[2,2,64,64]{3,2,1,0:T(8,128)}, u32[]{:S(2)}) copy-start(f32[2,2,64,64]{3,2,1,0:T(8,128)} %all-reduce.3.cloned.1.call-done) | copy-start | bytes 196612
  116.7 96.2 %copy-start.4 = (bf16[1,2,64,2048]{3,2,0,1:T(8,128)(2,1)S(1)}, bf16[1,2,64,2048]{3,2,0,1:T(8,128)(2,1)}, u32[]{:S(2)}) copy-start(bf16[1,2,64,2048]{3,2,0,1:T(8,128)(2,1)} %copy-done.3) | copy-start | bytes 1572868
  116.8 96.2 %copy-start.7 = (bf16[2,64,2048]{2,1,0:T(8,128)(2,1)S(1)}, bf16[2,64,2048]{2,1,0:T(8,128)(2,1)}, u32[]{:S(2)}) copy-start(bf16[2,64,2048]{2,1,0:T(8,128)(2,1)} %copy-done.6) | copy-start | bytes 1572868
  116.8 96.2 %copy-start.9 = (bf16[2,64,2048]{2,1,0:T(8,128)(2,1)S(1)}, bf16[2,64,2048]{2,1,0:T(8,128)(2,1)}, u32[]{:S(2)}) copy-start(bf16[2,64,2048]{2,1,0:T(8,128)(2,1)} %copy-done.8) | copy-start | bytes 1572868
  116.8 189.1 %all-gather.7.cloned.1.call-start = ((), (), s32[]{:S(2)}) async-start(), calls=%async_computation.6 | async-start | bytes 8912896 | tf_op jit(solution)/shard_map/all_gather | solution.py:93
  204.0 12.7 %collective-permute-start.5 = (bf16[2,64,2048]{2,1,0:T(8,128)(2,1)S(1)}, bf16[2,64,2048]{2,1,0:T(8,128)(2,1)}, u32[]{:S(2)}, u32[]{:S(2)}) collective-permute-start(bf16[2,64,2048]{2,1,0:T(8,128)(2,1)S(1)} %bitcast.110), channel_id=1, source_target_pairs={{0,1},{1,2},{2,3},{3,0},{4,5},{5,6},{6,7},{7,4},{8,9},{9,10},{10,1... | collective-permute-start | bytes 1572872 | tf_op jit(solution)/shard_map/ppermute | solution.py:18
  205.3 23.8 %collective-permute-start.6 = (bf16[2,64,2048]{2,1,0:T(8,128)(2,1)S(1)}, bf16[2,64,2048]{2,1,0:T(8,128)(2,1)}, u32[]{:S(2)}, u32[]{:S(2)}) collective-permute-start(bf16[2,64,2048]{2,1,0:T(8,128)(2,1)S(1)} %bitcast.111), channel_id=1, source_target_pairs={{0,2},{1,3},{2,0},{3,1},{4,6},{5,7},{6,4},{7,5},{8,10},{9,11},{10,... | collective-permute-start | bytes 1572872 | tf_op jit(solution)/shard_map/ppermute | solution.py:18
  207.9 22.1 %collective-permute-start.7 = (bf16[2,64,2048]{2,1,0:T(8,128)(2,1)S(1)}, bf16[2,64,2048]{2,1,0:T(8,128)(2,1)}, u32[]{:S(2)}, u32[]{:S(2)}) collective-permute-start(bf16[2,64,2048]{2,1,0:T(8,128)(2,1)S(1)} %bitcast.112), channel_id=1, source_target_pairs={{0,3},{1,0},{2,1},{3,2},{4,7},{5,4},{6,5},{7,6},{8,11},{9,8},{10,9... | collective-permute-start | bytes 1572872 | tf_op jit(solution)/shard_map/ppermute | solution.py:18
  209.0 4.0 %collective-permute-start.8 = (f32[2,2,64,64]{3,2,1,0:T(8,128)S(1)}, f32[2,2,64,64]{3,2,1,0:T(8,128)S(1)}, u32[]{:S(2)}, u32[]{:S(2)}) collective-permute-start(f32[2,2,64,64]{3,2,1,0:T(8,128)S(1)} %copy-done.11), channel_id=1, source_target_pairs={{0,64},{64,0},{1,65},{65,1},{2,66},{66,2},{3,67},{67,3},{4,68},{68... | collective-permute-start | bytes 196616 | tf_op jit(solution)/shard_map/ppermute | solution.py:9
  244.0 58.0 %all-to-all-start.1 = ((bf16[16,144,512]{2,1,0:T(8,128)(2,1)}), bf16[16,144,512]{2,1,0:T(8,128)(2,1)S(1)}, u32[]{:S(2)}, u32[]{:S(2)}) async-start(bf16[16,144,512]{2,1,0:T(8,128)(2,1)} %pad_maximum_fusion.1), calls=%async_computation.2 | async-start | bytes 4718592 | tf_op jit(solution)/shard_map/all_to_all | solution.py:51
  248.3 74.6 %collective-permute-start.4 = (bf16[2048,512]{1,0:T(8,128)(2,1)}, bf16[2048,512]{1,0:T(8,128)(2,1)}, u32[]{:S(2)}, u32[]{:S(2)}) collective-permute-start(bf16[2048,512]{1,0:T(8,128)(2,1)} %bitcast.103), channel_id=1, source_target_pairs={{0,64},{64,0},{1,65},{65,1},{2,66},{66,2},{3,67},{67,3},{4,68},{68... | collective-permute-start | bytes 6291464 | tf_op jit(solution)/shard_map/ppermute | solution.py:9
  303.5 19.4 %collective-permute-start.9 = (bf16[2048,512]{1,0:T(8,128)(2,1)}, bf16[2048,512]{1,0:T(8,128)(2,1)}, u32[]{:S(2)}, u32[]{:S(2)}) collective-permute-start(bf16[2048,512]{1,0:T(8,128)(2,1)} %bitcast.37), channel_id=1, source_target_pairs={{0,64},{64,0},{1,65},{65,1},{2,66},{66,2},{3,67},{67,3},{4,68},{68... | collective-permute-start | bytes 6291464 | tf_op jit(solution)/shard_map/ppermute | solution.py:9
  319.6 1.2 collective-permute-start.11
  321.5 1.2 collective-permute-start.10
  330.4 13.9 %copy-start.1 = (bf16[2,2,64,2048]{3,2,1,0:T(8,128)(2,1)S(1)}, bf16[2,2,64,2048]{3,2,1,0:T(8,128)(2,1)}, u32[]{:S(2)}) copy-start(bf16[2,2,64,2048]{3,2,1,0:T(8,128)(2,1)} %param.11) | copy-start | bytes 3145732
  (6 other events, 29.0 us)
Sparse Core Ops, SparseCore 0:
  11.1 52.7 all-reduce.2
Sparse Core Ops, SparseCore 1:
  13.5 96.0 all-gather.4
  116.8 85.9 reduce-scatter.1
  204.8 96.3 all-gather.6

commit v12 on v11

--- a/solution.py
+++ b/solution.py
@@ -91,7 +91,6 @@
     terms, input_grams, early_inputs = lax.optimization_barrier((terms, input_grams, early_inputs))
     summed = lax.psum_scatter(terms, "dp", scatter_dimension=0, tiled=True).astype(jnp.float32)
     late_inputs = lax.all_gather(local_inputs[1:], "dp", axis=1, tiled=True)
-    gathered_inputs = jnp.concatenate([early_inputs, late_inputs], axis=0)
     other_input_grams = swapped(input_grams, "pipe")
     renewed = (own_cotangent.reshape(token_count, width_part).astype(jnp.float32) + summed).astype(
         jnp.bfloat16
@@ -125,10 +124,14 @@
         )
         * row_scales.reshape(micro_count, group_count, example_count)[:, :, :, None, None]
     ).astype(jnp.bfloat16)
-    flat_inputs = gathered_inputs.reshape(micro_count * group_count * token_count, width_part)
-    flat_grads = scaled_blocks.reshape(micro_count * group_count * token_count, column_part)
-    summed_grad = lax.dot_general(
-        flat_inputs, flat_grads, (((0,), (0,)), ((), ())), preferred_element_type=jnp.float32
+    summed_grad = sum(
+        lax.dot_general(
+            half.reshape(group_count * token_count, width_part),
+            scaled_blocks[index].reshape(group_count * token_count, column_part),
+            (((0,), (0,)), ((), ())),
+            preferred_element_type=jnp.float32,
+        )
+        for index, half in enumerate([early_inputs[0], late_inputs[0]])
     )
     noise_weight = 1.5 / full_width
     per_example_sum = micro_count * group_count * example_count

time: 353 us -> 346 us (0.980)
  other arithmetic: 31.8 us -> 18 us
  matrix products: 30.5 us -> 34.9 us
    concatenate x1 -> x0, other arithmetic: 13.8 us -> none  [local(): gathered_inputs = jnp.concatenate([early_inputs, late_inputs], axis=0)]
    dot_general x1 -> x2, matrix products: 13.9 us -> 18.3 us  [local(): lax.dot_general(half.reshape(group_count * token_count, width_part), scal...]
  transfers between devices with their start and end apart: 18 -> 18, of which waited for: 10 -> 11; matrix products, arithmetic and copies ran while one was open for 16% -> 15% of each run, Pallas kernels for 0% -> 0%
where the time goes in v12:
time: 346 us
  waiting for transfers between devices  222 us (64%)
  matrix products  34.9 us (10%)
  starting transfers between devices  33.3 us (10%)
  local copies, waits for them, and re-layouts  20.8 us (6%)
  other arithmetic  18 us (5%)
  between operations  16.6 us (5%)
    all_to_all x2, waiting for transfers between devices, column_blocks(): lax.all_to_all(chunks, 'dp', split_axis=0, concat_axis=1, tiled=True)  100 us
    reduce_scatter x1, waiting for transfers between devices, local(): lax.psum_scatter(terms, 'dp', scatter_dimension=0, tiled=True)  82.5 us
    ppermute x6, waiting for transfers between devices, ring_pieces(): lax.ppermute(values, axis, [(source, (source + offset) % count) for sourc...  33.3 us
    dot_general x2, matrix products, local(): lax.dot_general(half.reshape(group_count * token_count, width_part), scal...  18.3 us
    ppermute x6, starting transfers between devices, ring_pieces(): lax.ppermute(values, axis, [(source, (source + offset) % count) for sourc...  11.5 us
    all_to_all x2, starting transfers between devices, column_blocks(): lax.all_to_all(chunks, 'dp', split_axis=0, concat_axis=1, tiled=True)  11 us
    ppermute x6, starting transfers between devices, swapped(): lax.ppermute(value, axis, [(source, count - 1 - source) for source in ran...  10.6 us
    another operation x16, local copies, waits for them, and re-layouts, ring_pieces(): stacked = jnp.stack(pieces)  10.4 us
  transfers between devices with their start and end apart: 18, of which 11 were waited for; matrix products, arithmetic and copies ran while one was open for 15% of the time, Pallas kernels for 0%

profile of v12, /device:TPU:1, one launch (start us, length us, event | category | flops | bytes accessed | tf_op | source)
XLA Modules:
  0.0 345.8 jit_solution(5287654525957281249)
XLA Ops:
  8.1 2.8 fusion.29
  12.9 2.5 collective-permute-start
  15.4 3.3 collective-permute-start.1
  22.3 7.5 %collective-permute-done = bf16[2,64,2048]{2,1,0:T(8,128)(2,1)S(1)} collective-permute-done((bf16[2,64,2048]{2,1,0:T(8,128)(2,1)}, bf16[2,64,2048]{2,1,0:T(8,128)(2,1)S(1)}, u32[]{:S(2)}, u32[]{:S(2)}) %collective-permute-start) | collective-permute-done | bytes 524320 | tf_op jit(solution)/shard_map/ppermute | solution.py:18
  31.1 11.3 %collective-permute-done.1 = bf16[2,64,2048]{2,1,0:T(8,128)(2,1)S(1)} collective-permute-done((bf16[2,64,2048]{2,1,0:T(8,128)(2,1)}, bf16[2,64,2048]{2,1,0:T(8,128)(2,1)S(1)}, u32[]{:S(2)}, u32[]{:S(2)}) %collective-permute-start.1) | collective-permute-done | bytes 524320 | tf_op jit(solution)/shard_map/ppermute | solution.py:18
  46.9 2.0 gather_fusion
  48.9 3.2 broadcast_select_fusion.1
  52.0 6.8 %all-to-all-start = ((bf16[16,128,512]{2,1,0:T(8,128)(2,1)}), bf16[16,128,512]{2,1,0:T(8,128)(2,1)S(1)}, u32[]{:S(2)}, u32[]{:S(2)}) async-start(bf16[16,128,512]{2,1,0:T(8,128)(2,1)} %bitcast.111), calls=%async_computation | async-start | bytes 4194304 | tf_op jit(solution)/shard_map/all_to_all | solution.py:51
  58.9 49.8 %all-to-all-done = bf16[16,128,512]{2,1,0:T(8,128)(2,1)S(1)} async-done(((bf16[16,128,512]{2,1,0:T(8,128)(2,1)}), bf16[16,128,512]{2,1,0:T(8,128)(2,1)S(1)}, u32[]{:S(2)}, u32[]{:S(2)}) %all-to-all-start) | async-done | bytes 2097184 | tf_op jit(solution)/shard_map/all_to_all | solution.py:51
  108.7 9.1 %convolution_convert_fusion = bf16[2048,2048]{1,0:T(8,128)(2,1)} fusion(bf16[2048,512]{1,0:T(8,128)(2,1)S(1)} %bitcast.108, bf16[2048,512]{1,0:T(8,128)(2,1)} %collective-permute-done.3, pred[]{:T(512)S(6)} %eq.6, bf16[1,2048,512]{2,1,0:T(8,128)(2,1)} %param.9), kind=kOutput, calls=%fused_computation.3 | convolution fusion | flops 4300210176 | bytes 14680065 | tf_op jit(solution)/shard_map/dot_general | solution.py:88
  118.5 82.5 %reduce-scatter.2.cloned.1.call-done = bf16[128,2048]{1,0:T(8,128)(2,1)} async-done(((bf16[2048,2048]{1,0:T(8,128)(2,1)}), bf16[128,2048]{1,0:T(8,128)(2,1)}) %reduce-scatter.2.cloned.1.call-update) | async-done | bytes 524304 | tf_op jit(solution)/shard_map/reduce_scatter | solution.py:92
  203.6 2.6 collective-permute-start.6
  207.2 3.0 collective-permute-start.8
  214.9 12.4 %collective-permute-done.6 = bf16[2,64,2048]{2,1,0:T(8,128)(2,1)} collective-permute-done((bf16[2,64,2048]{2,1,0:T(8,128)(2,1)S(1)}, bf16[2,64,2048]{2,1,0:T(8,128)(2,1)}, u32[]{:S(2)}, u32[]{:S(2)}) %collective-permute-start.6) | collective-permute-done | bytes 524320 | tf_op jit(solution)/shard_map/ppermute | solution.py:18
  228.2 2.7 fusion.32
  237.6 2.6 gather_fusion.1
  242.2 4.3 %all-to-all-start.1 = ((bf16[16,144,512]{2,1,0:T(8,128)(2,1)}), bf16[16,144,512]{2,1,0:T(8,128)(2,1)S(1)}, u32[]{:S(2)}, u32[]{:S(2)}) async-start(bf16[16,144,512]{2,1,0:T(8,128)(2,1)} %pad_maximum_fusion), calls=%async_computation.2 | async-start | bytes 4718592 | tf_op jit(solution)/shard_map/all_to_all | solution.py:51
  246.5 3.0 collective-permute-start.4
  249.5 50.6 %all-to-all-done.1 = bf16[16,144,512]{2,1,0:T(8,128)(2,1)S(1)} async-done(((bf16[16,144,512]{2,1,0:T(8,128)(2,1)}), bf16[16,144,512]{2,1,0:T(8,128)(2,1)S(1)}, u32[]{:S(2)}, u32[]{:S(2)}) %all-to-all-start.1) | async-done | bytes 2359328 | tf_op jit(solution)/shard_map/all_to_all | solution.py:51
  301.7 2.4 collective-permute-start.9
  304.1 4.1 %collective-permute-done.11 = f32[2]{0:T(128)S(1)} collective-permute-done((f32[2]{0:T(128)S(1)}, f32[2]{0:T(128)S(1)}, u32[]{:S(2)}, u32[]{:S(2)}) %collective-permute-start.11) | collective-permute-done | bytes 40 | tf_op jit(solution)/shard_map/ppermute | solution.py:9
  310.5 7.7 %multiply_convert_fusion = bf16[2,16,2,64,512]{4,3,2,1,0:T(8,128)(2,1)S(1)} fusion(bf16[1,16,2,64,512]{4,3,2,1,0:T(8,128)(2,1)} %bitcast.110, bf16[1,16,2,64,512]{4,3,2,1,0:T(8,128)(2,1)} %bitcast.8, bf16[1,16,2,64,512]{4,3,2,1,0:T(8,128)(2,1)} %bitcast.38, bf16[1,16,2,64,512]{4,3,2,1,0:T(8,128)(2,1)} %bitcast.37, f32[2,16,2]{2,1,0:T(8,128)S(1)} %copy.118, ...), kind=kLoop, calls=%fused_computation.2 | loop fusion | flops 20971520 | bytes 12583169 | tf_op jit(solution)/shard_map/convert_element_type | solution.py:126
  319.9 7.8 %fusion.54 = f32[512,2048]{0,1:T(8,128)S(1)} fusion(bf16[2048,512]{1,0:T(8,128)(2,1)} %bitcast.118, bf16[2048,2048]{1,0:T(8,128)(2,1)} %bitcast.128), kind=kOutput, calls=%fused_computation.80 | convolution fusion | flops 4294967296 | bytes 14680064 | tf_op jit(solution)/shard_map/dot_general | solution.py:128
  327.7 10.5 %fusion.2 = f32[1,2048,512]{2,1,0:T(8,128)} fusion(f32[512,2048]{0,1:T(8,128)S(1)} %fusion.54, bf16[1,2048,512]{2,1,0:T(8,128)(2,1)S(1)} %copy-done.10, bf16[2048,2048]{1,0:T(8,128)(2,1)} %bitcast.127, bf16[2048,512]{1,0:T(8,128)(2,1)S(1)} %bitcast.117, f32[]{:T(128)S(6)} %mul_shard_map.3), kind=kOutput, calls=%fused_computation.9 | convolution fusion | flops 4300210176 | bytes 20971524 | tf_op jit(solution)/shard_map/dot_general | solution.py:128
  (95 shorter events, 34.7 us)
Async XLA Ops:
  8.0 109.8 %all-reduce.3.cloned.1.call-start = ((), (), s32[]{:S(2)}) async-start(), calls=%async_computation.3 | async-start | bytes 262144 | tf_op jit(solution)/shard_map/psum | solution.py:80
  10.8 107.0 %all-gather.5.cloned.1.call-start = ((), (), s32[]{:S(2)}) async-start(), calls=%async_computation.5 | async-start | bytes 8912896 | tf_op jit(solution)/shard_map/all_gather | solution.py:79
  12.9 16.9 %collective-permute-start = (bf16[2,64,2048]{2,1,0:T(8,128)(2,1)}, bf16[2,64,2048]{2,1,0:T(8,128)(2,1)S(1)}, u32[]{:S(2)}, u32[]{:S(2)}) collective-permute-start(bf16[2,64,2048]{2,1,0:T(8,128)(2,1)} %fusion.63), channel_id=1, source_target_pairs={{0,1},{1,2},{2,3},{3,0},{4,5},{5,6},{6,7},{7,4},{8,9},{9,10},{10,1... | collective-permute-start | bytes 1572872 | tf_op jit(solution)/shard_map/ppermute | solution.py:18
  15.4 27.0 %collective-permute-start.1 = (bf16[2,64,2048]{2,1,0:T(8,128)(2,1)}, bf16[2,64,2048]{2,1,0:T(8,128)(2,1)S(1)}, u32[]{:S(2)}, u32[]{:S(2)}) collective-permute-start(bf16[2,64,2048]{2,1,0:T(8,128)(2,1)} %fusion.63), channel_id=1, source_target_pairs={{0,2},{1,3},{2,0},{3,1},{4,6},{5,7},{6,4},{7,5},{8,10},{9,11},{10,... | collective-permute-start | bytes 1572872 | tf_op jit(solution)/shard_map/ppermute | solution.py:18
  18.7 25.0 %collective-permute-start.2 = (bf16[2,64,2048]{2,1,0:T(8,128)(2,1)}, bf16[2,64,2048]{2,1,0:T(8,128)(2,1)}, u32[]{:S(2)}, u32[]{:S(2)}) collective-permute-start(bf16[2,64,2048]{2,1,0:T(8,128)(2,1)} %fusion.63), channel_id=1, source_target_pairs={{0,3},{1,0},{2,1},{3,2},{4,7},{5,4},{6,5},{7,6},{8,11},{9,8},{10,9... | collective-permute-start | bytes 1572872 | tf_op jit(solution)/shard_map/ppermute | solution.py:18
  19.4 39.4 %collective-permute-start.3 = (bf16[2048,512]{1,0:T(8,128)(2,1)}, bf16[2048,512]{1,0:T(8,128)(2,1)}, u32[]{:S(2)}, u32[]{:S(2)}) collective-permute-start(bf16[2048,512]{1,0:T(8,128)(2,1)} %bitcast.129), channel_id=1, source_target_pairs={{0,64},{64,0},{1,65},{65,1},{2,66},{66,2},{3,67},{67,3},{4,68},{68... | collective-permute-start | bytes 6291464 | tf_op jit(solution)/shard_map/ppermute | solution.py:9
  29.8 13.9 %copy-start.6 = (bf16[2,64,2048]{2,1,0:T(8,128)(2,1)}, bf16[2,64,2048]{2,1,0:T(8,128)(2,1)S(1)}, u32[]{:S(2)}) copy-start(bf16[2,64,2048]{2,1,0:T(8,128)(2,1)S(1)} %collective-permute-done) | copy-start | bytes 1572868
  52.0 56.6 %all-to-all-start = ((bf16[16,128,512]{2,1,0:T(8,128)(2,1)}), bf16[16,128,512]{2,1,0:T(8,128)(2,1)S(1)}, u32[]{:S(2)}, u32[]{:S(2)}) async-start(bf16[16,128,512]{2,1,0:T(8,128)(2,1)} %bitcast.111), calls=%async_computation | async-start | bytes 4194304 | tf_op jit(solution)/shard_map/all_to_all | solution.py:51
  58.8 142.2 %reduce-scatter.2.cloned.1.call-start = ((), (), s32[]{:S(2)}) async-start(), calls=%async_computation.4 | async-start | bytes 8912896 | tf_op jit(solution)/shard_map/reduce_scatter | solution.py:92
  117.8 89.4 %copy-start.11 = (f32[2,2,64,64]{3,2,1,0:T(8,128)S(1)}, f32[2,2,64,64]{3,2,1,0:T(8,128)}, u32[]{:S(2)}) copy-start(f32[2,2,64,64]{3,2,1,0:T(8,128)} %all-reduce.3.cloned.1.call-done) | copy-start | bytes 196612
  117.8 93.3 %copy-start.4 = (bf16[1,2,64,2048]{3,2,0,1:T(8,128)(2,1)S(1)}, bf16[1,2,64,2048]{3,2,0,1:T(8,128)(2,1)}, u32[]{:S(2)}) copy-start(bf16[1,2,64,2048]{3,2,0,1:T(8,128)(2,1)} %copy-done.3) | copy-start | bytes 1572868
  117.9 93.3 %copy-start.7 = (bf16[2,64,2048]{2,1,0:T(8,128)(2,1)S(1)}, bf16[2,64,2048]{2,1,0:T(8,128)(2,1)}, u32[]{:S(2)}) copy-start(bf16[2,64,2048]{2,1,0:T(8,128)(2,1)} %copy-done.6) | copy-start | bytes 1572868
  117.9 93.3 %copy-start.9 = (bf16[2,64,2048]{2,1,0:T(8,128)(2,1)S(1)}, bf16[2,64,2048]{2,1,0:T(8,128)(2,1)}, u32[]{:S(2)}) copy-start(bf16[2,64,2048]{2,1,0:T(8,128)(2,1)} %copy-done.8) | copy-start | bytes 1572868
  117.9 202.0 %all-gather.7.cloned.1.call-start = ((), (), s32[]{:S(2)}) async-start(), calls=%async_computation.6 | async-start | bytes 8912896 | tf_op jit(solution)/shard_map/all_gather | solution.py:93
  202.2 12.7 %collective-permute-start.5 = (bf16[2,64,2048]{2,1,0:T(8,128)(2,1)S(1)}, bf16[2,64,2048]{2,1,0:T(8,128)(2,1)}, u32[]{:S(2)}, u32[]{:S(2)}) collective-permute-start(bf16[2,64,2048]{2,1,0:T(8,128)(2,1)S(1)} %bitcast.113), channel_id=1, source_target_pairs={{0,1},{1,2},{2,3},{3,0},{4,5},{5,6},{6,7},{7,4},{8,9},{9,10},{10,1... | collective-permute-start | bytes 1572872 | tf_op jit(solution)/shard_map/ppermute | solution.py:18
  203.6 23.8 %collective-permute-start.6 = (bf16[2,64,2048]{2,1,0:T(8,128)(2,1)S(1)}, bf16[2,64,2048]{2,1,0:T(8,128)(2,1)}, u32[]{:S(2)}, u32[]{:S(2)}) collective-permute-start(bf16[2,64,2048]{2,1,0:T(8,128)(2,1)S(1)} %bitcast.114), channel_id=1, source_target_pairs={{0,2},{1,3},{2,0},{3,1},{4,6},{5,7},{6,4},{7,5},{8,10},{9,11},{10,... | collective-permute-start | bytes 1572872 | tf_op jit(solution)/shard_map/ppermute | solution.py:18
  206.1 22.1 %collective-permute-start.7 = (bf16[2,64,2048]{2,1,0:T(8,128)(2,1)S(1)}, bf16[2,64,2048]{2,1,0:T(8,128)(2,1)}, u32[]{:S(2)}, u32[]{:S(2)}) collective-permute-start(bf16[2,64,2048]{2,1,0:T(8,128)(2,1)S(1)} %bitcast.115), channel_id=1, source_target_pairs={{0,3},{1,0},{2,1},{3,2},{4,7},{5,4},{6,5},{7,6},{8,11},{9,8},{10,9... | collective-permute-start | bytes 1572872 | tf_op jit(solution)/shard_map/ppermute | solution.py:18
  207.2 4.0 %collective-permute-start.8 = (f32[2,2,64,64]{3,2,1,0:T(8,128)S(1)}, f32[2,2,64,64]{3,2,1,0:T(8,128)S(1)}, u32[]{:S(2)}, u32[]{:S(2)}) collective-permute-start(f32[2,2,64,64]{3,2,1,0:T(8,128)S(1)} %copy-done.11), channel_id=1, source_target_pairs={{0,64},{64,0},{1,65},{65,1},{2,66},{66,2},{3,67},{67,3},{4,68},{68... | collective-permute-start | bytes 196616 | tf_op jit(solution)/shard_map/ppermute | solution.py:9
  242.2 58.0 %all-to-all-start.1 = ((bf16[16,144,512]{2,1,0:T(8,128)(2,1)}), bf16[16,144,512]{2,1,0:T(8,128)(2,1)S(1)}, u32[]{:S(2)}, u32[]{:S(2)}) async-start(bf16[16,144,512]{2,1,0:T(8,128)(2,1)} %pad_maximum_fusion), calls=%async_computation.2 | async-start | bytes 4718592 | tf_op jit(solution)/shard_map/all_to_all | solution.py:51
  246.5 64.0 %collective-permute-start.4 = (bf16[2048,512]{1,0:T(8,128)(2,1)}, bf16[2048,512]{1,0:T(8,128)(2,1)}, u32[]{:S(2)}, u32[]{:S(2)}) collective-permute-start(bf16[2048,512]{1,0:T(8,128)(2,1)} %bitcast.109), channel_id=1, source_target_pairs={{0,64},{64,0},{1,65},{65,1},{2,66},{66,2},{3,67},{67,3},{4,68},{68... | collective-permute-start | bytes 6291464 | tf_op jit(solution)/shard_map/ppermute | solution.py:9
  301.7 8.8 %collective-permute-start.9 = (bf16[2048,512]{1,0:T(8,128)(2,1)}, bf16[2048,512]{1,0:T(8,128)(2,1)}, u32[]{:S(2)}, u32[]{:S(2)}) collective-permute-start(bf16[2048,512]{1,0:T(8,128)(2,1)} %bitcast.36), channel_id=1, source_target_pairs={{0,64},{64,0},{1,65},{65,1},{2,66},{66,2},{3,67},{67,3},{4,68},{68... | collective-permute-start | bytes 6291464 | tf_op jit(solution)/shard_map/ppermute | solution.py:9
  304.1 4.1 %collective-permute-start.11 = (f32[2]{0:T(128)S(1)}, f32[2]{0:T(128)S(1)}, u32[]{:S(2)}, u32[]{:S(2)}) collective-permute-start(f32[2]{0:T(128)S(1)} %get-tuple-element.22), channel_id=1, source_target_pairs={{0,64},{64,0},{1,65},{65,1},{2,66},{66,2},{3,67},{67,3},{4,68},{68... | collective-permute-start | bytes 32 | tf_op jit(solution)/shard_map/ppermute | solution.py:9
  308.9 1.5 collective-permute-start.10
  327.7 10.5 %copy-start.1 = (bf16[2,2,64,2048]{3,2,1,0:T(8,128)(2,1)S(1)}, bf16[2,2,64,2048]{3,2,1,0:T(8,128)(2,1)}, u32[]{:S(2)}) copy-start(bf16[2,2,64,2048]{3,2,1,0:T(8,128)(2,1)} %param.11) | copy-start | bytes 3145732
  (6 other events, 36.7 us)
Sparse Core Ops, SparseCore 0:
  11.1 56.8 all-reduce.2
Sparse Core Ops, SparseCore 1:
  13.5 96.0 all-gather.4
  117.9 83.0 reduce-scatter.1
  203.0 96.3 all-gather.6

commit v13 on v3

--- a/solution.py
+++ b/solution.py
@@ -19,6 +19,26 @@
         )
     stacked = jnp.stack(pieces)
     return stacked, (position - jnp.arange(count)) % count
+
+
+def grid_gather(values, group_count):
+    columns = 4 if group_count % 4 == 0 else group_count
+    rows = group_count // columns
+    position = lax.axis_index("dp")
+
+    def along(piece, count, stride):
+        pieces = [piece]
+        for offset in range(1, count):
+            pairs = []
+            for source in range(group_count):
+                at = (source // stride) % count
+                pairs.append((source, source + (((at + offset) % count) - at) * stride))
+            pieces.append(lax.ppermute(piece, "dp", pairs))
+        order = ((position // stride) % count - jnp.arange(count)) % count
+        return jnp.take(jnp.stack(pieces), order, axis=0)
+
+    across = along(values, columns, 1)
+    return along(across, rows, columns).reshape((group_count,) + values.shape)
 
 
 def column_blocks(values, group_count, column_part):
@@ -82,8 +102,7 @@
     bound = clip_norm[0]
     own_scales = bound / jnp.maximum(jnp.sqrt(norm_square), bound)
     scale_terms = by_micro(is_last, own_scales, swapped(own_scales, "pipe"))
-    scale_pieces, scale_order = ring_pieces(scale_terms, "dp")
-    all_scales = jnp.take(scale_pieces, scale_order, axis=0).transpose(1, 0, 2)
+    all_scales = grid_gather(scale_terms, group_count).transpose(1, 0, 2)
 
     grad_blocks = jnp.where(
         is_last,
@@ -96,10 +115,14 @@
         )
         * all_scales[:, :, :, None, None]
     ).astype(jnp.bfloat16)
-    flat_inputs = gathered_inputs.reshape(micro_count * group_count * token_count, width_part)
-    flat_grads = scaled_blocks.reshape(micro_count * group_count * token_count, column_part)
-    summed_grad = lax.dot_general(
-        flat_inputs, flat_grads, (((0,), (0,)), ((), ())), preferred_element_type=jnp.float32
+    summed_grad = sum(
+        lax.dot_general(
+            gathered_inputs[index].reshape(group_count * token_count, width_part),
+            scaled_blocks[index].reshape(group_count * token_count, column_part),
+            (((0,), (0,)), ((), ())),
+            preferred_element_type=jnp.float32,
+        )
+        for index in range(micro_count)
     )
     noise_weight = 1.5 / full_width
     per_example_sum = micro_count * group_count * example_count

time: 344 us -> 346 us (level)
  starting transfers between devices: 65.4 us -> 30.8 us
  waiting for transfers between devices: 177 us -> 210 us
  local copies, waits for them, and re-layouts: 31.4 us -> 41.3 us
  matrix products: 32.4 us -> 27.4 us
    all_to_all x2, waiting for transfers between devices: 28 us -> 74.6 us  [column_blocks(): lax.all_to_all(chunks, 'dp', split_axis=0, concat_axis=1, tiled=True)]
    ppermute x21 -> x6, starting transfers between devices: 40.1 us -> 9.1 us  [ring_pieces(): lax.ppermute(values, axis, [(source, (source + offset) % count) for sourc...]
    ppermute x21 -> x6, waiting for transfers between devices: 60.3 us -> 39.7 us  [ring_pieces(): lax.ppermute(values, axis, [(source, (source + offset) % count) for sourc...]
    slice x0 -> x2, local copies, waits for them, and re-layouts: none -> 8.55 us  [the longest x1 6.7 us: local(): gathered_inputs[index].reshape(group_count * token_count, width_part)]
    ppermute x0 -> x6, waiting for transfers between devices: none -> 7.96 us  [along(): pieces.append(lax.ppermute(piece, 'dp', pairs))]
    ppermute x5, starting transfers between devices: 13.6 us -> 6.43 us  [swapped(): lax.ppermute(value, axis, [(source, count - 1 - source) for source in ran...]
    all_gather x1, waiting for transfers between devices: 8.5 us -> 3.73 us  [local(): gathered_inputs = lax.all_gather(local_inputs, 'dp', axis=1, tiled=True)]
    dot_general x1 -> x2, matrix products: 15.3 us -> 10.8 us  [local(): lax.dot_general(gathered_inputs[index].reshape(group_count * token_count,...]
  transfers between devices with their start and end apart: 31 -> 22, of which waited for: 12 -> 17; matrix products, arithmetic and copies ran while one was open for 15% -> 16% of each run, Pallas kernels for 0% -> 0%
where the time goes in v13:
time: 346 us; the launch traced here: 345 us
  waiting for transfers between devices  210 us (61%)
  local copies, waits for them, and re-layouts  41.3 us (12%)
  starting transfers between devices  30.8 us (9%)
  matrix products  27.4 us (8%)
  other arithmetic  18.9 us (5%)
  between operations  16.4 us (5%)
    reduce_scatter x1, waiting for transfers between devices, local(): lax.psum_scatter(terms, 'dp', scatter_dimension=0, tiled=True)  78.8 us
    all_to_all x2, waiting for transfers between devices, column_blocks(): lax.all_to_all(chunks, 'dp', split_axis=0, concat_axis=1, tiled=True)  74.6 us
    ppermute x6, waiting for transfers between devices, ring_pieces(): lax.ppermute(values, axis, [(source, (source + offset) % count) for sourc...  39.7 us
    another operation x16, local copies, waits for them, and re-layouts, ring_pieces(): stacked = jnp.stack(pieces)  12.9 us
    all_to_all x2, starting transfers between devices, column_blocks(): lax.all_to_all(chunks, 'dp', split_axis=0, concat_axis=1, tiled=True)  11.5 us
    dot_general x2, matrix products, local(): lax.dot_general(gathered_inputs[index].reshape(group_count * token_count,...  10.8 us
    unnamed x23, local copies, waits for them, and re-layouts  10.7 us
    ppermute x6, starting transfers between devices, ring_pieces(): lax.ppermute(values, axis, [(source, (source + offset) % count) for sourc...  9.1 us
  transfers between devices with their start and end apart: 22, of which 17 were waited for; matrix products, arithmetic and copies ran while one was open for 16% of the time, Pallas kernels for 0%

profile of v13, /device:TPU:1, one launch (start us, length us, event | category | flops | bytes accessed | tf_op | source)
XLA Modules:
  0.0 345.0 jit_solution(9460140735058155875)
XLA Ops:
  10.1 4.6 %collective-permute-start.2 = (bf16[2,64,2048]{2,1,0:T(8,128)(2,1)}, bf16[2,64,2048]{2,1,0:T(8,128)(2,1)S(1)}, u32[]{:S(2)}, u32[]{:S(2)}) collective-permute-start(bf16[2,64,2048]{2,1,0:T(8,128)(2,1)} %fusion.55), channel_id=1, source_target_pairs={{0,3},{1,0},{2,1},{3,2},{4,7},{5,4},{6,5},{7,6},{8,11},{9,8},{10,9... | collective-permute-start | bytes 1572872 | tf_op jit(solution)/shard_map/ppermute | solution.py:18
  18.3 18.4 %collective-permute-done.2 = bf16[2,64,2048]{2,1,0:T(8,128)(2,1)S(1)} collective-permute-done((bf16[2,64,2048]{2,1,0:T(8,128)(2,1)}, bf16[2,64,2048]{2,1,0:T(8,128)(2,1)S(1)}, u32[]{:S(2)}, u32[]{:S(2)}) %collective-permute-start.2) | collective-permute-done | bytes 524320 | tf_op jit(solution)/shard_map/ppermute | solution.py:18
  46.1 3.2 broadcast_select_fusion.1
  49.3 6.8 %all-to-all-start = ((bf16[16,128,512]{2,1,0:T(8,128)(2,1)}), bf16[16,128,512]{2,1,0:T(8,128)(2,1)S(1)}, u32[]{:S(2)}, u32[]{:S(2)}) async-start(bf16[16,128,512]{2,1,0:T(8,128)(2,1)} %bitcast.117), calls=%async_computation | async-start | bytes 4194304 | tf_op jit(solution)/shard_map/all_to_all | solution.py:53
  56.1 30.3 %all-to-all-done = bf16[16,128,512]{2,1,0:T(8,128)(2,1)S(1)} async-done(((bf16[16,128,512]{2,1,0:T(8,128)(2,1)}), bf16[16,128,512]{2,1,0:T(8,128)(2,1)S(1)}, u32[]{:S(2)}, u32[]{:S(2)}) %all-to-all-start) | async-done | bytes 2097184 | tf_op jit(solution)/shard_map/all_to_all | solution.py:53
  86.4 8.4 %convolution_convert_fusion = bf16[2048,2048]{1,0:T(8,128)(2,1)} fusion(bf16[2048,512]{1,0:T(8,128)(2,1)S(1)} %bitcast.113, bf16[2048,512]{1,0:T(8,128)(2,1)} %collective-permute-done.4, pred[]{:T(512)S(6)} %eq.11, bf16[1,2048,512]{2,1,0:T(8,128)(2,1)} %param.7), kind=kOutput, calls=%fused_computation.5 | convolution fusion | flops 4300210176 | bytes 14680065 | tf_op jit(solution)/shard_map/dot_general | solution.py:85
  99.2 78.8 %reduce-scatter.2.cloned.1.call-done = bf16[128,2048]{1,0:T(8,128)(2,1)} async-done(((bf16[2048,2048]{1,0:T(8,128)(2,1)}), bf16[128,2048]{1,0:T(8,128)(2,1)}) %reduce-scatter.2.cloned.1.call-update) | async-done | bytes 524304 | tf_op jit(solution)/shard_map/reduce_scatter | solution.py:88
  179.3 2.7 collective-permute-start.7
  184.5 7.8 %collective-permute-done.7 = bf16[2,64,2048]{2,1,0:T(8,128)(2,1)} collective-permute-done((bf16[2,64,2048]{2,1,0:T(8,128)(2,1)S(1)}, bf16[2,64,2048]{2,1,0:T(8,128)(2,1)}, u32[]{:S(2)}, u32[]{:S(2)}) %collective-permute-start.7) | collective-permute-done | bytes 524320 | tf_op jit(solution)/shard_map/ppermute | solution.py:18
  197.2 11.5 %collective-permute-done.5 = bf16[2,64,2048]{2,1,0:T(8,128)(2,1)} collective-permute-done((bf16[2,64,2048]{2,1,0:T(8,128)(2,1)S(1)}, bf16[2,64,2048]{2,1,0:T(8,128)(2,1)}, u32[]{:S(2)}, u32[]{:S(2)}) %collective-permute-start.5) | collective-permute-done | bytes 524320 | tf_op jit(solution)/shard_map/ppermute | solution.py:18
  210.3 2.9 maximum_bitcast_fusion.1
  213.2 3.6 %gather_fusion.3 = bf16[4,4,128,512]{3,2,1,0:T(8,128)(2,1)} fusion(bf16[4,4,128,512]{3,2,1,0:T(8,128)(2,1)} %maximum_bitcast_fusion.1, s32[1024]{0:T(1024)S(1)} %pad_clamp_fusion.2), kind=kCustom, calls=%fused_computation.1.clone | custom fusion | bytes 4194320 | tf_op jit(solution)/shard_map/jit(_take)/gather | solution.py:52
  216.9 3.2 broadcast_select_fusion
  220.1 4.7 %all-to-all-start.1 = ((bf16[16,128,512]{2,1,0:T(8,128)(2,1)}), bf16[16,128,512]{2,1,0:T(8,128)(2,1)}, u32[]{:S(2)}, u32[]{:S(2)}) async-start(bf16[16,128,512]{2,1,0:T(8,128)(2,1)} %bitcast.116), calls=%async_computation.2 | async-start | bytes 4194304 | tf_op jit(solution)/shard_map/all_to_all | solution.py:53
  225.7 4.0 %copy.76 = bf16[1,2048,512]{1,2,0:T(8,128)(2,1)} copy(bf16[1,2048,512]{2,1,0:T(8,128)(2,1)} %param.11) | data formatting | bytes 4194304 | tf_op args[4]
  231.5 44.3 %all-to-all-done.1 = bf16[16,128,512]{2,1,0:T(8,128)(2,1)} async-done(((bf16[16,128,512]{2,1,0:T(8,128)(2,1)}), bf16[16,128,512]{2,1,0:T(8,128)(2,1)}, u32[]{:S(2)}, u32[]{:S(2)}) %all-to-all-start.1) | async-done | bytes 2097184 | tf_op jit(solution)/shard_map/all_to_all | solution.py:53
  278.5 3.8 %collective-permute-done.9 = f32[2,2,64,64]{3,2,1,0:T(8,128)S(1)} collective-permute-done((f32[2,2,64,64]{3,2,1,0:T(8,128)}, f32[2,2,64,64]{3,2,1,0:T(8,128)S(1)}, u32[]{:S(2)}, u32[]{:S(2)}) %collective-permute-start.9) | collective-permute-done | bytes 65568 | tf_op jit(solution)/shard_map/ppermute | solution.py:9
  282.3 2.9 fusion.30
  302.6 6.4 %multiply_convert_fusion = bf16[2,16,2,64,512]{4,3,2,1,0:T(8,128)(2,1)S(1)} fusion(bf16[1,16,2,64,512]{4,3,2,1,0:T(8,128)(2,1)S(1)} %bitcast.115, bf16[1,16,2,64,512]{4,3,2,1,0:T(8,128)(2,1)} %bitcast.4, bf16[1,16,2,64,512]{4,3,2,1,0:T(8,128)(2,1)} %bitcast.13, bf16[1,16,2,64,512]{4,3,2,1,0:T(8,128)(2,1)} %bitcast.12, f32[2,16,2]{2,1,0:T(8,128)S(1)} %copy.75, ...), kind=kLoop, calls=%fused_computation.4 | loop fusion | flops 20971520 | bytes 12583169 | tf_op jit(solution)/shard_map/convert_element_type | solution.py:117
  310.9 3.7 %all-gather.3.cloned.1.call-done = bf16[1,2,32,64,2048]{4,3,2,1,0:T(8,128)(2,1)} async-done(((bf16[1,2,2,64,2048]{4,3,2,1,0:T(8,128)(2,1)}), bf16[1,2,32,64,2048]{4,3,2,1,0:T(8,128)(2,1)}) %all-gather.3.cloned.1.call-update) | async-done | bytes 16777232 | tf_op jit(solution)/shard_map/all_gather | solution.py:76
  314.6 6.7 %fusion.46 = (bf16[1,1,32,64,2048]{4,3,2,1,0:T(8,128)(2,1)S(1)}, bf16[1,1,32,64,2048]{4,3,2,1,0:T(8,128)(2,1)S(1)}) fusion(bf16[1,2,32,64,2048]{4,3,2,1,0:T(8,128)(2,1)} %all-gather.3.cloned.1.call-done), kind=kLoop, calls=%fused_computation.89 | loop fusion | bytes 33554432 | tf_op jit(solution)/shard_map/slice | solution.py:120
  321.3 4.6 %fusion.48 = f32[512,2048]{1,0:T(8,128)S(1)} fusion(bf16[2048,512]{1,0:T(8,128)(2,1)S(1)} %bitcast.123, bf16[2048,2048]{1,0:T(8,128)(2,1)S(1)} %bitcast.118), kind=kOutput, calls=%fused_computation.91 | convolution fusion | flops 4294967296 | bytes 14680064 | tf_op jit(solution)/shard_map/dot_general | solution.py:119
  325.9 6.2 %fusion.2 = f32[1,2048,512]{1,2,0:T(8,128)} fusion(bf16[1,2048,512]{1,2,0:T(8,128)(2,1)S(1)} %copy-done.2, f32[512,2048]{1,0:T(8,128)S(1)} %fusion.48, bf16[2048,512]{1,0:T(8,128)(2,1)S(1)} %bitcast.112, bf16[2048,2048]{1,0:T(8,128)(2,1)S(1)} %bitcast.111, f32[]{:T(128)S(6)} %mul_shard_map.3), kind=kOutput, calls=%fused_computation.11 | convolution fusion | flops 4300210176 | bytes 20971524 | tf_op jit(solution)/shard_map/dot_general | solution.py:119
  332.2 5.4 %copy.77 = f32[1,2048,512]{2,1,0:T(8,128)} copy(f32[1,2048,512]{1,2,0:T(8,128)} %fusion.2) | data formatting | bytes 8388608
  (107 shorter events, 53.5 us)
Async XLA Ops:
  10.1 26.6 %collective-permute-start.2 = (bf16[2,64,2048]{2,1,0:T(8,128)(2,1)}, bf16[2,64,2048]{2,1,0:T(8,128)(2,1)S(1)}, u32[]{:S(2)}, u32[]{:S(2)}) collective-permute-start(bf16[2,64,2048]{2,1,0:T(8,128)(2,1)} %fusion.55), channel_id=1, source_target_pairs={{0,3},{1,0},{2,1},{3,2},{4,7},{5,4},{6,5},{7,6},{8,11},{9,8},{10,9... | collective-permute-start | bytes 1572872 | tf_op jit(solution)/shard_map/ppermute | solution.py:18
  14.6 23.3 %collective-permute-start.1 = (bf16[2,64,2048]{2,1,0:T(8,128)(2,1)}, bf16[2,64,2048]{2,1,0:T(8,128)(2,1)S(1)}, u32[]{:S(2)}, u32[]{:S(2)}) collective-permute-start(bf16[2,64,2048]{2,1,0:T(8,128)(2,1)} %fusion.55), channel_id=1, source_target_pairs={{0,2},{1,3},{2,0},{3,1},{4,6},{5,7},{6,4},{7,5},{8,10},{9,11},{10,... | collective-permute-start | bytes 1572872 | tf_op jit(solution)/shard_map/ppermute | solution.py:18
  14.6 26.3 %collective-permute-start = (bf16[2,64,2048]{2,1,0:T(8,128)(2,1)}, bf16[2,64,2048]{2,1,0:T(8,128)(2,1)}, u32[]{:S(2)}, u32[]{:S(2)}) collective-permute-start(bf16[2,64,2048]{2,1,0:T(8,128)(2,1)} %fusion.55), channel_id=1, source_target_pairs={{0,1},{1,2},{2,3},{3,0},{4,5},{5,6},{6,7},{7,4},{8,9},{9,10},{10,1... | collective-permute-start | bytes 1572872 | tf_op jit(solution)/shard_map/ppermute | solution.py:18
  15.3 40.8 %collective-permute-start.4 = (bf16[2048,512]{1,0:T(8,128)(2,1)}, bf16[2048,512]{1,0:T(8,128)(2,1)}, u32[]{:S(2)}, u32[]{:S(2)}) collective-permute-start(bf16[2048,512]{1,0:T(8,128)(2,1)} %bitcast.136), channel_id=1, source_target_pairs={{0,64},{64,0},{1,65},{65,1},{2,66},{66,2},{3,67},{67,3},{4,68},{68... | collective-permute-start | bytes 6291464 | tf_op jit(solution)/shard_map/ppermute | solution.py:9
  16.9 21.0 %copy-start.3 = (bf16[1,2,64,2048]{3,2,0,1:T(8,128)(2,1)}, bf16[1,2,64,2048]{3,2,0,1:T(8,128)(2,1)S(1)}, u32[]{:S(2)}) copy-start(bf16[1,2,64,2048]{3,2,0,1:T(8,128)(2,1)S(1)} %fusion.54) | copy-start | bytes 1572868
  49.3 37.1 %all-to-all-start = ((bf16[16,128,512]{2,1,0:T(8,128)(2,1)}), bf16[16,128,512]{2,1,0:T(8,128)(2,1)S(1)}, u32[]{:S(2)}, u32[]{:S(2)}) async-start(bf16[16,128,512]{2,1,0:T(8,128)(2,1)} %bitcast.117), calls=%async_computation | async-start | bytes 4194304 | tf_op jit(solution)/shard_map/all_to_all | solution.py:53
  56.1 121.9 %reduce-scatter.2.cloned.1.call-start = ((), (), s32[]{:S(2)}) async-start(), calls=%async_computation.3 | async-start | bytes 8912896 | tf_op jit(solution)/shard_map/reduce_scatter | solution.py:88
  94.9 183.3 %all-reduce.2.cloned.1.call-start = ((), (), s32[]{:S(2)}) async-start(), calls=%async_computation.4 | async-start | bytes 262144 | tf_op jit(solution)/shard_map/psum | solution.py:77
  97.6 217.0 %all-gather.3.cloned.1.call-start = ((), (), s32[]{:S(2)}) async-start(), calls=%async_computation.5 | async-start | bytes 17825792 | tf_op jit(solution)/shard_map/all_gather | solution.py:76
  179.3 12.9 %collective-permute-start.7 = (bf16[2,64,2048]{2,1,0:T(8,128)(2,1)S(1)}, bf16[2,64,2048]{2,1,0:T(8,128)(2,1)}, u32[]{:S(2)}, u32[]{:S(2)}) collective-permute-start(bf16[2,64,2048]{2,1,0:T(8,128)(2,1)S(1)} %bitcast.119), channel_id=1, source_target_pairs={{0,3},{1,0},{2,1},{3,2},{4,7},{5,4},{6,5},{7,6},{8,11},{9,8},{10,9... | collective-permute-start | bytes 1572872 | tf_op jit(solution)/shard_map/ppermute | solution.py:18
  182.1 12.8 %collective-permute-start.6 = (bf16[2,64,2048]{2,1,0:T(8,128)(2,1)S(1)}, bf16[2,64,2048]{2,1,0:T(8,128)(2,1)}, u32[]{:S(2)}, u32[]{:S(2)}) collective-permute-start(bf16[2,64,2048]{2,1,0:T(8,128)(2,1)S(1)} %bitcast.120), channel_id=1, source_target_pairs={{0,2},{1,3},{2,0},{3,1},{4,6},{5,7},{6,4},{7,5},{8,10},{9,11},{10,... | collective-permute-start | bytes 1572872 | tf_op jit(solution)/shard_map/ppermute | solution.py:18
  182.5 26.3 %collective-permute-start.5 = (bf16[2,64,2048]{2,1,0:T(8,128)(2,1)S(1)}, bf16[2,64,2048]{2,1,0:T(8,128)(2,1)}, u32[]{:S(2)}, u32[]{:S(2)}) collective-permute-start(bf16[2,64,2048]{2,1,0:T(8,128)(2,1)S(1)} %bitcast.121), channel_id=1, source_target_pairs={{0,1},{1,2},{2,3},{3,0},{4,5},{5,6},{6,7},{7,4},{8,9},{9,10},{10,1... | collective-permute-start | bytes 1572872 | tf_op jit(solution)/shard_map/ppermute | solution.py:18
  220.1 55.6 %all-to-all-start.1 = ((bf16[16,128,512]{2,1,0:T(8,128)(2,1)}), bf16[16,128,512]{2,1,0:T(8,128)(2,1)}, u32[]{:S(2)}, u32[]{:S(2)}) async-start(bf16[16,128,512]{2,1,0:T(8,128)(2,1)} %bitcast.116), calls=%async_computation.2 | async-start | bytes 4194304 | tf_op jit(solution)/shard_map/all_to_all | solution.py:53
  225.7 56.6 %copy-start.4 = (bf16[1,2,64,2048]{3,2,0,1:T(8,128)(2,1)S(1)}, bf16[1,2,64,2048]{3,2,0,1:T(8,128)(2,1)}, u32[]{:S(2)}) copy-start(bf16[1,2,64,2048]{3,2,0,1:T(8,128)(2,1)} %copy-done.3) | copy-start | bytes 1572868
  229.7 72.9 %collective-permute-start.3 = (bf16[2048,512]{1,0:T(8,128)(2,1)S(1)}, bf16[2048,512]{1,0:T(8,128)(2,1)}, u32[]{:S(2)}, u32[]{:S(2)}) collective-permute-start(bf16[2048,512]{1,0:T(8,128)(2,1)S(1)} %bitcast.114), channel_id=1, source_target_pairs={{0,64},{64,0},{1,65},{65,1},{2,66},{66,2},{3,67},{67,3},{4,68},{68... | collective-permute-start | bytes 6291464 | tf_op jit(solution)/shard_map/ppermute | solution.py:9
  275.7 26.9 %collective-permute-start.8 = (bf16[2048,512]{1,0:T(8,128)(2,1)}, bf16[2048,512]{1,0:T(8,128)(2,1)}, u32[]{:S(2)}, u32[]{:S(2)}) collective-permute-start(bf16[2048,512]{1,0:T(8,128)(2,1)} %bitcast.11), channel_id=1, source_target_pairs={{0,64},{64,0},{1,65},{65,1},{2,66},{66,2},{3,67},{67,3},{4,68},{68... | collective-permute-start | bytes 6291464 | tf_op jit(solution)/shard_map/ppermute | solution.py:9
  278.2 4.1 %collective-permute-start.9 = (f32[2,2,64,64]{3,2,1,0:T(8,128)}, f32[2,2,64,64]{3,2,1,0:T(8,128)S(1)}, u32[]{:S(2)}, u32[]{:S(2)}) collective-permute-start(f32[2,2,64,64]{3,2,1,0:T(8,128)} %all-reduce.2.cloned.1.call-done), channel_id=1, source_target_pairs={{0,64},{64,0},{1,65},{65,1},{2,66},{66,2},{3,67},{67,3},{4,68},{68... | collective-permute-start | bytes 196616 | tf_op jit(solution)/shard_map/ppermute | solution.py:9
  287.9 1.3 collective-permute-start.10
  289.2 3.0 collective-permute-start.13
  289.3 4.2 %collective-permute-start.12 = (f32[2,2]{1,0:T(2,128)S(1)}, f32[2,2]{1,0:T(2,128)S(1)}, u32[]{:S(2)}, u32[]{:S(2)}) collective-permute-start(f32[2,2]{1,0:T(2,128)S(1)} %maximum_select_fusion.3), channel_id=1, source_target_pairs={{0,8},{4,12},{8,0},{12,4},{16,24},{20,28},{24,16},{28,20},{32,40},... | collective-permute-start | bytes 56 | tf_op jit(solution)/shard_map/ppermute | solution.py:36
  291.3 4.2 %collective-permute-start.11 = (f32[2,2]{1,0:T(2,128)S(1)}, f32[2,2]{1,0:T(2,128)S(1)}, u32[]{:S(2)}, u32[]{:S(2)}) collective-permute-start(f32[2,2]{1,0:T(2,128)S(1)} %maximum_select_fusion.3), channel_id=1, source_target_pairs={{0,4},{4,8},{8,12},{12,0},{16,20},{20,24},{24,28},{28,16},{32,36},... | collective-permute-start | bytes 56 | tf_op jit(solution)/shard_map/ppermute | solution.py:36
  296.3 3.1 collective-permute-start.16
  296.9 4.2 %collective-permute-start.15 = (f32[4,2,2]{2,1,0:T(2,128)S(1)}, f32[4,2,2]{2,1,0:T(2,128)S(1)}, u32[]{:S(2)}, u32[]{:S(2)}) collective-permute-start(f32[4,2,2]{2,1,0:T(2,128)S(1)} %broadcast_select_fusion.2), channel_id=1, source_target_pairs={{0,32},{4,36},{8,40},{12,44},{16,48},{20,52},{24,56},{28,60},{32,0... | collective-permute-start | bytes 200 | tf_op jit(solution)/shard_map/ppermute | solution.py:36
  297.2 4.6 %collective-permute-start.14 = (f32[4,2,2]{2,1,0:T(2,128)S(1)}, f32[4,2,2]{2,1,0:T(2,128)S(1)}, u32[]{:S(2)}, u32[]{:S(2)}) collective-permute-start(f32[4,2,2]{2,1,0:T(2,128)S(1)} %broadcast_select_fusion.2), channel_id=1, source_target_pairs={{0,16},{4,20},{8,24},{12,28},{16,32},{20,36},{24,40},{28,44},{32,4... | collective-permute-start | bytes 200 | tf_op jit(solution)/shard_map/ppermute | solution.py:36
  (8 other events, 47.7 us)
Sparse Core Ops, SparseCore 0:
  95.0 82.9 reduce-scatter.1
  180.2 134.3 all-gather.2
Sparse Core Ops, SparseCore 1:
  97.6 38.1 all-reduce.1

commit v14 on v13

--- a/solution.py
+++ b/solution.py
@@ -41,7 +41,7 @@
     return along(across, rows, columns).reshape((group_count,) + values.shape)
 
 
-def column_blocks(values, group_count, column_part):
+def column_blocks(values, group_count, column_part, before_send=None):
     example_count, length_count, width_part = values.shape
     token_count = example_count * length_count
     stacked, order = ring_pieces(values, "tensor")
@@ -50,8 +50,12 @@
     per_piece = width_part // column_part
     chunks = stacked.reshape(pieces, token_count, per_piece, column_part).transpose(0, 2, 1, 3)
     chunks = jnp.take(chunks, order, axis=0).reshape(pieces * per_piece, token_count, column_part)
+    extra = None
+    if before_send is not None:
+        extra = before_send(grams)
+        chunks, extra = lax.optimization_barrier((chunks, extra))
     moved = lax.all_to_all(chunks, "dp", split_axis=0, concat_axis=1, tiled=True)
-    return grams, moved.reshape(group_count * token_count, column_part)
+    return grams, moved.reshape(group_count * token_count, column_part), extra
 
 
 def token_grams(values):
@@ -78,7 +82,7 @@
     other_input_grams = swapped(input_grams, "pipe")
 
     own_cotangent = lax.dynamic_index_in_dim(cotangent, section_index, 0, keepdims=False)
-    last_grams, last_blocks = column_blocks(own_cotangent, group_count, column_part)
+    last_grams, last_blocks, _ = column_blocks(own_cotangent, group_count, column_part)
     last_blocks_other = swapped(last_blocks, "pipe")
 
     last_weights = jnp.where(is_last, weight_block, swapped(weight_block, "pipe"))
@@ -89,20 +93,22 @@
     renewed = (own_cotangent.reshape(token_count, width_part).astype(jnp.float32) + summed).astype(
         jnp.bfloat16
     ).reshape(example_count, length_count, width_part)
-    first_grams, first_blocks = column_blocks(renewed, group_count, column_part)
-    first_blocks_other = swapped(first_blocks, "pipe")
-
     own_input_grams = lax.dynamic_index_in_dim(input_grams, section_index, 0, keepdims=False)
     held_input_grams = lax.dynamic_index_in_dim(other_input_grams, section_index, 0, keepdims=False)
     last_input_grams = jnp.where(is_last, own_input_grams, held_input_grams)
     first_input_grams = jnp.where(is_last, held_input_grams, own_input_grams)
-    norm_square = jnp.sum(first_input_grams * first_grams, axis=(1, 2)) + jnp.sum(
-        last_input_grams * last_grams, axis=(1, 2)
-    )
     bound = clip_norm[0]
-    own_scales = bound / jnp.maximum(jnp.sqrt(norm_square), bound)
-    scale_terms = by_micro(is_last, own_scales, swapped(own_scales, "pipe"))
-    all_scales = grid_gather(scale_terms, group_count).transpose(1, 0, 2)
+
+    def clip_factors(first_grams):
+        norm_square = jnp.sum(first_input_grams * first_grams, axis=(1, 2)) + jnp.sum(
+            last_input_grams * last_grams, axis=(1, 2)
+        )
+        own_scales = bound / jnp.maximum(jnp.sqrt(norm_square), bound)
+        scale_terms = by_micro(is_last, own_scales, swapped(own_scales, "pipe"))
+        return scale_terms, grid_gather(scale_terms, group_count).transpose(1, 0, 2)
+
+    _, first_blocks, (scale_terms, all_scales) = column_blocks(renewed, group_count, column_part, clip_factors)
+    first_blocks_other = swapped(first_blocks, "pipe")
 
     grad_blocks = jnp.where(
         is_last,

time: 346 us -> 346 us (level)
  waiting for transfers between devices: 210 us -> 203 us
  starting transfers between devices: 30.8 us -> 37.4 us
    ppermute x6, waiting for transfers between devices: 39.7 us -> 32.4 us  [ring_pieces(): lax.ppermute(values, axis, [(source, (source + offset) % count) for sourc...]
    ppermute x5, starting transfers between devices: 6.43 us -> 12.3 us  [swapped(): lax.ppermute(value, axis, [(source, count - 1 - source) for source in ran...]
    all_to_all x2, waiting for transfers between devices: 74.6 us -> 78.1 us  [column_blocks(): lax.all_to_all(chunks, 'dp', split_axis=0, concat_axis=1, tiled=True)]
  transfers between devices with their start and end apart: 22 -> 22, of which waited for: 17 -> 16; matrix products, arithmetic and copies ran while one was open for 16% -> 16% of each run, Pallas kernels for 0% -> 0%
where the time goes in v14:
time: 346 us; the launch traced here: 345 us
  waiting for transfers between devices  203 us (59%)
  local copies, waits for them, and re-layouts  41.2 us (12%)
  starting transfers between devices  37.4 us (11%)
  matrix products  27.6 us (8%)
  other arithmetic  19.3 us (6%)
  between operations  16.4 us (5%)
    all_to_all x2, waiting for transfers between devices, column_blocks(): lax.all_to_all(chunks, 'dp', split_axis=0, concat_axis=1, tiled=True)  78.1 us
    reduce_scatter x1, waiting for transfers between devices, local(): lax.psum_scatter(terms, 'dp', scatter_dimension=0, tiled=True)  77.9 us
    ppermute x6, waiting for transfers between devices, ring_pieces(): lax.ppermute(values, axis, [(source, (source + offset) % count) for sourc...  32.4 us
    another operation x16, local copies, waits for them, and re-layouts, ring_pieces(): stacked = jnp.stack(pieces)  12.8 us
    ppermute x5, starting transfers between devices, swapped(): lax.ppermute(value, axis, [(source, count - 1 - source) for source in ran...  12.3 us
    all_to_all x2, starting transfers between devices, column_blocks(): lax.all_to_all(chunks, 'dp', split_axis=0, concat_axis=1, tiled=True)  11.2 us
    dot_general x2, matrix products, local(): lax.dot_general(gathered_inputs[index].reshape(group_count * token_count,...  10.8 us
    unnamed x23, local copies, waits for them, and re-layouts  10.6 us
  transfers between devices with their start and end apart: 22, of which 16 were waited for; matrix products, arithmetic and copies ran while one was open for 16% of the time, Pallas kernels for 0%

profile of v14, /device:TPU:1, one launch (start us, length us, event | category | flops | bytes accessed | tf_op | source)
XLA Modules:
  0.0 345.0 jit_solution(14576714164280047906)
XLA Ops:
  10.1 4.6 %collective-permute-start.2 = (bf16[2,64,2048]{2,1,0:T(8,128)(2,1)}, bf16[2,64,2048]{2,1,0:T(8,128)(2,1)S(1)}, u32[]{:S(2)}, u32[]{:S(2)}) collective-permute-start(bf16[2,64,2048]{2,1,0:T(8,128)(2,1)} %fusion.55), channel_id=1, source_target_pairs={{0,3},{1,0},{2,1},{3,2},{4,7},{5,4},{6,5},{7,6},{8,11},{9,8},{10,9... | collective-permute-start | bytes 1572872 | tf_op jit(solution)/shard_map/ppermute | solution.py:18
  18.3 18.4 %collective-permute-done.2 = bf16[2,64,2048]{2,1,0:T(8,128)(2,1)S(1)} collective-permute-done((bf16[2,64,2048]{2,1,0:T(8,128)(2,1)}, bf16[2,64,2048]{2,1,0:T(8,128)(2,1)S(1)}, u32[]{:S(2)}, u32[]{:S(2)}) %collective-permute-start.2) | collective-permute-done | bytes 524320 | tf_op jit(solution)/shard_map/ppermute | solution.py:18
  46.1 3.2 broadcast_select_fusion.1
  49.3 6.8 %all-to-all-start = ((bf16[16,128,512]{2,1,0:T(8,128)(2,1)}), bf16[16,128,512]{2,1,0:T(8,128)(2,1)S(1)}, u32[]{:S(2)}, u32[]{:S(2)}) async-start(bf16[16,128,512]{2,1,0:T(8,128)(2,1)} %bitcast.117), calls=%async_computation | async-start | bytes 4194304 | tf_op jit(solution)/shard_map/all_to_all | solution.py:57
  56.1 30.3 %all-to-all-done = bf16[16,128,512]{2,1,0:T(8,128)(2,1)S(1)} async-done(((bf16[16,128,512]{2,1,0:T(8,128)(2,1)}), bf16[16,128,512]{2,1,0:T(8,128)(2,1)S(1)}, u32[]{:S(2)}, u32[]{:S(2)}) %all-to-all-start) | async-done | bytes 2097184 | tf_op jit(solution)/shard_map/all_to_all | solution.py:57
  86.4 8.4 %convolution_convert_fusion = bf16[2048,2048]{1,0:T(8,128)(2,1)} fusion(bf16[2048,512]{1,0:T(8,128)(2,1)S(1)} %bitcast.113, bf16[2048,512]{1,0:T(8,128)(2,1)} %collective-permute-done.4, pred[]{:T(512)S(6)} %eq.11, bf16[1,2048,512]{2,1,0:T(8,128)(2,1)} %param.7), kind=kOutput, calls=%fused_computation.5 | convolution fusion | flops 4300210176 | bytes 14680065 | tf_op jit(solution)/shard_map/dot_general | solution.py:89
  100.0 77.9 %reduce-scatter.2.cloned.1.call-done = bf16[128,2048]{1,0:T(8,128)(2,1)} async-done(((bf16[2048,2048]{1,0:T(8,128)(2,1)}), bf16[128,2048]{1,0:T(8,128)(2,1)}) %reduce-scatter.2.cloned.1.call-update) | async-done | bytes 524304 | tf_op jit(solution)/shard_map/reduce_scatter | solution.py:92
  183.1 3.1 collective-permute-start.8
  187.4 3.1 fusion.30
  197.1 11.6 %collective-permute-done.5 = bf16[2,64,2048]{2,1,0:T(8,128)(2,1)} collective-permute-done((bf16[2,64,2048]{2,1,0:T(8,128)(2,1)S(1)}, bf16[2,64,2048]{2,1,0:T(8,128)(2,1)}, u32[]{:S(2)}, u32[]{:S(2)}) %collective-permute-start.5) | collective-permute-done | bytes 524320 | tf_op jit(solution)/shard_map/ppermute | solution.py:18
  214.6 2.8 maximum_bitcast_fusion.1
  217.4 3.6 %gather_fusion.3 = bf16[4,4,128,512]{3,2,1,0:T(8,128)(2,1)} fusion(bf16[4,4,128,512]{3,2,1,0:T(8,128)(2,1)} %maximum_bitcast_fusion.1, s32[1024]{0:T(1024)S(1)} %pad_clamp_fusion.2), kind=kCustom, calls=%fused_computation.1.clone | custom fusion | bytes 4194320 | tf_op jit(solution)/shard_map/jit(_take)/gather | solution.py:52
  221.0 3.8 %broadcast_select_fusion = bf16[4,4,128,512]{3,2,1,0:T(8,128)(2,1)} fusion(bf16[4,4,128,512]{3,2,1,0:T(8,128)(2,1)} %gather_fusion.3, pred[4]{0:T(512)(128)(4,1)S(1)} %get-tuple-element.21), kind=kLoop, calls=%fused_computation.31 | loop fusion | flops 1048576 | bytes 4194308 | tf_op jit(solution)/shard_map/jit(_take)/select_n | solution.py:52
  228.0 3.0 collective-permute-done.11
  238.8 4.4 %all-to-all-start.1 = ((bf16[16,128,512]{2,1,0:T(8,128)(2,1)}), bf16[16,128,512]{2,1,0:T(8,128)(2,1)}, u32[]{:S(2)}, u32[]{:S(2)}) async-start(bf16[16,128,512]{2,1,0:T(8,128)(2,1)} %bitcast.116), calls=%async_computation.2 | async-start | bytes 4194304 | tf_op jit(solution)/shard_map/all_to_all | solution.py:57
  245.9 47.8 %all-to-all-done.1 = bf16[16,128,512]{2,1,0:T(8,128)(2,1)} async-done(((bf16[16,128,512]{2,1,0:T(8,128)(2,1)}), bf16[16,128,512]{2,1,0:T(8,128)(2,1)}, u32[]{:S(2)}, u32[]{:S(2)}) %all-to-all-start.1) | async-done | bytes 2097184 | tf_op jit(solution)/shard_map/all_to_all | solution.py:57
  293.7 3.4 collective-permute-start.16
  297.1 3.9 %copy.76 = bf16[1,2048,512]{1,2,0:T(8,128)(2,1)} copy(bf16[1,2048,512]{2,1,0:T(8,128)(2,1)} %param.11) | data formatting | bytes 4194304 | tf_op args[4]
  301.2 6.4 %multiply_convert_fusion = bf16[2,16,2,64,512]{4,3,2,1,0:T(8,128)(2,1)S(1)} fusion(bf16[1,16,2,64,512]{4,3,2,1,0:T(8,128)(2,1)S(1)} %bitcast.115, bf16[1,16,2,64,512]{4,3,2,1,0:T(8,128)(2,1)} %bitcast.4, bf16[1,16,2,64,512]{4,3,2,1,0:T(8,128)(2,1)} %bitcast.47, bf16[1,16,2,64,512]{4,3,2,1,0:T(8,128)(2,1)} %bitcast.46, f32[2,16,2]{2,1,0:T(8,128)S(1)} %copy.75, ...), kind=kLoop, calls=%fused_computation.4 | loop fusion | flops 20971520 | bytes 12583169 | tf_op jit(solution)/shard_map/convert_element_type | solution.py:123
  309.4 5.1 %all-gather.3.cloned.1.call-done = bf16[1,2,32,64,2048]{4,3,2,1,0:T(8,128)(2,1)} async-done(((bf16[1,2,2,64,2048]{4,3,2,1,0:T(8,128)(2,1)}), bf16[1,2,32,64,2048]{4,3,2,1,0:T(8,128)(2,1)}) %all-gather.3.cloned.1.call-update) | async-done | bytes 16777232 | tf_op jit(solution)/shard_map/all_gather | solution.py:80
  314.5 6.7 %fusion.46 = (bf16[1,1,32,64,2048]{4,3,2,1,0:T(8,128)(2,1)S(1)}, bf16[1,1,32,64,2048]{4,3,2,1,0:T(8,128)(2,1)S(1)}) fusion(bf16[1,2,32,64,2048]{4,3,2,1,0:T(8,128)(2,1)} %all-gather.3.cloned.1.call-done), kind=kLoop, calls=%fused_computation.89 | loop fusion | bytes 33554432 | tf_op jit(solution)/shard_map/slice | solution.py:126
  321.3 4.6 %fusion.48 = f32[512,2048]{1,0:T(8,128)S(1)} fusion(bf16[2048,512]{1,0:T(8,128)(2,1)S(1)} %bitcast.123, bf16[2048,2048]{1,0:T(8,128)(2,1)S(1)} %bitcast.118), kind=kOutput, calls=%fused_computation.91 | convolution fusion | flops 4294967296 | bytes 14680064 | tf_op jit(solution)/shard_map/dot_general | solution.py:125
  325.9 6.2 %fusion.2 = f32[1,2048,512]{1,2,0:T(8,128)} fusion(bf16[1,2048,512]{1,2,0:T(8,128)(2,1)S(1)} %copy-done.2, f32[512,2048]{1,0:T(8,128)S(1)} %fusion.48, bf16[2048,512]{1,0:T(8,128)(2,1)S(1)} %bitcast.112, bf16[2048,2048]{1,0:T(8,128)(2,1)S(1)} %bitcast.111, f32[]{:T(128)S(6)} %mul_shard_map.3), kind=kOutput, calls=%fused_computation.11 | convolution fusion | flops 4300210176 | bytes 20971524 | tf_op jit(solution)/shard_map/dot_general | solution.py:125
  332.1 5.4 %copy.77 = f32[1,2048,512]{2,1,0:T(8,128)} copy(f32[1,2048,512]{1,2,0:T(8,128)} %fusion.2) | data formatting | bytes 8388608
  (107 shorter events, 54.1 us)
Async XLA Ops:
  10.1 26.6 %collective-permute-start.2 = (bf16[2,64,2048]{2,1,0:T(8,128)(2,1)}, bf16[2,64,2048]{2,1,0:T(8,128)(2,1)S(1)}, u32[]{:S(2)}, u32[]{:S(2)}) collective-permute-start(bf16[2,64,2048]{2,1,0:T(8,128)(2,1)} %fusion.55), channel_id=1, source_target_pairs={{0,3},{1,0},{2,1},{3,2},{4,7},{5,4},{6,5},{7,6},{8,11},{9,8},{10,9... | collective-permute-start | bytes 1572872 | tf_op jit(solution)/shard_map/ppermute | solution.py:18
  14.6 23.3 %collective-permute-start.1 = (bf16[2,64,2048]{2,1,0:T(8,128)(2,1)}, bf16[2,64,2048]{2,1,0:T(8,128)(2,1)S(1)}, u32[]{:S(2)}, u32[]{:S(2)}) collective-permute-start(bf16[2,64,2048]{2,1,0:T(8,128)(2,1)} %fusion.55), channel_id=1, source_target_pairs={{0,2},{1,3},{2,0},{3,1},{4,6},{5,7},{6,4},{7,5},{8,10},{9,11},{10,... | collective-permute-start | bytes 1572872 | tf_op jit(solution)/shard_map/ppermute | solution.py:18
  14.6 26.3 %collective-permute-start = (bf16[2,64,2048]{2,1,0:T(8,128)(2,1)}, bf16[2,64,2048]{2,1,0:T(8,128)(2,1)}, u32[]{:S(2)}, u32[]{:S(2)}) collective-permute-start(bf16[2,64,2048]{2,1,0:T(8,128)(2,1)} %fusion.55), channel_id=1, source_target_pairs={{0,1},{1,2},{2,3},{3,0},{4,5},{5,6},{6,7},{7,4},{8,9},{9,10},{10,1... | collective-permute-start | bytes 1572872 | tf_op jit(solution)/shard_map/ppermute | solution.py:18
  15.3 40.8 %collective-permute-start.4 = (bf16[2048,512]{1,0:T(8,128)(2,1)}, bf16[2048,512]{1,0:T(8,128)(2,1)}, u32[]{:S(2)}, u32[]{:S(2)}) collective-permute-start(bf16[2048,512]{1,0:T(8,128)(2,1)} %bitcast.136), channel_id=1, source_target_pairs={{0,64},{64,0},{1,65},{65,1},{2,66},{66,2},{3,67},{67,3},{4,68},{68... | collective-permute-start | bytes 6291464 | tf_op jit(solution)/shard_map/ppermute | solution.py:9
  16.9 21.0 %copy-start.3 = (bf16[1,2,64,2048]{3,2,0,1:T(8,128)(2,1)}, bf16[1,2,64,2048]{3,2,0,1:T(8,128)(2,1)S(1)}, u32[]{:S(2)}) copy-start(bf16[1,2,64,2048]{3,2,0,1:T(8,128)(2,1)S(1)} %fusion.54) | copy-start | bytes 1572868
  49.3 37.1 %all-to-all-start = ((bf16[16,128,512]{2,1,0:T(8,128)(2,1)}), bf16[16,128,512]{2,1,0:T(8,128)(2,1)S(1)}, u32[]{:S(2)}, u32[]{:S(2)}) async-start(bf16[16,128,512]{2,1,0:T(8,128)(2,1)} %bitcast.117), calls=%async_computation | async-start | bytes 4194304 | tf_op jit(solution)/shard_map/all_to_all | solution.py:57
  56.1 121.9 %reduce-scatter.2.cloned.1.call-start = ((), (), s32[]{:S(2)}) async-start(), calls=%async_computation.3 | async-start | bytes 8912896 | tf_op jit(solution)/shard_map/reduce_scatter | solution.py:92
  94.8 88.3 %all-reduce.2.cloned.1.call-start = ((), (), s32[]{:S(2)}) async-start(), calls=%async_computation.4 | async-start | bytes 262144 | tf_op jit(solution)/shard_map/psum | solution.py:81
  97.6 217.0 %all-gather.3.cloned.1.call-start = ((), (), s32[]{:S(2)}) async-start(), calls=%async_computation.5 | async-start | bytes 17825792 | tf_op jit(solution)/shard_map/all_gather | solution.py:80
  179.3 12.8 %collective-permute-start.7 = (bf16[2,64,2048]{2,1,0:T(8,128)(2,1)S(1)}, bf16[2,64,2048]{2,1,0:T(8,128)(2,1)}, u32[]{:S(2)}, u32[]{:S(2)}) collective-permute-start(bf16[2,64,2048]{2,1,0:T(8,128)(2,1)S(1)} %bitcast.119), channel_id=1, source_target_pairs={{0,3},{1,0},{2,1},{3,2},{4,7},{5,4},{6,5},{7,6},{8,11},{9,8},{10,9... | collective-permute-start | bytes 1572872 | tf_op jit(solution)/shard_map/ppermute | solution.py:18
  182.0 12.8 %collective-permute-start.6 = (bf16[2,64,2048]{2,1,0:T(8,128)(2,1)S(1)}, bf16[2,64,2048]{2,1,0:T(8,128)(2,1)}, u32[]{:S(2)}, u32[]{:S(2)}) collective-permute-start(bf16[2,64,2048]{2,1,0:T(8,128)(2,1)S(1)} %bitcast.120), channel_id=1, source_target_pairs={{0,2},{1,3},{2,0},{3,1},{4,6},{5,7},{6,4},{7,5},{8,10},{9,11},{10,... | collective-permute-start | bytes 1572872 | tf_op jit(solution)/shard_map/ppermute | solution.py:18
  182.4 26.3 %collective-permute-start.5 = (bf16[2,64,2048]{2,1,0:T(8,128)(2,1)S(1)}, bf16[2,64,2048]{2,1,0:T(8,128)(2,1)}, u32[]{:S(2)}, u32[]{:S(2)}) collective-permute-start(bf16[2,64,2048]{2,1,0:T(8,128)(2,1)S(1)} %bitcast.121), channel_id=1, source_target_pairs={{0,1},{1,2},{2,3},{3,0},{4,5},{5,6},{6,7},{7,4},{8,9},{9,10},{10,1... | collective-permute-start | bytes 1572872 | tf_op jit(solution)/shard_map/ppermute | solution.py:18
  183.1 4.3 %collective-permute-start.8 = (f32[2,2,64,64]{3,2,1,0:T(8,128)}, f32[2,2,64,64]{3,2,1,0:T(8,128)S(1)}, u32[]{:S(2)}, u32[]{:S(2)}) collective-permute-start(f32[2,2,64,64]{3,2,1,0:T(8,128)} %all-reduce.2.cloned.1.call-done), channel_id=1, source_target_pairs={{0,64},{64,0},{1,65},{65,1},{2,66},{66,2},{3,67},{67,3},{4,68},{68... | collective-permute-start | bytes 196616 | tf_op jit(solution)/shard_map/ppermute | solution.py:9
  191.7 16.9 %copy-start.9 = (f32[2,2,64,64]{3,2,1,0:T(8,128)S(1)}, f32[2,2,64,64]{3,2,1,0:T(8,128)}, u32[]{:S(2)}) copy-start(f32[2,2,64,64]{3,2,1,0:T(8,128)} %all-reduce.2.cloned.1.call-done) | copy-start | bytes 196612
  211.4 13.4 %collective-permute-start.9 = (f32[2]{0:T(128)S(1)}, f32[2]{0:T(128)S(1)}, u32[]{:S(2)}, u32[]{:S(2)}) collective-permute-start(f32[2]{0:T(128)S(1)} %maximum_divide_fusion), channel_id=1, source_target_pairs={{0,64},{64,0},{1,65},{65,1},{2,66},{66,2},{3,67},{67,3},{4,68},{68... | collective-permute-start | bytes 32 | tf_op jit(solution)/shard_map/ppermute | solution.py:9
  224.8 3.2 collective-permute-start.12
  226.9 4.1 %collective-permute-start.11 = (f32[2,2]{1,0:T(2,128)S(1)}, f32[2,2]{1,0:T(2,128)S(1)}, u32[]{:S(2)}, u32[]{:S(2)}) collective-permute-start(f32[2,2]{1,0:T(2,128)S(1)} %maximum_select_fusion.2), channel_id=1, source_target_pairs={{0,8},{4,12},{8,0},{12,4},{16,24},{20,28},{24,16},{28,20},{32,40},... | collective-permute-start | bytes 56 | tf_op jit(solution)/shard_map/ppermute | solution.py:36
  227.5 4.2 %collective-permute-start.10 = (f32[2,2]{1,0:T(2,128)S(1)}, f32[2,2]{1,0:T(2,128)S(1)}, u32[]{:S(2)}, u32[]{:S(2)}) collective-permute-start(f32[2,2]{1,0:T(2,128)S(1)} %maximum_select_fusion.2), channel_id=1, source_target_pairs={{0,4},{4,8},{8,12},{12,0},{16,20},{20,24},{24,28},{28,16},{32,36},... | collective-permute-start | bytes 56 | tf_op jit(solution)/shard_map/ppermute | solution.py:36
  232.4 3.1 collective-permute-start.15
  233.1 4.2 %collective-permute-start.14 = (f32[4,2,2]{2,1,0:T(2,128)S(1)}, f32[4,2,2]{2,1,0:T(2,128)S(1)}, u32[]{:S(2)}, u32[]{:S(2)}) collective-permute-start(f32[4,2,2]{2,1,0:T(2,128)S(1)} %broadcast_select_fusion.2), channel_id=1, source_target_pairs={{0,32},{4,36},{8,40},{12,44},{16,48},{20,52},{24,56},{28,60},{32,0... | collective-permute-start | bytes 200 | tf_op jit(solution)/shard_map/ppermute | solution.py:36
  233.7 4.3 %collective-permute-start.13 = (f32[4,2,2]{2,1,0:T(2,128)S(1)}, f32[4,2,2]{2,1,0:T(2,128)S(1)}, u32[]{:S(2)}, u32[]{:S(2)}) collective-permute-start(f32[4,2,2]{2,1,0:T(2,128)S(1)} %broadcast_select_fusion.2), channel_id=1, source_target_pairs={{0,16},{4,20},{8,24},{12,28},{16,32},{20,36},{24,40},{28,44},{32,4... | collective-permute-start | bytes 200 | tf_op jit(solution)/shard_map/ppermute | solution.py:36
  238.8 55.0 %all-to-all-start.1 = ((bf16[16,128,512]{2,1,0:T(8,128)(2,1)}), bf16[16,128,512]{2,1,0:T(8,128)(2,1)}, u32[]{:S(2)}, u32[]{:S(2)}) async-start(bf16[16,128,512]{2,1,0:T(8,128)(2,1)} %bitcast.116), calls=%async_computation.2 | async-start | bytes 4194304 | tf_op jit(solution)/shard_map/all_to_all | solution.py:57
  243.2 57.9 %collective-permute-start.3 = (bf16[2048,512]{1,0:T(8,128)(2,1)S(1)}, bf16[2048,512]{1,0:T(8,128)(2,1)}, u32[]{:S(2)}, u32[]{:S(2)}) collective-permute-start(bf16[2048,512]{1,0:T(8,128)(2,1)S(1)} %bitcast.114), channel_id=1, source_target_pairs={{0,64},{64,0},{1,65},{65,1},{2,66},{66,2},{3,67},{67,3},{4,68},{68... | collective-permute-start | bytes 6291464 | tf_op jit(solution)/shard_map/ppermute | solution.py:9
  293.7 7.5 %collective-permute-start.16 = (bf16[2048,512]{1,0:T(8,128)(2,1)}, bf16[2048,512]{1,0:T(8,128)(2,1)}, u32[]{:S(2)}, u32[]{:S(2)}) collective-permute-start(bf16[2048,512]{1,0:T(8,128)(2,1)} %bitcast.45), channel_id=1, source_target_pairs={{0,64},{64,0},{1,65},{65,1},{2,66},{66,2},{3,67},{67,3},{4,68},{68... | collective-permute-start | bytes 6291464 | tf_op jit(solution)/shard_map/ppermute | solution.py:9
  (8 other events, 42.2 us)
Sparse Core Ops, SparseCore 0:
  95.0 82.9 reduce-scatter.1
  180.1 134.3 all-gather.2
Sparse Core Ops, SparseCore 1:
  97.6 38.1 all-reduce.1

commit v15 on v3

--- a/solution.py
+++ b/solution.py
@@ -85,11 +85,8 @@
     scale_pieces, scale_order = ring_pieces(scale_terms, "dp")
     all_scales = jnp.take(scale_pieces, scale_order, axis=0).transpose(1, 0, 2)
 
-    grad_blocks = jnp.where(
-        is_last,
-        by_micro(is_last, last_blocks, last_blocks_other),
-        by_micro(is_last, first_blocks, first_blocks_other),
-    )
+    candidates = jnp.stack([first_blocks, first_blocks_other, last_blocks_other, last_blocks])
+    grad_blocks = lax.dynamic_slice_in_dim(candidates, micro_count * section_index, micro_count, axis=0)
     scaled_blocks = (
         grad_blocks.reshape(micro_count, group_count, example_count, length_count, column_part).astype(
             jnp.float32

time: 344 us -> 344 us (level)
  no operation moved by 1% of the time
where the time goes in v15:
time: 344 us; the launch traced here: 343 us
  waiting for transfers between devices  178 us (52%)
  starting transfers between devices  65.4 us (19%)
  matrix products  32.4 us (9%)
  local copies, waits for them, and re-layouts  31.6 us (9%)
  other arithmetic  19 us (6%)
  between operations  16.4 us (5%)
    reduce_scatter x1, waiting for transfers between devices, local(): lax.psum_scatter(terms, 'dp', scatter_dimension=0, tiled=True)  77.6 us
    ppermute x21, waiting for transfers between devices, ring_pieces(): lax.ppermute(values, axis, [(source, (source + offset) % count) for sourc...  60.3 us
    ppermute x21, starting transfers between devices, ring_pieces(): lax.ppermute(values, axis, [(source, (source + offset) % count) for sourc...  40.1 us
    all_to_all x2, waiting for transfers between devices, column_blocks(): lax.all_to_all(chunks, 'dp', split_axis=0, concat_axis=1, tiled=True)  28 us
    dot_general x1, matrix products, local(): lax.dot_general(flat_inputs, flat_grads, (((0,), (0,)), ((), ())), prefer...  15.3 us
    ppermute x5, starting transfers between devices, swapped(): lax.ppermute(value, axis, [(source, count - 1 - source) for source in ran...  13.6 us
    another operation x17, local copies, waits for them, and re-layouts, ring_pieces(): stacked = jnp.stack(pieces)  12.8 us
    all_to_all x2, starting transfers between devices, column_blocks(): lax.all_to_all(chunks, 'dp', split_axis=0, concat_axis=1, tiled=True)  11.6 us
  transfers between devices with their start and end apart: 31, of which 12 were waited for; matrix products, arithmetic and copies ran while one was open for 15% of the time, Pallas kernels for 0%

profile of v15, /device:TPU:1, one launch (start us, length us, event | category | flops | bytes accessed | tf_op | source)
XLA Modules:
  0.0 342.8 jit_solution(12456967262532397921)
XLA Ops:
  12.5 3.3 collective-permute-start.1
  19.5 7.0 %collective-permute-done = bf16[2,64,2048]{2,1,0:T(8,128)(2,1)S(1)} collective-permute-done((bf16[2,64,2048]{2,1,0:T(8,128)(2,1)}, bf16[2,64,2048]{2,1,0:T(8,128)(2,1)S(1)}, u32[]{:S(2)}, u32[]{:S(2)}) %collective-permute-start) | collective-permute-done | bytes 524320 | tf_op jit(solution)/shard_map/ppermute | solution.py:18
  27.8 10.9 %collective-permute-done.1 = bf16[2,64,2048]{2,1,0:T(8,128)(2,1)S(1)} collective-permute-done((bf16[2,64,2048]{2,1,0:T(8,128)(2,1)}, bf16[2,64,2048]{2,1,0:T(8,128)(2,1)S(1)}, u32[]{:S(2)}, u32[]{:S(2)}) %collective-permute-start.1) | collective-permute-done | bytes 524320 | tf_op jit(solution)/shard_map/ppermute | solution.py:18
  45.1 3.2 broadcast_select_fusion
  48.2 6.8 %all-to-all-start = ((bf16[16,128,512]{2,1,0:T(8,128)(2,1)}), bf16[16,128,512]{2,1,0:T(8,128)(2,1)S(1)}, u32[]{:S(2)}, u32[]{:S(2)}) async-start(bf16[16,128,512]{2,1,0:T(8,128)(2,1)} %bitcast.129), calls=%async_computation | async-start | bytes 4194304 | tf_op jit(solution)/shard_map/all_to_all | solution.py:33
  55.1 28.0 %all-to-all-done = bf16[16,128,512]{2,1,0:T(8,128)(2,1)S(1)} async-done(((bf16[16,128,512]{2,1,0:T(8,128)(2,1)}), bf16[16,128,512]{2,1,0:T(8,128)(2,1)S(1)}, u32[]{:S(2)}, u32[]{:S(2)}) %all-to-all-start) | async-done | bytes 2097184 | tf_op jit(solution)/shard_map/all_to_all | solution.py:33
  83.0 8.4 %convolution_convert_fusion = bf16[2048,2048]{1,0:T(8,128)(2,1)} fusion(bf16[2048,512]{1,0:T(8,128)(2,1)S(1)} %bitcast.125, bf16[2048,512]{1,0:T(8,128)(2,1)} %collective-permute-done.3, pred[]{:T(512)S(6)} %eq.8, bf16[1,2048,512]{2,1,0:T(8,128)(2,1)} %param.7), kind=kOutput, calls=%fused_computation.8 | convolution fusion | flops 4300210176 | bytes 14680065 | tf_op jit(solution)/shard_map/dot_general | solution.py:65
  95.6 4.0 %copy.140 = bf16[1,2048,512]{1,2,0:T(8,128)(2,1)} copy(bf16[1,2048,512]{2,1,0:T(8,128)(2,1)} %param.11) | data formatting | bytes 4194304 | tf_op args[4]
  100.4 77.6 %reduce-scatter.2.cloned.1.call-done = bf16[128,2048]{1,0:T(8,128)(2,1)} async-done(((bf16[2048,2048]{1,0:T(8,128)(2,1)}), bf16[128,2048]{1,0:T(8,128)(2,1)}) %reduce-scatter.2.cloned.1.call-update) | async-done | bytes 524304 | tf_op jit(solution)/shard_map/reduce_scatter | solution.py:68
  184.3 3.1 collective-permute-start.9
  188.6 3.2 fusion.32
  195.9 8.6 %collective-permute-done.5 = bf16[2,64,2048]{2,1,0:T(8,128)(2,1)} collective-permute-done((bf16[2,64,2048]{2,1,0:T(8,128)(2,1)S(1)}, bf16[2,64,2048]{2,1,0:T(8,128)(2,1)}, u32[]{:S(2)}, u32[]{:S(2)}) %collective-permute-start.5) | collective-permute-done | bytes 524320 | tf_op jit(solution)/shard_map/ppermute | solution.py:18
  211.3 3.6 %gather_fusion.2 = bf16[4,4,128,512]{3,2,1,0:T(8,128)(2,1)} fusion(bf16[4,4,128,512]{3,2,1,0:T(8,128)(2,1)} %maximum_bitcast_fusion.1, s32[1024]{0:T(1024)S(1)} %pad_clamp_fusion.1), kind=kCustom, calls=%fused_computation.1.clone | custom fusion | bytes 4194320 | tf_op jit(solution)/shard_map/jit(_take)/gather | solution.py:32
  214.9 3.2 broadcast_select_fusion.1
  218.1 4.8 %all-to-all-start.1 = ((bf16[16,128,512]{2,1,0:T(8,128)(2,1)}), bf16[16,128,512]{2,1,0:T(8,128)(2,1)}, u32[]{:S(2)}, u32[]{:S(2)}) async-start(bf16[16,128,512]{2,1,0:T(8,128)(2,1)} %bitcast.128), calls=%async_computation.2 | async-start | bytes 4194304 | tf_op jit(solution)/shard_map/all_to_all | solution.py:33
  225.8 3.1 collective-permute-start.10
  237.2 30.4 %collective-permute-done.11 = f32[2,2]{1,0:T(2,128)S(1)} collective-permute-done((f32[2,2]{1,0:T(2,128)S(1)}, f32[2,2]{1,0:T(2,128)S(1)}, u32[]{:S(2)}, u32[]{:S(2)}) %collective-permute-start.11) | collective-permute-done | bytes 48 | tf_op jit(solution)/shard_map/ppermute | solution.py:18
  267.6 3.3 collective-permute-start.15
  279.9 3.3 collective-permute-start.20
  283.3 5.3 %collective-permute-start.7 = (bf16[2048,512]{1,0:T(8,128)(2,1)}, bf16[2048,512]{1,0:T(8,128)(2,1)}, u32[]{:S(2)}, u32[]{:S(2)}) collective-permute-start(bf16[2048,512]{1,0:T(8,128)(2,1)} %bitcast.10), channel_id=1, source_target_pairs={{0,64},{64,0},{1,65},{65,1},{2,66},{66,2},{3,67},{67,3},{4,68},{68... | collective-permute-start | bytes 6291464 | tf_op jit(solution)/shard_map/ppermute | solution.py:9
  298.6 6.6 %multiply_convert_fusion = bf16[2,2048,512]{2,1,0:T(8,128)(2,1)} fusion(s32[]{:T(128)S(6)} %select_n.116, bf16[1,2048,512]{2,1,0:T(8,128)(2,1)} %bitcast.9, bf16[1,2048,512]{2,1,0:T(8,128)(2,1)} %bitcast.11, bf16[1,2048,512]{2,1,0:T(8,128)(2,1)} %bitcast.12, bf16[1,2048,512]{2,1,0:T(8,128)(2,1)S(1)} %bitcast.127, f32[2,2048]{1,0:T(2,128)S(1)} %mul.32), kind=kLoop, calls=%fused_computation.7 | loop fusion | flops 12582912 | bytes 12599300 | tf_op jit(solution)/shard_map/convert_element_type | solution.py:95
  305.3 9.3 %all-gather.3.cloned.1.call-done = bf16[1,2,32,64,2048]{4,3,2,1,0:T(8,128)(2,1)} async-done(((bf16[1,2,2,64,2048]{4,3,2,1,0:T(8,128)(2,1)}), bf16[1,2,32,64,2048]{4,3,2,1,0:T(8,128)(2,1)}) %all-gather.3.cloned.1.call-update) | async-done | bytes 16777232 | tf_op jit(solution)/shard_map/all_gather | solution.py:56
  314.5 15.3 %fusion.4 = f32[1,2048,512]{1,2,0:T(8,128)} fusion(bf16[1,2048,512]{1,2,0:T(8,128)(2,1)} %copy.140, bf16[4096,512]{1,0:T(8,128)(2,1)} %bitcast.130, bf16[4096,2048]{1,0:T(8,128)(2,1)} %bitcast.141, f32[]{:T(128)S(6)} %mul_shard_map.7), kind=kOutput, calls=%fused_computation.14 | convolution fusion | flops 8594128896 | bytes 27262980 | tf_op jit(solution)/shard_map/dot_general | solution.py:98
  329.9 5.4 %copy.141 = f32[1,2048,512]{2,1,0:T(8,128)} copy(f32[1,2048,512]{1,2,0:T(8,128)} %fusion.4) | data formatting | bytes 8388608
  (118 shorter events, 68.6 us)
Async XLA Ops:
  10.1 16.4 %collective-permute-start = (bf16[2,64,2048]{2,1,0:T(8,128)(2,1)}, bf16[2,64,2048]{2,1,0:T(8,128)(2,1)S(1)}, u32[]{:S(2)}, u32[]{:S(2)}) collective-permute-start(bf16[2,64,2048]{2,1,0:T(8,128)(2,1)} %fusion.49), channel_id=1, source_target_pairs={{0,1},{1,2},{2,3},{3,0},{4,5},{5,6},{6,7},{7,4},{8,9},{9,10},{10,1... | collective-permute-start | bytes 1572872 | tf_op jit(solution)/shard_map/ppermute | solution.py:18
  12.5 26.1 %collective-permute-start.1 = (bf16[2,64,2048]{2,1,0:T(8,128)(2,1)}, bf16[2,64,2048]{2,1,0:T(8,128)(2,1)S(1)}, u32[]{:S(2)}, u32[]{:S(2)}) collective-permute-start(bf16[2,64,2048]{2,1,0:T(8,128)(2,1)} %fusion.49), channel_id=1, source_target_pairs={{0,2},{1,3},{2,0},{3,1},{4,6},{5,7},{6,4},{7,5},{8,10},{9,11},{10,... | collective-permute-start | bytes 1572872 | tf_op jit(solution)/shard_map/ppermute | solution.py:18
  15.8 24.1 %collective-permute-start.2 = (bf16[2,64,2048]{2,1,0:T(8,128)(2,1)}, bf16[2,64,2048]{2,1,0:T(8,128)(2,1)}, u32[]{:S(2)}, u32[]{:S(2)}) collective-permute-start(bf16[2,64,2048]{2,1,0:T(8,128)(2,1)} %fusion.49), channel_id=1, source_target_pairs={{0,3},{1,0},{2,1},{3,2},{4,7},{5,4},{6,5},{7,6},{8,11},{9,8},{10,9... | collective-permute-start | bytes 1572872 | tf_op jit(solution)/shard_map/ppermute | solution.py:18
  16.6 38.5 %collective-permute-start.3 = (bf16[2048,512]{1,0:T(8,128)(2,1)}, bf16[2048,512]{1,0:T(8,128)(2,1)}, u32[]{:S(2)}, u32[]{:S(2)}) collective-permute-start(bf16[2048,512]{1,0:T(8,128)(2,1)} %bitcast.142), channel_id=1, source_target_pairs={{0,64},{64,0},{1,65},{65,1},{2,66},{66,2},{3,67},{67,3},{4,68},{68... | collective-permute-start | bytes 6291464 | tf_op jit(solution)/shard_map/ppermute | solution.py:9
  48.2 34.8 %all-to-all-start = ((bf16[16,128,512]{2,1,0:T(8,128)(2,1)}), bf16[16,128,512]{2,1,0:T(8,128)(2,1)S(1)}, u32[]{:S(2)}, u32[]{:S(2)}) async-start(bf16[16,128,512]{2,1,0:T(8,128)(2,1)} %bitcast.129), calls=%async_computation | async-start | bytes 4194304 | tf_op jit(solution)/shard_map/all_to_all | solution.py:33
  55.0 123.0 %reduce-scatter.2.cloned.1.call-start = ((), (), s32[]{:S(2)}) async-start(), calls=%async_computation.3 | async-start | bytes 8912896 | tf_op jit(solution)/shard_map/reduce_scatter | solution.py:68
  91.4 92.9 %all-reduce.2.cloned.1.call-start = ((), (), s32[]{:S(2)}) async-start(), calls=%async_computation.4 | async-start | bytes 262144 | tf_op jit(solution)/shard_map/psum | solution.py:57
  94.2 220.4 %all-gather.3.cloned.1.call-start = ((), (), s32[]{:S(2)}) async-start(), calls=%async_computation.5 | async-start | bytes 17825792 | tf_op jit(solution)/shard_map/all_gather | solution.py:56
  179.3 14.3 %collective-permute-start.4 = (bf16[2,64,2048]{2,1,0:T(8,128)(2,1)S(1)}, bf16[2,64,2048]{2,1,0:T(8,128)(2,1)}, u32[]{:S(2)}, u32[]{:S(2)}) collective-permute-start(bf16[2,64,2048]{2,1,0:T(8,128)(2,1)S(1)} %bitcast.131), channel_id=1, source_target_pairs={{0,1},{1,2},{2,3},{3,0},{4,5},{5,6},{6,7},{7,4},{8,9},{9,10},{10,1... | collective-permute-start | bytes 1572872 | tf_op jit(solution)/shard_map/ppermute | solution.py:18
  180.6 23.9 %collective-permute-start.5 = (bf16[2,64,2048]{2,1,0:T(8,128)(2,1)S(1)}, bf16[2,64,2048]{2,1,0:T(8,128)(2,1)}, u32[]{:S(2)}, u32[]{:S(2)}) collective-permute-start(bf16[2,64,2048]{2,1,0:T(8,128)(2,1)S(1)} %bitcast.132), channel_id=1, source_target_pairs={{0,2},{1,3},{2,0},{3,1},{4,6},{5,7},{6,4},{7,5},{8,10},{9,11},{10,... | collective-permute-start | bytes 1572872 | tf_op jit(solution)/shard_map/ppermute | solution.py:18
  183.2 23.6 %collective-permute-start.6 = (bf16[2,64,2048]{2,1,0:T(8,128)(2,1)S(1)}, bf16[2,64,2048]{2,1,0:T(8,128)(2,1)}, u32[]{:S(2)}, u32[]{:S(2)}) collective-permute-start(bf16[2,64,2048]{2,1,0:T(8,128)(2,1)S(1)} %bitcast.133), channel_id=1, source_target_pairs={{0,3},{1,0},{2,1},{3,2},{4,7},{5,4},{6,5},{7,6},{8,11},{9,8},{10,9... | collective-permute-start | bytes 1572872 | tf_op jit(solution)/shard_map/ppermute | solution.py:18
  191.8 106.9 %collective-permute-start.8 = (bf16[2048,512]{1,0:T(8,128)(2,1)S(1)}, bf16[2048,512]{1,0:T(8,128)(2,1)}, u32[]{:S(2)}, u32[]{:S(2)}) collective-permute-start(bf16[2048,512]{1,0:T(8,128)(2,1)S(1)} %bitcast.126), channel_id=1, source_target_pairs={{0,64},{64,0},{1,65},{65,1},{2,66},{66,2},{3,67},{67,3},{4,68},{68... | collective-permute-start | bytes 6291464 | tf_op jit(solution)/shard_map/ppermute | solution.py:9
  218.1 65.2 %all-to-all-start.1 = ((bf16[16,128,512]{2,1,0:T(8,128)(2,1)}), bf16[16,128,512]{2,1,0:T(8,128)(2,1)}, u32[]{:S(2)}, u32[]{:S(2)}) async-start(bf16[16,128,512]{2,1,0:T(8,128)(2,1)} %bitcast.128), calls=%async_computation.2 | async-start | bytes 4194304 | tf_op jit(solution)/shard_map/all_to_all | solution.py:33
  229.8 37.8 %collective-permute-start.11 = (f32[2,2]{1,0:T(2,128)S(1)}, f32[2,2]{1,0:T(2,128)S(1)}, u32[]{:S(2)}, u32[]{:S(2)}) collective-permute-start(f32[2,2]{1,0:T(2,128)S(1)} %maximum_select_fusion.1), channel_id=1, source_target_pairs={{0,4},{4,8},{8,12},{12,16},{16,20},{20,24},{24,28},{28,32},{32,36}... | collective-permute-start | bytes 56 | tf_op jit(solution)/shard_map/ppermute | solution.py:18
  231.5 41.9 %collective-permute-start.12 = (f32[2,2]{1,0:T(2,128)S(1)}, f32[2,2]{1,0:T(2,128)S(1)}, u32[]{:S(2)}, u32[]{:S(2)}) collective-permute-start(f32[2,2]{1,0:T(2,128)S(1)} %maximum_select_fusion.1), channel_id=1, source_target_pairs={{0,8},{4,12},{8,16},{12,20},{16,24},{20,28},{24,32},{28,36},{32,40... | collective-permute-start | bytes 56 | tf_op jit(solution)/shard_map/ppermute | solution.py:18
  233.9 40.7 %collective-permute-start.13 = (f32[2,2]{1,0:T(2,128)S(1)}, f32[2,2]{1,0:T(2,128)S(1)}, u32[]{:S(2)}, u32[]{:S(2)}) collective-permute-start(f32[2,2]{1,0:T(2,128)S(1)} %maximum_select_fusion.1), channel_id=1, source_target_pairs={{0,12},{4,16},{8,20},{12,24},{16,28},{20,32},{24,36},{28,40},{32,4... | collective-permute-start | bytes 56 | tf_op jit(solution)/shard_map/ppermute | solution.py:18
  236.0 40.7 %collective-permute-start.14 = (f32[2,2]{1,0:T(2,128)S(1)}, f32[2,2]{1,0:T(2,128)S(1)}, u32[]{:S(2)}, u32[]{:S(2)}) collective-permute-start(f32[2,2]{1,0:T(2,128)S(1)} %maximum_select_fusion.1), channel_id=1, source_target_pairs={{0,16},{4,20},{8,24},{12,28},{16,32},{20,36},{24,40},{28,44},{32,4... | collective-permute-start | bytes 56 | tf_op jit(solution)/shard_map/ppermute | solution.py:18
  267.6 10.5 %collective-permute-start.15 = (f32[2,2]{1,0:T(2,128)S(1)}, f32[2,2]{1,0:T(2,128)S(1)}, u32[]{:S(2)}, u32[]{:S(2)}) collective-permute-start(f32[2,2]{1,0:T(2,128)S(1)} %maximum_select_fusion.1), channel_id=1, source_target_pairs={{0,20},{4,24},{8,28},{12,32},{16,36},{20,40},{24,44},{28,48},{32,5... | collective-permute-start | bytes 56 | tf_op jit(solution)/shard_map/ppermute | solution.py:18
  273.4 6.5 %collective-permute-start.16 = (f32[2,2]{1,0:T(2,128)S(1)}, f32[2,2]{1,0:T(2,128)S(1)}, u32[]{:S(2)}, u32[]{:S(2)}) collective-permute-start(f32[2,2]{1,0:T(2,128)S(1)} %maximum_select_fusion.1), channel_id=1, source_target_pairs={{0,24},{4,28},{8,32},{12,36},{16,40},{20,44},{24,48},{28,52},{32,5... | collective-permute-start | bytes 56 | tf_op jit(solution)/shard_map/ppermute | solution.py:18
  274.5 8.7 %collective-permute-start.17 = (f32[2,2]{1,0:T(2,128)S(1)}, f32[2,2]{1,0:T(2,128)S(1)}, u32[]{:S(2)}, u32[]{:S(2)}) collective-permute-start(f32[2,2]{1,0:T(2,128)S(1)} %maximum_select_fusion.1), channel_id=1, source_target_pairs={{0,28},{4,32},{8,36},{12,40},{16,44},{20,48},{24,52},{28,56},{32,6... | collective-permute-start | bytes 56 | tf_op jit(solution)/shard_map/ppermute | solution.py:18
  276.7 12.0 %collective-permute-start.18 = (f32[2,2]{1,0:T(2,128)S(1)}, f32[2,2]{1,0:T(2,128)S(1)}, u32[]{:S(2)}, u32[]{:S(2)}) collective-permute-start(f32[2,2]{1,0:T(2,128)S(1)} %maximum_select_fusion.1), channel_id=1, source_target_pairs={{0,32},{4,36},{8,40},{12,44},{16,48},{20,52},{24,56},{28,60},{32,0... | collective-permute-start | bytes 56 | tf_op jit(solution)/shard_map/ppermute | solution.py:18
  278.2 11.5 %collective-permute-start.19 = (f32[2,2]{1,0:T(2,128)S(1)}, f32[2,2]{1,0:T(2,128)S(1)}, u32[]{:S(2)}, u32[]{:S(2)}) collective-permute-start(f32[2,2]{1,0:T(2,128)S(1)} %maximum_select_fusion.1), channel_id=1, source_target_pairs={{0,36},{4,40},{8,44},{12,48},{16,52},{20,56},{24,60},{28,0},{32,4}... | collective-permute-start | bytes 56 | tf_op jit(solution)/shard_map/ppermute | solution.py:18
  279.9 11.3 %collective-permute-start.20 = (f32[2,2]{1,0:T(2,128)S(1)}, f32[2,2]{1,0:T(2,128)S(1)}, u32[]{:S(2)}, u32[]{:S(2)}) collective-permute-start(f32[2,2]{1,0:T(2,128)S(1)} %maximum_select_fusion.1), channel_id=1, source_target_pairs={{0,40},{4,44},{8,48},{12,52},{16,56},{20,60},{24,0},{28,4},{32,8},... | collective-permute-start | bytes 56 | tf_op jit(solution)/shard_map/ppermute | solution.py:18
  283.3 15.3 %collective-permute-start.7 = (bf16[2048,512]{1,0:T(8,128)(2,1)}, bf16[2048,512]{1,0:T(8,128)(2,1)}, u32[]{:S(2)}, u32[]{:S(2)}) collective-permute-start(bf16[2048,512]{1,0:T(8,128)(2,1)} %bitcast.10), channel_id=1, source_target_pairs={{0,64},{64,0},{1,65},{65,1},{2,66},{66,2},{3,67},{67,3},{4,68},{68... | collective-permute-start | bytes 6291464 | tf_op jit(solution)/shard_map/ppermute | solution.py:9
  (14 other events, 143.0 us)
Sparse Core Ops, SparseCore 0:
  91.6 86.3 reduce-scatter.1
  180.1 134.3 all-gather.2
Sparse Core Ops, SparseCore 1:
  94.3 41.5 all-reduce.1
